TPU v7x, 32 devices: a whole 2x2x4 slice. The times are simulated.
32 devices in a mesh: parts: 2 (over y), tm: 4 (over x, core), cols: 4 (over z).
Axes of the slice: x: 2, y: 2, z: 4, core: 2. Of those that a mesh axis runs over, the one named last changes fastest.
Arguments:
- noise: float32 [16, 1024, 1024], P(('parts', 'tm'), None, 'cols'), parts along dimension 0, may hold values from -6 to 6
- inv_diag: float32 [16, 1024, 1024], P(('parts', 'tm'), None, 'cols'), parts along dimension 0, may hold values from -2 to 2, as said below
- coupling: float32 [16, 1024, 1024], P(('parts', 'tm'), None, 'cols'), parts along dimension 0, may hold values from -1 to 1, as said below
- order: int32 [1024], replicated, may hold values from 0 to 1023, each once
Outputs:
- sample: float32 [16, 1024, 1024], P(('parts', 'tm'), None, 'cols'), parts along dimension 0
There are 2 independent parts, one for each index of `parts`. A program takes and returns all parts, laid end to end along the dimension named above; an argument that names none is the same for every part. Nothing has to cross between parts.
Inputs may be any that keep to these rules, and one draw needn't show every extreme that they name: `order`: each of 0 to 1023 appears once. `inv_diag`: diagonal entries lie between 0.5 and 2, off-diagonal entries are small in magnitude. `coupling`: diagonal entries lie between 0.5 and 0.97, off-diagonal entries are small in magnitude.
All inputs are finite; a program needn't handle non-finite values.
Results may differ from a plain program's by a relative error of at most 0.00013.
Values sent between devices are 32-bit elements; how exact they have to be, the bound alone decides.
No kernel may reach another device: no remote copies, remote signals or barrier semaphores. Data moves between devices by JAX's collectives and lax.ppermute only.
A program may use at most 128 MiB of HBM per device.

v0:
```python
import jax
import jax.numpy as jnp
from jax import lax
from jax.sharding import PartitionSpec as P
from jax.experimental import pallas as pl
from jax.experimental.pallas import tpu as pltpu

low = jnp.bfloat16


def shifted(block, axis, distance):
    devices = range(lax.axis_size(axis))
    route = [(i - distance, i) for i in devices if i - distance in devices]
    return lax.ppermute(block, axis, route)


def split(value, count):
    parts = []
    rest = value
    for index in range(count):
        kept = lax.reduce_precision(rest, exponent_bits=8, mantissa_bits=7)
        parts.append(kept.astype(low))
        if index < count - 1:
            rest = rest - kept
    return parts


def bdot(left, right):
    return jnp.dot(left, right, preferred_element_type=jnp.float32)


def apply(matrix_parts, operand):
    high, small = matrix_parts
    width = operand.shape[1]
    operand_high, operand_small = split(operand, 2)
    both = bdot(high, jnp.concatenate([operand_high, operand_small], axis=1))
    return both[:, :width] + (both[:, width:] + bdot(small, operand_high))


def line_reduce_scatter(partial, axis):
    count = lax.axis_size(axis)
    me = lax.axis_index(axis)
    width = partial.shape[2] // count

    def tile(owner):
        owner = jnp.clip(owner, 0, count - 1)
        return lax.dynamic_slice_in_dim(partial, owner * width, width, axis=2)

    rightward = jnp.zeros_like(tile(me))
    leftward = jnp.zeros_like(tile(me))
    for step in range(1, count):
        right_route = [(k, k + 1) for k in range(0, min(step, count - 1))]
        left_route = [(k, k - 1) for k in range(max(count - step, 1), count)]
        rightward = lax.ppermute(tile(me + count - step) + rightward, axis, right_route)
        leftward = lax.ppermute(tile(me - count + step) + leftward, axis, left_route)
    return tile(me) + (rightward + leftward)


def add_at(whole, piece, slot, axis):
    count = whole.shape[axis] // piece.shape[axis]
    start = jnp.clip(slot, 0, count - 1) * piece.shape[axis]
    current = lax.dynamic_slice_in_dim(whole, start, piece.shape[axis], axis=axis)
    return lax.dynamic_update_slice_in_dim(whole, current + piece, start, axis=axis)


def line_all_gather(tile, axis):
    count = lax.axis_size(axis)
    me = lax.axis_index(axis)
    last = tile.ndim - 1
    shape = tile.shape[:-1] + (count * tile.shape[-1],)
    whole = add_at(jnp.zeros(shape, tile.dtype), tile, me, last)
    from_left = tile
    from_right = tile
    for step in range(1, count):
        from_left = lax.ppermute(from_left, axis, [(k, k + 1) for k in range(step - 1, count - 1)])
        from_right = lax.ppermute(from_right, axis, [(k, k - 1) for k in range(1, count - step + 1)])
        whole = add_at(whole, from_left, me - step, last)
        whole = add_at(whole, from_right, me + step, last)
    return whole


def line_all_to_all(value, axis):
    count = lax.axis_size(axis)
    me = lax.axis_index(axis)
    rows = value.shape[1] // count

    def own_rows(target):
        return lax.dynamic_slice_in_dim(value, jnp.clip(target, 0, count - 1) * rows, rows, axis=1)

    shape = (value.shape[0], rows, count * value.shape[2])
    whole = add_at(jnp.zeros(shape, value.dtype), own_rows(me), me, 2)
    for distance in range(1, count):
        right = lax.ppermute(own_rows(me + distance), axis, [(k, k + distance) for k in range(0, count - distance)])
        left = lax.ppermute(own_rows(me - distance), axis, [(k, k - distance) for k in range(distance, count)])
        whole = add_at(whole, right, me - distance, 2)
        whole = add_at(whole, left, me + distance, 2)
    return whole


def pick_rows_kernel(order_ref, field_ref, out_ref):
    blocks = field_ref.shape[0]

    def body(row, carry):
        source = order_ref[row]
        for block in range(blocks):
            out_ref[block, pl.ds(row, 1), :] = field_ref[block, pl.ds(source, 1), :]
        return carry

    lax.fori_loop(0, field_ref.shape[1], body, 0, unroll=8)


def pick_rows(field, order):
    return pl.pallas_call(
        pick_rows_kernel,
        out_shape=jax.ShapeDtypeStruct(field.shape, field.dtype),
        in_specs=[pl.BlockSpec(memory_space=pltpu.SMEM), pl.BlockSpec(memory_space=pltpu.VMEM)],
        out_specs=pl.BlockSpec(memory_space=pltpu.VMEM),
        cost_estimate=pl.CostEstimate(flops=0, transcendentals=0, bytes_accessed=2 * field.size * 4),
    )(order, field)


def shards(noise, inv_diag, coupling, order):
    block_count = noise.shape[0]
    node_count = noise.shape[1]
    sample_count = noise.shape[2]
    coupling_full = line_all_gather(coupling, "cols")
    noise_rows = line_all_to_all(noise, "cols")
    partial = jnp.stack(
        [apply(split(inv_diag[block], 2), noise_rows[block]) for block in range(block_count)], axis=0
    )
    driven_all = line_reduce_scatter(partial, "cols")
    driven = [driven_all[block] for block in range(block_count)]
    coupling_parts = [split(coupling_full[block], 2) for block in range(block_count)]

    def chain(entering, skip_last):
        carried = entering
        results = [None] * block_count
        for block in range(block_count - 1, -1, -1):
            if skip_last and block == block_count - 1:
                carried = driven[block]
            else:
                carried = driven[block] + apply(coupling_parts[block], carried)
            results[block] = carried
        return results

    relays = lax.axis_size("tm")
    entering = jnp.zeros_like(driven[0])
    for step in range(relays - 1):
        sender = relays - 1 - step
        leaving = chain(entering, step == 0)[0]
        entering = entering + lax.ppermute(leaving, "tm", [(sender, sender - 1)])
    finals = chain(entering, False)
    return pick_rows(jnp.stack(finals, axis=0), order)


def solution(mesh):
    return jax.shard_map(
        shards,
        mesh=mesh,
        in_specs=(
            P(("parts", "tm"), None, "cols"),
            P(("parts", "tm"), None, "cols"),
            P(("parts", "tm"), None, "cols"),
            P(),
        ),
        out_specs=P(("parts", "tm"), None, "cols"),
        check_vma=False,
    )
```

profile of v0, /device:TPU:25, one launch (start us, length us, event | category | flops | bytes accessed | tf_op | source)
XLA Modules:
  0.0 305.7 jit_solution(1827611151873295524)
XLA Ops:
  1.9 1.4 collective-permute-start
  3.3 4.0 %collective-permute-start.1 = (f32[2,256,256]{2,1,0:T(8,128)S(1)}, f32[2,256,256]{2,1,0:T(8,128)S(1)}, u32[]{:S(2)}, u32[]{:S(2)}) collective-permute-start(f32[2,256,256]{2,1,0:T(8,128)S(1)} %get-tuple-element.24), channel_id=1, source_target_pairs={{1,0},{2,1},{3,2},{5,4},{6,5},{7,6},{9,8},{10,9},{11,10},{13,12},{... | collective-permute-start | bytes 1572872 | tf_op jit(solution)/shard_map/ppermute | solution.py:94
  10.0 4.1 %collective-permute-start.13 = (f32[2,1024,256]{2,1,0:T(8,128)S(1)}, f32[2,1024,256]{2,1,0:T(8,128)S(1)}, u32[]{:S(2)}, u32[]{:S(2)}) collective-permute-start(f32[2,1024,256]{2,1,0:T(8,128)S(1)} %copy-done.3), channel_id=1, source_target_pairs={{1,0},{2,1},{3,2},{5,4},{6,5},{7,6},{9,8},{10,9},{11,10},{13,12},{... | collective-permute-start | bytes 6291464 | tf_op jit(solution)/shard_map/ppermute | solution.py:76
  14.1 2.6 collective-permute-done
  16.7 2.3 collective-permute-start.3
  20.6 18.5 %collective-permute-done.2 = f32[2,256,256]{2,1,0:T(8,128)S(1)} collective-permute-done((f32[2,256,256]{2,1,0:T(8,128)S(1)}, f32[2,256,256]{2,1,0:T(8,128)S(1)}, u32[]{:S(2)}, u32[]{:S(2)}) %collective-permute-start.2) | collective-permute-done | bytes 524320 | tf_op jit(solution)/shard_map/ppermute | solution.py:93
  40.6 33.2 %collective-permute-done.3 = f32[2,256,256]{2,1,0:T(8,128)S(1)} collective-permute-done((f32[2,256,256]{2,1,0:T(8,128)S(1)}, f32[2,256,256]{2,1,0:T(8,128)S(1)}, u32[]{:S(2)}, u32[]{:S(2)}) %collective-permute-start.3) | collective-permute-done | bytes 524320 | tf_op jit(solution)/shard_map/ppermute | solution.py:94
  73.9 10.1 %collective-permute-done.4 = f32[2,256,256]{2,1,0:T(8,128)S(1)} collective-permute-done((f32[2,256,256]{2,1,0:T(8,128)S(1)}, f32[2,256,256]{2,1,0:T(8,128)S(1)}, u32[]{:S(2)}, u32[]{:S(2)}) %collective-permute-start.4) | collective-permute-done | bytes 524320 | tf_op jit(solution)/shard_map/ppermute | solution.py:93
  92.1 13.7 %collective-permute-start.9 = (f32[2,1024,256]{2,1,0:T(8,128)S(1)}, f32[2,1024,256]{2,1,0:T(8,128)S(1)}, u32[]{:S(2)}, u32[]{:S(2)}) collective-permute-start(f32[2,1024,256]{2,1,0:T(8,128)S(1)} %get-tuple-element.11), channel_id=1, source_target_pairs={{3,2},{7,6},{11,10},{15,14},{19,18},{23,22},{27,26},{31,30}} | collective-permute-start | bytes 6291464 | tf_op jit(solution)/shard_map/ppermute | solution.py:55
  107.9 40.8 %collective-permute-done.9 = f32[2,1024,256]{2,1,0:T(8,128)S(1)} collective-permute-done((f32[2,1024,256]{2,1,0:T(8,128)S(1)}, f32[2,1024,256]{2,1,0:T(8,128)S(1)}, u32[]{:S(2)}, u32[]{:S(2)}) %collective-permute-start.9) | collective-permute-done | bytes 2097184 | tf_op jit(solution)/shard_map/ppermute | solution.py:55
  148.7 2.2 fusion.24
  150.9 4.1 %collective-permute-start.10 = (f32[2,1024,256]{2,1,0:T(8,128)}, f32[2,1024,256]{2,1,0:T(8,128)S(1)}, u32[]{:S(2)}, u32[]{:S(2)}) collective-permute-start(f32[2,1024,256]{2,1,0:T(8,128)} %get-tuple-element.9), channel_id=1, source_target_pairs={{2,1},{3,2},{6,5},{7,6},{10,9},{11,10},{14,13},{15,14},{18,17},{19... | collective-permute-start | bytes 6291464 | tf_op jit(solution)/shard_map/ppermute | solution.py:55
  155.1 2.2 collective-permute-start.7
  160.9 36.4 %collective-permute-done.10 = f32[2,1024,256]{2,1,0:T(8,128)S(1)} collective-permute-done((f32[2,1024,256]{2,1,0:T(8,128)}, f32[2,1024,256]{2,1,0:T(8,128)S(1)}, u32[]{:S(2)}, u32[]{:S(2)}) %collective-permute-start.10) | collective-permute-done | bytes 2097184 | tf_op jit(solution)/shard_map/ppermute | solution.py:55
  198.7 4.4 %fusion.22 = (f32[2,1024,256]{2,1,0:T(8,128)}, f32[2,1024,256]{2,1,0:T(8,128)S(1)}) fusion(f32[2,1024,256]{2,1,0:T(8,128)} %copy-done.2, s32[]{:T(128)S(6)} %select_n.15, f32[1,1024,1024]{2,1,0:T(8,128)S(1)} %fusion.9, f32[1,1024,1024]{2,1,0:T(8,128)S(1)} %fusion.7, f32[2,1024,256]{2,1,0:T(8,128)} %collective-permute-done.7, s32[]{:T(128)S(6)} %select_n.16), kind=kLoop, calls=%fused_computation.45 | loop fusion | flops 2097152 | bytes 16777224 | tf_op jit(solution)/shard_map/add | solution.py:55
  203.1 5.4 %collective-permute-start.11 = (f32[2,1024,256]{2,1,0:T(8,128)}, f32[2,1024,256]{2,1,0:T(8,128)S(1)}, u32[]{:S(2)}, u32[]{:S(2)}) collective-permute-start(f32[2,1024,256]{2,1,0:T(8,128)} %get-tuple-element.7), channel_id=1, source_target_pairs={{1,0},{2,1},{3,2},{5,4},{6,5},{7,6},{9,8},{10,9},{11,10},{13,12},{... | collective-permute-start | bytes 6291464 | tf_op jit(solution)/shard_map/ppermute | solution.py:55
  214.1 35.8 %collective-permute-done.11 = f32[2,1024,256]{2,1,0:T(8,128)S(1)} collective-permute-done((f32[2,1024,256]{2,1,0:T(8,128)}, f32[2,1024,256]{2,1,0:T(8,128)S(1)}, u32[]{:S(2)}, u32[]{:S(2)}) %collective-permute-start.11) | collective-permute-done | bytes 2097184 | tf_op jit(solution)/shard_map/ppermute | solution.py:55
  249.9 3.6 %collective-permute-done.8 = f32[2,1024,256]{2,1,0:T(8,128)S(1)} collective-permute-done((f32[2,1024,256]{2,1,0:T(8,128)S(1)}, f32[2,1024,256]{2,1,0:T(8,128)S(1)}, u32[]{:S(2)}, u32[]{:S(2)}) %collective-permute-start.8) | collective-permute-done | bytes 2097184 | tf_op jit(solution)/shard_map/ppermute | solution.py:54
  261.2 1.5 collective-permute-start.19
  262.8 22.1 %collective-permute-done.19 = f32[1024,256]{1,0:T(8,128)S(1)} collective-permute-done((f32[1024,256]{1,0:T(8,128)S(1)}, f32[1024,256]{1,0:T(8,128)S(1)}, u32[]{:S(2)}, u32[]{:S(2)}) %collective-permute-start.19) | collective-permute-done | bytes 1048608 | tf_op jit(solution)/shard_map/ppermute | solution.py:151
  289.2 1.4 collective-permute-start.20
  290.5 2.2 collective-permute-done.20
  297.0 1.5 pad_maximum_fusion.field_ref
  298.5 7.2 %shard_map.46 = f32[2,1024,256]{2,1,0:T(8,128)} custom-call(s32[1024]{0:T(1024)} %order_ref.1, f32[2,1024,256]{2,1,0:T(8,128)} %pad_maximum_fusion.field_ref), custom_call_target="tpu_custom_call" | custom-call | bytes 4194304 | tf_op jit(solution)/shard_map/pallas_call | solution.py:113
  (75 shorter events, 44.3 us)
Async XLA Ops:
  1.6 7.1 %copy-start.3 = (f32[2,1024,256]{2,1,0:T(8,128)S(1)}, f32[2,1024,256]{2,1,0:T(8,128)}, u32[]{:S(2)}) copy-start(f32[2,1024,256]{2,1,0:T(8,128)} %param.6) | copy-start | bytes 6291460
  1.9 14.8 %collective-permute-start = (f32[2,256,256]{2,1,0:T(8,128)S(1)}, f32[2,256,256]{2,1,0:T(8,128)S(1)}, u32[]{:S(2)}, u32[]{:S(2)}) collective-permute-start(f32[2,256,256]{2,1,0:T(8,128)S(1)} %get-tuple-element.25), channel_id=1, source_target_pairs={{0,1},{1,2},{2,3},{4,5},{5,6},{6,7},{8,9},{9,10},{10,11},{12,13},{... | collective-permute-start | bytes 1572872 | tf_op jit(solution)/shard_map/ppermute | solution.py:93
  3.3 15.9 %collective-permute-start.1 = (f32[2,256,256]{2,1,0:T(8,128)S(1)}, f32[2,256,256]{2,1,0:T(8,128)S(1)}, u32[]{:S(2)}, u32[]{:S(2)}) collective-permute-start(f32[2,256,256]{2,1,0:T(8,128)S(1)} %get-tuple-element.24), channel_id=1, source_target_pairs={{1,0},{2,1},{3,2},{5,4},{6,5},{7,6},{9,8},{10,9},{11,10},{13,12},{... | collective-permute-start | bytes 1572872 | tf_op jit(solution)/shard_map/ppermute | solution.py:94
  7.4 31.8 %collective-permute-start.2 = (f32[2,256,256]{2,1,0:T(8,128)S(1)}, f32[2,256,256]{2,1,0:T(8,128)S(1)}, u32[]{:S(2)}, u32[]{:S(2)}) collective-permute-start(f32[2,256,256]{2,1,0:T(8,128)S(1)} %get-tuple-element.23), channel_id=1, source_target_pairs={{0,2},{1,3},{4,6},{5,7},{8,10},{9,11},{12,14},{13,15},{16,18},{17,... | collective-permute-start | bytes 1572872 | tf_op jit(solution)/shard_map/ppermute | solution.py:93
  8.7 97.1 %collective-permute-start.12 = (f32[2,1024,256]{2,1,0:T(8,128)S(1)}, f32[2,1024,256]{2,1,0:T(8,128)S(1)}, u32[]{:S(2)}, u32[]{:S(2)}) collective-permute-start(f32[2,1024,256]{2,1,0:T(8,128)S(1)} %copy-done.3), channel_id=1, source_target_pairs={{0,1},{1,2},{2,3},{4,5},{5,6},{6,7},{8,9},{9,10},{10,11},{12,13},{... | collective-permute-start | bytes 6291464 | tf_op jit(solution)/shard_map/ppermute | solution.py:75
  10.0 97.1 %collective-permute-start.13 = (f32[2,1024,256]{2,1,0:T(8,128)S(1)}, f32[2,1024,256]{2,1,0:T(8,128)S(1)}, u32[]{:S(2)}, u32[]{:S(2)}) collective-permute-start(f32[2,1024,256]{2,1,0:T(8,128)S(1)} %copy-done.3), channel_id=1, source_target_pairs={{1,0},{2,1},{3,2},{5,4},{6,5},{7,6},{9,8},{10,9},{11,10},{13,12},{... | collective-permute-start | bytes 6291464 | tf_op jit(solution)/shard_map/ppermute | solution.py:76
  16.7 57.1 %collective-permute-start.3 = (f32[2,256,256]{2,1,0:T(8,128)S(1)}, f32[2,256,256]{2,1,0:T(8,128)S(1)}, u32[]{:S(2)}, u32[]{:S(2)}) collective-permute-start(f32[2,256,256]{2,1,0:T(8,128)S(1)} %get-tuple-element.22), channel_id=1, source_target_pairs={{2,0},{3,1},{6,4},{7,5},{10,8},{11,9},{14,12},{15,13},{18,16},{19,... | collective-permute-start | bytes 1572872 | tf_op jit(solution)/shard_map/ppermute | solution.py:94
  19.2 64.8 %collective-permute-start.4 = (f32[2,256,256]{2,1,0:T(8,128)S(1)}, f32[2,256,256]{2,1,0:T(8,128)S(1)}, u32[]{:S(2)}, u32[]{:S(2)}) collective-permute-start(f32[2,256,256]{2,1,0:T(8,128)S(1)} %get-tuple-element.27), channel_id=1, source_target_pairs={{0,3},{4,7},{8,11},{12,15},{16,19},{20,23},{24,27},{28,31}} | collective-permute-start | bytes 1572872 | tf_op jit(solution)/shard_map/ppermute | solution.py:93
  39.1 45.9 %collective-permute-start.5 = (f32[2,256,256]{2,1,0:T(8,128)S(1)}, f32[2,256,256]{2,1,0:T(8,128)S(1)}, u32[]{:S(2)}, u32[]{:S(2)}) collective-permute-start(f32[2,256,256]{2,1,0:T(8,128)S(1)} %get-tuple-element.21), channel_id=1, source_target_pairs={{3,0},{7,4},{11,8},{15,12},{19,16},{23,20},{27,24},{31,28}} | collective-permute-start | bytes 1572872 | tf_op jit(solution)/shard_map/ppermute | solution.py:94
  85.2 1.6 copy-start
  91.3 16.6 %collective-permute-start.6 = (f32[2,1024,256]{2,1,0:T(8,128)S(1)}, f32[2,1024,256]{2,1,0:T(8,128)S(1)}, u32[]{:S(2)}, u32[]{:S(2)}) collective-permute-start(f32[2,1024,256]{2,1,0:T(8,128)S(1)} %get-tuple-element.12), channel_id=1, source_target_pairs={{0,1},{4,5},{8,9},{12,13},{16,17},{20,21},{24,25},{28,29}} | collective-permute-start | bytes 6291464 | tf_op jit(solution)/shard_map/ppermute | solution.py:54
  92.1 56.6 %collective-permute-start.9 = (f32[2,1024,256]{2,1,0:T(8,128)S(1)}, f32[2,1024,256]{2,1,0:T(8,128)S(1)}, u32[]{:S(2)}, u32[]{:S(2)}) collective-permute-start(f32[2,1024,256]{2,1,0:T(8,128)S(1)} %get-tuple-element.11), channel_id=1, source_target_pairs={{3,2},{7,6},{11,10},{15,14},{19,18},{23,22},{27,26},{31,30}} | collective-permute-start | bytes 6291464 | tf_op jit(solution)/shard_map/ppermute | solution.py:55
  105.8 51.4 %collective-permute-start.14 = (f32[2,1024,256]{2,1,0:T(8,128)S(1)}, f32[2,1024,256]{2,1,0:T(8,128)S(1)}, u32[]{:S(2)}, u32[]{:S(2)}) collective-permute-start(f32[2,1024,256]{2,1,0:T(8,128)S(1)} %collective-permute-done.12), channel_id=1, source_target_pairs={{1,2},{2,3},{5,6},{6,7},{9,10},{10,11},{13,14},{14,15},{17,18},{18... | collective-permute-start | bytes 6291464 | tf_op jit(solution)/shard_map/ppermute | solution.py:75
  107.1 51.4 %collective-permute-start.15 = (f32[2,1024,256]{2,1,0:T(8,128)S(1)}, f32[2,1024,256]{2,1,0:T(8,128)S(1)}, u32[]{:S(2)}, u32[]{:S(2)}) collective-permute-start(f32[2,1024,256]{2,1,0:T(8,128)S(1)} %collective-permute-done.13), channel_id=1, source_target_pairs={{1,0},{2,1},{5,4},{6,5},{9,8},{10,9},{13,12},{14,13},{17,16},{18,1... | collective-permute-start | bytes 6291464 | tf_op jit(solution)/shard_map/ppermute | solution.py:76
  150.9 46.4 %collective-permute-start.10 = (f32[2,1024,256]{2,1,0:T(8,128)}, f32[2,1024,256]{2,1,0:T(8,128)S(1)}, u32[]{:S(2)}, u32[]{:S(2)}) collective-permute-start(f32[2,1024,256]{2,1,0:T(8,128)} %get-tuple-element.9), channel_id=1, source_target_pairs={{2,1},{3,2},{6,5},{7,6},{10,9},{11,10},{14,13},{15,14},{18,17},{19... | collective-permute-start | bytes 6291464 | tf_op jit(solution)/shard_map/ppermute | solution.py:55
  155.1 5.5 %copy-start.4 = (f32[2,1024,256]{2,1,0:T(8,128)S(1)}, f32[2,1024,256]{2,1,0:T(8,128)}, u32[]{:S(2)}) copy-start(f32[2,1024,256]{2,1,0:T(8,128)} %param.6) | copy-start | bytes 6291460
  155.1 43.6 %collective-permute-start.7 = (f32[2,1024,256]{2,1,0:T(8,128)S(1)}, f32[2,1024,256]{2,1,0:T(8,128)}, u32[]{:S(2)}, u32[]{:S(2)}) collective-permute-start(f32[2,1024,256]{2,1,0:T(8,128)S(1)} %get-tuple-element.10), channel_id=1, source_target_pairs={{0,1},{1,2},{4,5},{5,6},{8,9},{9,10},{12,13},{13,14},{16,17},{17,1... | collective-permute-start | bytes 6291464 | tf_op jit(solution)/shard_map/ppermute | solution.py:54
  157.2 55.3 %collective-permute-start.16 = (f32[2,1024,256]{2,1,0:T(8,128)S(1)}, f32[2,1024,256]{2,1,0:T(8,128)S(1)}, u32[]{:S(2)}, u32[]{:S(2)}) collective-permute-start(f32[2,1024,256]{2,1,0:T(8,128)S(1)} %collective-permute-done.14), channel_id=1, source_target_pairs={{2,3},{6,7},{10,11},{14,15},{18,19},{22,23},{26,27},{30,31}} | collective-permute-start | bytes 6291464 | tf_op jit(solution)/shard_map/ppermute | solution.py:75
  158.5 54.6 %collective-permute-start.17 = (f32[2,1024,256]{2,1,0:T(8,128)S(1)}, f32[2,1024,256]{2,1,0:T(8,128)S(1)}, u32[]{:S(2)}, u32[]{:S(2)}) collective-permute-start(f32[2,1024,256]{2,1,0:T(8,128)S(1)} %collective-permute-done.15), channel_id=1, source_target_pairs={{1,0},{5,4},{9,8},{13,12},{17,16},{21,20},{25,24},{29,28}} | collective-permute-start | bytes 6291464 | tf_op jit(solution)/shard_map/ppermute | solution.py:76
  203.1 46.8 %collective-permute-start.11 = (f32[2,1024,256]{2,1,0:T(8,128)}, f32[2,1024,256]{2,1,0:T(8,128)S(1)}, u32[]{:S(2)}, u32[]{:S(2)}) collective-permute-start(f32[2,1024,256]{2,1,0:T(8,128)} %get-tuple-element.7), channel_id=1, source_target_pairs={{1,0},{2,1},{3,2},{5,4},{6,5},{7,6},{9,8},{10,9},{11,10},{13,12},{... | collective-permute-start | bytes 6291464 | tf_op jit(solution)/shard_map/ppermute | solution.py:55
  208.6 45.0 %collective-permute-start.8 = (f32[2,1024,256]{2,1,0:T(8,128)S(1)}, f32[2,1024,256]{2,1,0:T(8,128)S(1)}, u32[]{:S(2)}, u32[]{:S(2)}) collective-permute-start(f32[2,1024,256]{2,1,0:T(8,128)S(1)} %get-tuple-element.8), channel_id=1, source_target_pairs={{0,1},{1,2},{2,3},{4,5},{5,6},{6,7},{8,9},{9,10},{10,11},{12,13},{... | collective-permute-start | bytes 6291464 | tf_op jit(solution)/shard_map/ppermute | solution.py:54
  256.3 0.7 collective-permute-start.18
  261.2 23.6 %collective-permute-start.19 = (f32[1024,256]{1,0:T(8,128)S(1)}, f32[1024,256]{1,0:T(8,128)S(1)}, u32[]{:S(2)}, u32[]{:S(2)}) collective-permute-start(f32[1024,256]{1,0:T(8,128)S(1)} %fusion.57), channel_id=1, source_target_pairs={{8,4},{9,5},{10,6},{11,7},{24,20},{25,21},{26,22},{27,23}} | collective-permute-start | bytes 3145736 | tf_op jit(solution)/shard_map/ppermute | solution.py:151
  289.2 3.6 %collective-permute-start.20 = (f32[1024,256]{1,0:T(8,128)S(1)}, f32[1024,256]{1,0:T(8,128)S(1)}, u32[]{:S(2)}, u32[]{:S(2)}) collective-permute-start(f32[1024,256]{1,0:T(8,128)S(1)} %fusion.53), channel_id=1, source_target_pairs={{4,0},{5,1},{6,2},{7,3},{20,16},{21,17},{22,18},{23,19}} | collective-permute-start | bytes 3145736 | tf_op jit(solution)/shard_map/ppermute | solution.py:151
  (2 other events, 2.9 us)
where the time goes:
time: 306 us
  waiting for transfers between devices  206 us (67%)
  starting transfers between devices  52.5 us (17%)
  matrix products  18 us (6%)
  other arithmetic  15.4 us (5%)
  Pallas kernels  7.23 us (2%)
  local copies, waits for them, and re-layouts  5.73 us (2%)
    ppermute x3, waiting for transfers between devices, line_reduce_scatter(): lax.ppermute(tile(me - count + step) + leftward, axis, left_route)  113 us
    ppermute x3, waiting for transfers between devices, line_all_to_all(): lax.ppermute(own_rows(me - distance), axis, [(k, k - distance) for k in r...  34.2 us
    ppermute x3, waiting for transfers between devices, line_all_to_all(): lax.ppermute(own_rows(me + distance), axis, [(k, k + distance) for k in r...  31.2 us
    ppermute x3, waiting for transfers between devices, shards(): entering = entering + lax.ppermute(leaving, 'tm', [(sender, sender - 1)])  24.3 us
    ppermute x3, starting transfers between devices, line_reduce_scatter(): lax.ppermute(tile(me - count + step) + leftward, axis, left_route)  23.3 us
    dot_general x18, matrix products, bdot(): return jnp.dot(left, right, preferred_element_type=jnp.float32)  18 us
    ppermute x3, starting transfers between devices, line_all_to_all(): lax.ppermute(own_rows(me - distance), axis, [(k, k - distance) for k in r...  7.67 us
    pallas_call x1, Pallas kernels, pick_rows(): pl.pallas_call(pick_rows_kernel, out_shape=jax.ShapeDtypeStruct(field.sha...  7.23 us
  transfers between devices with their start and end apart: 21, of which 11 were waited for; matrix products, arithmetic and copies ran while one was open for 6% of the time, Pallas kernels for 0%

commit v1 on v0

--- a/solution.py
+++ b/solution.py
@@ -99,14 +99,17 @@
 
 def pick_rows_kernel(order_ref, field_ref, out_ref):
     blocks = field_ref.shape[0]
+    group = 8
 
-    def body(row, carry):
-        source = order_ref[row]
+    def body(index, carry):
+        start = pl.multiple_of(index * group, group)
+        sources = [order_ref[start + row] for row in range(group)]
         for block in range(blocks):
-            out_ref[block, pl.ds(row, 1), :] = field_ref[block, pl.ds(source, 1), :]
+            rows = [field_ref[block, pl.ds(source, 1), :] for source in sources]
+            out_ref[block, pl.ds(start, group), :] = jnp.concatenate(rows, axis=0)
         return carry
 
-    lax.fori_loop(0, field_ref.shape[1], body, 0, unroll=8)
+    lax.fori_loop(0, field_ref.shape[1] // group, body, 0, unroll=2)
 
 
 def pick_rows(field, order):

time: 306 us -> 304 us (level)
  no operation moved by 1% of the time
where the time goes in v1:
time: 304 us
  waiting for transfers between devices  206 us (68%)
  starting transfers between devices  52.5 us (17%)
  matrix products  18 us (6%)
  other arithmetic  15.4 us (5%)
  local copies, waits for them, and re-layouts  5.73 us (2%)
  Pallas kernels  5.24 us (2%)
    ppermute x3, waiting for transfers between devices, line_reduce_scatter(): lax.ppermute(tile(me - count + step) + leftward, axis, left_route)  113 us
    ppermute x3, waiting for transfers between devices, line_all_to_all(): lax.ppermute(own_rows(me - distance), axis, [(k, k - distance) for k in r...  34.2 us
    ppermute x3, waiting for transfers between devices, line_all_to_all(): lax.ppermute(own_rows(me + distance), axis, [(k, k + distance) for k in r...  31.2 us
    ppermute x3, waiting for transfers between devices, shards(): entering = entering + lax.ppermute(leaving, 'tm', [(sender, sender - 1)])  24.3 us
    ppermute x3, starting transfers between devices, line_reduce_scatter(): lax.ppermute(tile(me - count + step) + leftward, axis, left_route)  23.3 us
    dot_general x18, matrix products, bdot(): return jnp.dot(left, right, preferred_element_type=jnp.float32)  18 us
    ppermute x3, starting transfers between devices, line_all_to_all(): lax.ppermute(own_rows(me - distance), axis, [(k, k - distance) for k in r...  7.67 us
    add x2, other arithmetic, line_reduce_scatter(): tile(me - count + step) + leftward  6.65 us
  transfers between devices with their start and end apart: 21, of which 11 were waited for; matrix products, arithmetic and copies ran while one was open for 6% of the time, Pallas kernels for 0%

profile of v1, /device:TPU:25, one launch (start us, length us, event | category | flops | bytes accessed | tf_op | source)
XLA Modules:
  0.0 303.7 jit_solution(12274489993570669669)
XLA Ops:
  1.9 1.4 collective-permute-start
  3.3 4.0 %collective-permute-start.1 = (f32[2,256,256]{2,1,0:T(8,128)S(1)}, f32[2,256,256]{2,1,0:T(8,128)S(1)}, u32[]{:S(2)}, u32[]{:S(2)}) collective-permute-start(f32[2,256,256]{2,1,0:T(8,128)S(1)} %get-tuple-element.24), channel_id=1, source_target_pairs={{1,0},{2,1},{3,2},{5,4},{6,5},{7,6},{9,8},{10,9},{11,10},{13,12},{... | collective-permute-start | bytes 1572872 | tf_op jit(solution)/shard_map/ppermute | solution.py:94
  10.0 4.1 %collective-permute-start.13 = (f32[2,1024,256]{2,1,0:T(8,128)S(1)}, f32[2,1024,256]{2,1,0:T(8,128)S(1)}, u32[]{:S(2)}, u32[]{:S(2)}) collective-permute-start(f32[2,1024,256]{2,1,0:T(8,128)S(1)} %copy-done.3), channel_id=1, source_target_pairs={{1,0},{2,1},{3,2},{5,4},{6,5},{7,6},{9,8},{10,9},{11,10},{13,12},{... | collective-permute-start | bytes 6291464 | tf_op jit(solution)/shard_map/ppermute | solution.py:76
  14.1 2.6 collective-permute-done
  16.7 2.3 collective-permute-start.3
  20.6 18.5 %collective-permute-done.2 = f32[2,256,256]{2,1,0:T(8,128)S(1)} collective-permute-done((f32[2,256,256]{2,1,0:T(8,128)S(1)}, f32[2,256,256]{2,1,0:T(8,128)S(1)}, u32[]{:S(2)}, u32[]{:S(2)}) %collective-permute-start.2) | collective-permute-done | bytes 524320 | tf_op jit(solution)/shard_map/ppermute | solution.py:93
  40.6 33.2 %collective-permute-done.3 = f32[2,256,256]{2,1,0:T(8,128)S(1)} collective-permute-done((f32[2,256,256]{2,1,0:T(8,128)S(1)}, f32[2,256,256]{2,1,0:T(8,128)S(1)}, u32[]{:S(2)}, u32[]{:S(2)}) %collective-permute-start.3) | collective-permute-done | bytes 524320 | tf_op jit(solution)/shard_map/ppermute | solution.py:94
  73.9 10.1 %collective-permute-done.4 = f32[2,256,256]{2,1,0:T(8,128)S(1)} collective-permute-done((f32[2,256,256]{2,1,0:T(8,128)S(1)}, f32[2,256,256]{2,1,0:T(8,128)S(1)}, u32[]{:S(2)}, u32[]{:S(2)}) %collective-permute-start.4) | collective-permute-done | bytes 524320 | tf_op jit(solution)/shard_map/ppermute | solution.py:93
  92.1 13.7 %collective-permute-start.9 = (f32[2,1024,256]{2,1,0:T(8,128)S(1)}, f32[2,1024,256]{2,1,0:T(8,128)S(1)}, u32[]{:S(2)}, u32[]{:S(2)}) collective-permute-start(f32[2,1024,256]{2,1,0:T(8,128)S(1)} %get-tuple-element.11), channel_id=1, source_target_pairs={{3,2},{7,6},{11,10},{15,14},{19,18},{23,22},{27,26},{31,30}} | collective-permute-start | bytes 6291464 | tf_op jit(solution)/shard_map/ppermute | solution.py:55
  107.9 40.8 %collective-permute-done.9 = f32[2,1024,256]{2,1,0:T(8,128)S(1)} collective-permute-done((f32[2,1024,256]{2,1,0:T(8,128)S(1)}, f32[2,1024,256]{2,1,0:T(8,128)S(1)}, u32[]{:S(2)}, u32[]{:S(2)}) %collective-permute-start.9) | collective-permute-done | bytes 2097184 | tf_op jit(solution)/shard_map/ppermute | solution.py:55
  148.7 2.2 fusion.24
  150.9 4.1 %collective-permute-start.10 = (f32[2,1024,256]{2,1,0:T(8,128)}, f32[2,1024,256]{2,1,0:T(8,128)S(1)}, u32[]{:S(2)}, u32[]{:S(2)}) collective-permute-start(f32[2,1024,256]{2,1,0:T(8,128)} %get-tuple-element.9), channel_id=1, source_target_pairs={{2,1},{3,2},{6,5},{7,6},{10,9},{11,10},{14,13},{15,14},{18,17},{19... | collective-permute-start | bytes 6291464 | tf_op jit(solution)/shard_map/ppermute | solution.py:55
  155.1 2.2 collective-permute-start.7
  160.9 36.4 %collective-permute-done.10 = f32[2,1024,256]{2,1,0:T(8,128)S(1)} collective-permute-done((f32[2,1024,256]{2,1,0:T(8,128)}, f32[2,1024,256]{2,1,0:T(8,128)S(1)}, u32[]{:S(2)}, u32[]{:S(2)}) %collective-permute-start.10) | collective-permute-done | bytes 2097184 | tf_op jit(solution)/shard_map/ppermute | solution.py:55
  198.7 4.4 %fusion.22 = (f32[2,1024,256]{2,1,0:T(8,128)}, f32[2,1024,256]{2,1,0:T(8,128)S(1)}) fusion(f32[2,1024,256]{2,1,0:T(8,128)} %copy-done.2, s32[]{:T(128)S(6)} %select_n.15, f32[1,1024,1024]{2,1,0:T(8,128)S(1)} %fusion.9, f32[1,1024,1024]{2,1,0:T(8,128)S(1)} %fusion.7, f32[2,1024,256]{2,1,0:T(8,128)} %collective-permute-done.7, s32[]{:T(128)S(6)} %select_n.16), kind=kLoop, calls=%fused_computation.45 | loop fusion | flops 2097152 | bytes 16777224 | tf_op jit(solution)/shard_map/add | solution.py:55
  203.1 5.4 %collective-permute-start.11 = (f32[2,1024,256]{2,1,0:T(8,128)}, f32[2,1024,256]{2,1,0:T(8,128)S(1)}, u32[]{:S(2)}, u32[]{:S(2)}) collective-permute-start(f32[2,1024,256]{2,1,0:T(8,128)} %get-tuple-element.7), channel_id=1, source_target_pairs={{1,0},{2,1},{3,2},{5,4},{6,5},{7,6},{9,8},{10,9},{11,10},{13,12},{... | collective-permute-start | bytes 6291464 | tf_op jit(solution)/shard_map/ppermute | solution.py:55
  214.1 35.8 %collective-permute-done.11 = f32[2,1024,256]{2,1,0:T(8,128)S(1)} collective-permute-done((f32[2,1024,256]{2,1,0:T(8,128)}, f32[2,1024,256]{2,1,0:T(8,128)S(1)}, u32[]{:S(2)}, u32[]{:S(2)}) %collective-permute-start.11) | collective-permute-done | bytes 2097184 | tf_op jit(solution)/shard_map/ppermute | solution.py:55
  249.9 3.6 %collective-permute-done.8 = f32[2,1024,256]{2,1,0:T(8,128)S(1)} collective-permute-done((f32[2,1024,256]{2,1,0:T(8,128)S(1)}, f32[2,1024,256]{2,1,0:T(8,128)S(1)}, u32[]{:S(2)}, u32[]{:S(2)}) %collective-permute-start.8) | collective-permute-done | bytes 2097184 | tf_op jit(solution)/shard_map/ppermute | solution.py:54
  261.2 1.5 collective-permute-start.19
  262.8 22.1 %collective-permute-done.19 = f32[1024,256]{1,0:T(8,128)S(1)} collective-permute-done((f32[1024,256]{1,0:T(8,128)S(1)}, f32[1024,256]{1,0:T(8,128)S(1)}, u32[]{:S(2)}, u32[]{:S(2)}) %collective-permute-start.19) | collective-permute-done | bytes 1048608 | tf_op jit(solution)/shard_map/ppermute | solution.py:154
  289.2 1.4 collective-permute-start.20
  290.5 2.2 collective-permute-done.20
  297.0 1.5 pad_maximum_fusion.field_ref
  298.5 5.2 %shard_map.46 = f32[2,1024,256]{2,1,0:T(8,128)} custom-call(s32[1024]{0:T(1024)} %order_ref.1, f32[2,1024,256]{2,1,0:T(8,128)} %pad_maximum_fusion.field_ref), custom_call_target="tpu_custom_call" | custom-call | bytes 4194304 | tf_op jit(solution)/shard_map/pallas_call | solution.py:116
  (75 shorter events, 44.3 us)
Async XLA Ops:
  1.6 7.1 %copy-start.3 = (f32[2,1024,256]{2,1,0:T(8,128)S(1)}, f32[2,1024,256]{2,1,0:T(8,128)}, u32[]{:S(2)}) copy-start(f32[2,1024,256]{2,1,0:T(8,128)} %param.6) | copy-start | bytes 6291460
  1.9 14.8 %collective-permute-start = (f32[2,256,256]{2,1,0:T(8,128)S(1)}, f32[2,256,256]{2,1,0:T(8,128)S(1)}, u32[]{:S(2)}, u32[]{:S(2)}) collective-permute-start(f32[2,256,256]{2,1,0:T(8,128)S(1)} %get-tuple-element.25), channel_id=1, source_target_pairs={{0,1},{1,2},{2,3},{4,5},{5,6},{6,7},{8,9},{9,10},{10,11},{12,13},{... | collective-permute-start | bytes 1572872 | tf_op jit(solution)/shard_map/ppermute | solution.py:93
  3.3 15.9 %collective-permute-start.1 = (f32[2,256,256]{2,1,0:T(8,128)S(1)}, f32[2,256,256]{2,1,0:T(8,128)S(1)}, u32[]{:S(2)}, u32[]{:S(2)}) collective-permute-start(f32[2,256,256]{2,1,0:T(8,128)S(1)} %get-tuple-element.24), channel_id=1, source_target_pairs={{1,0},{2,1},{3,2},{5,4},{6,5},{7,6},{9,8},{10,9},{11,10},{13,12},{... | collective-permute-start | bytes 1572872 | tf_op jit(solution)/shard_map/ppermute | solution.py:94
  7.4 31.8 %collective-permute-start.2 = (f32[2,256,256]{2,1,0:T(8,128)S(1)}, f32[2,256,256]{2,1,0:T(8,128)S(1)}, u32[]{:S(2)}, u32[]{:S(2)}) collective-permute-start(f32[2,256,256]{2,1,0:T(8,128)S(1)} %get-tuple-element.23), channel_id=1, source_target_pairs={{0,2},{1,3},{4,6},{5,7},{8,10},{9,11},{12,14},{13,15},{16,18},{17,... | collective-permute-start | bytes 1572872 | tf_op jit(solution)/shard_map/ppermute | solution.py:93
  8.7 97.1 %collective-permute-start.12 = (f32[2,1024,256]{2,1,0:T(8,128)S(1)}, f32[2,1024,256]{2,1,0:T(8,128)S(1)}, u32[]{:S(2)}, u32[]{:S(2)}) collective-permute-start(f32[2,1024,256]{2,1,0:T(8,128)S(1)} %copy-done.3), channel_id=1, source_target_pairs={{0,1},{1,2},{2,3},{4,5},{5,6},{6,7},{8,9},{9,10},{10,11},{12,13},{... | collective-permute-start | bytes 6291464 | tf_op jit(solution)/shard_map/ppermute | solution.py:75
  10.0 97.1 %collective-permute-start.13 = (f32[2,1024,256]{2,1,0:T(8,128)S(1)}, f32[2,1024,256]{2,1,0:T(8,128)S(1)}, u32[]{:S(2)}, u32[]{:S(2)}) collective-permute-start(f32[2,1024,256]{2,1,0:T(8,128)S(1)} %copy-done.3), channel_id=1, source_target_pairs={{1,0},{2,1},{3,2},{5,4},{6,5},{7,6},{9,8},{10,9},{11,10},{13,12},{... | collective-permute-start | bytes 6291464 | tf_op jit(solution)/shard_map/ppermute | solution.py:76
  16.7 57.1 %collective-permute-start.3 = (f32[2,256,256]{2,1,0:T(8,128)S(1)}, f32[2,256,256]{2,1,0:T(8,128)S(1)}, u32[]{:S(2)}, u32[]{:S(2)}) collective-permute-start(f32[2,256,256]{2,1,0:T(8,128)S(1)} %get-tuple-element.22), channel_id=1, source_target_pairs={{2,0},{3,1},{6,4},{7,5},{10,8},{11,9},{14,12},{15,13},{18,16},{19,... | collective-permute-start | bytes 1572872 | tf_op jit(solution)/shard_map/ppermute | solution.py:94
  19.2 64.8 %collective-permute-start.4 = (f32[2,256,256]{2,1,0:T(8,128)S(1)}, f32[2,256,256]{2,1,0:T(8,128)S(1)}, u32[]{:S(2)}, u32[]{:S(2)}) collective-permute-start(f32[2,256,256]{2,1,0:T(8,128)S(1)} %get-tuple-element.27), channel_id=1, source_target_pairs={{0,3},{4,7},{8,11},{12,15},{16,19},{20,23},{24,27},{28,31}} | collective-permute-start | bytes 1572872 | tf_op jit(solution)/shard_map/ppermute | solution.py:93
  39.1 45.9 %collective-permute-start.5 = (f32[2,256,256]{2,1,0:T(8,128)S(1)}, f32[2,256,256]{2,1,0:T(8,128)S(1)}, u32[]{:S(2)}, u32[]{:S(2)}) collective-permute-start(f32[2,256,256]{2,1,0:T(8,128)S(1)} %get-tuple-element.21), channel_id=1, source_target_pairs={{3,0},{7,4},{11,8},{15,12},{19,16},{23,20},{27,24},{31,28}} | collective-permute-start | bytes 1572872 | tf_op jit(solution)/shard_map/ppermute | solution.py:94
  85.2 1.6 copy-start
  91.3 16.6 %collective-permute-start.6 = (f32[2,1024,256]{2,1,0:T(8,128)S(1)}, f32[2,1024,256]{2,1,0:T(8,128)S(1)}, u32[]{:S(2)}, u32[]{:S(2)}) collective-permute-start(f32[2,1024,256]{2,1,0:T(8,128)S(1)} %get-tuple-element.12), channel_id=1, source_target_pairs={{0,1},{4,5},{8,9},{12,13},{16,17},{20,21},{24,25},{28,29}} | collective-permute-start | bytes 6291464 | tf_op jit(solution)/shard_map/ppermute | solution.py:54
  92.1 56.6 %collective-permute-start.9 = (f32[2,1024,256]{2,1,0:T(8,128)S(1)}, f32[2,1024,256]{2,1,0:T(8,128)S(1)}, u32[]{:S(2)}, u32[]{:S(2)}) collective-permute-start(f32[2,1024,256]{2,1,0:T(8,128)S(1)} %get-tuple-element.11), channel_id=1, source_target_pairs={{3,2},{7,6},{11,10},{15,14},{19,18},{23,22},{27,26},{31,30}} | collective-permute-start | bytes 6291464 | tf_op jit(solution)/shard_map/ppermute | solution.py:55
  105.8 51.4 %collective-permute-start.14 = (f32[2,1024,256]{2,1,0:T(8,128)S(1)}, f32[2,1024,256]{2,1,0:T(8,128)S(1)}, u32[]{:S(2)}, u32[]{:S(2)}) collective-permute-start(f32[2,1024,256]{2,1,0:T(8,128)S(1)} %collective-permute-done.12), channel_id=1, source_target_pairs={{1,2},{2,3},{5,6},{6,7},{9,10},{10,11},{13,14},{14,15},{17,18},{18... | collective-permute-start | bytes 6291464 | tf_op jit(solution)/shard_map/ppermute | solution.py:75
  107.1 51.4 %collective-permute-start.15 = (f32[2,1024,256]{2,1,0:T(8,128)S(1)}, f32[2,1024,256]{2,1,0:T(8,128)S(1)}, u32[]{:S(2)}, u32[]{:S(2)}) collective-permute-start(f32[2,1024,256]{2,1,0:T(8,128)S(1)} %collective-permute-done.13), channel_id=1, source_target_pairs={{1,0},{2,1},{5,4},{6,5},{9,8},{10,9},{13,12},{14,13},{17,16},{18,1... | collective-permute-start | bytes 6291464 | tf_op jit(solution)/shard_map/ppermute | solution.py:76
  150.9 46.4 %collective-permute-start.10 = (f32[2,1024,256]{2,1,0:T(8,128)}, f32[2,1024,256]{2,1,0:T(8,128)S(1)}, u32[]{:S(2)}, u32[]{:S(2)}) collective-permute-start(f32[2,1024,256]{2,1,0:T(8,128)} %get-tuple-element.9), channel_id=1, source_target_pairs={{2,1},{3,2},{6,5},{7,6},{10,9},{11,10},{14,13},{15,14},{18,17},{19... | collective-permute-start | bytes 6291464 | tf_op jit(solution)/shard_map/ppermute | solution.py:55
  155.1 5.5 %copy-start.4 = (f32[2,1024,256]{2,1,0:T(8,128)S(1)}, f32[2,1024,256]{2,1,0:T(8,128)}, u32[]{:S(2)}) copy-start(f32[2,1024,256]{2,1,0:T(8,128)} %param.6) | copy-start | bytes 6291460
  155.1 43.6 %collective-permute-start.7 = (f32[2,1024,256]{2,1,0:T(8,128)S(1)}, f32[2,1024,256]{2,1,0:T(8,128)}, u32[]{:S(2)}, u32[]{:S(2)}) collective-permute-start(f32[2,1024,256]{2,1,0:T(8,128)S(1)} %get-tuple-element.10), channel_id=1, source_target_pairs={{0,1},{1,2},{4,5},{5,6},{8,9},{9,10},{12,13},{13,14},{16,17},{17,1... | collective-permute-start | bytes 6291464 | tf_op jit(solution)/shard_map/ppermute | solution.py:54
  157.2 55.3 %collective-permute-start.16 = (f32[2,1024,256]{2,1,0:T(8,128)S(1)}, f32[2,1024,256]{2,1,0:T(8,128)S(1)}, u32[]{:S(2)}, u32[]{:S(2)}) collective-permute-start(f32[2,1024,256]{2,1,0:T(8,128)S(1)} %collective-permute-done.14), channel_id=1, source_target_pairs={{2,3},{6,7},{10,11},{14,15},{18,19},{22,23},{26,27},{30,31}} | collective-permute-start | bytes 6291464 | tf_op jit(solution)/shard_map/ppermute | solution.py:75
  158.5 54.6 %collective-permute-start.17 = (f32[2,1024,256]{2,1,0:T(8,128)S(1)}, f32[2,1024,256]{2,1,0:T(8,128)S(1)}, u32[]{:S(2)}, u32[]{:S(2)}) collective-permute-start(f32[2,1024,256]{2,1,0:T(8,128)S(1)} %collective-permute-done.15), channel_id=1, source_target_pairs={{1,0},{5,4},{9,8},{13,12},{17,16},{21,20},{25,24},{29,28}} | collective-permute-start | bytes 6291464 | tf_op jit(solution)/shard_map/ppermute | solution.py:76
  203.1 46.8 %collective-permute-start.11 = (f32[2,1024,256]{2,1,0:T(8,128)}, f32[2,1024,256]{2,1,0:T(8,128)S(1)}, u32[]{:S(2)}, u32[]{:S(2)}) collective-permute-start(f32[2,1024,256]{2,1,0:T(8,128)} %get-tuple-element.7), channel_id=1, source_target_pairs={{1,0},{2,1},{3,2},{5,4},{6,5},{7,6},{9,8},{10,9},{11,10},{13,12},{... | collective-permute-start | bytes 6291464 | tf_op jit(solution)/shard_map/ppermute | solution.py:55
  208.6 45.0 %collective-permute-start.8 = (f32[2,1024,256]{2,1,0:T(8,128)S(1)}, f32[2,1024,256]{2,1,0:T(8,128)S(1)}, u32[]{:S(2)}, u32[]{:S(2)}) collective-permute-start(f32[2,1024,256]{2,1,0:T(8,128)S(1)} %get-tuple-element.8), channel_id=1, source_target_pairs={{0,1},{1,2},{2,3},{4,5},{5,6},{6,7},{8,9},{9,10},{10,11},{12,13},{... | collective-permute-start | bytes 6291464 | tf_op jit(solution)/shard_map/ppermute | solution.py:54
  256.3 0.7 collective-permute-start.18
  261.2 23.6 %collective-permute-start.19 = (f32[1024,256]{1,0:T(8,128)S(1)}, f32[1024,256]{1,0:T(8,128)S(1)}, u32[]{:S(2)}, u32[]{:S(2)}) collective-permute-start(f32[1024,256]{1,0:T(8,128)S(1)} %fusion.57), channel_id=1, source_target_pairs={{8,4},{9,5},{10,6},{11,7},{24,20},{25,21},{26,22},{27,23}} | collective-permute-start | bytes 3145736 | tf_op jit(solution)/shard_map/ppermute | solution.py:154
  289.2 3.6 %collective-permute-start.20 = (f32[1024,256]{1,0:T(8,128)S(1)}, f32[1024,256]{1,0:T(8,128)S(1)}, u32[]{:S(2)}, u32[]{:S(2)}) collective-permute-start(f32[1024,256]{1,0:T(8,128)S(1)} %fusion.53), channel_id=1, source_target_pairs={{4,0},{5,1},{6,2},{7,3},{20,16},{21,17},{22,18},{23,19}} | collective-permute-start | bytes 3145736 | tf_op jit(solution)/shard_map/ppermute | solution.py:154
  (2 other events, 2.9 us)

commit v2 on v1

--- a/solution.py
+++ b/solution.py
@@ -97,29 +97,31 @@
     return whole
 
 
-def pick_rows_kernel(order_ref, field_ref, out_ref):
-    blocks = field_ref.shape[0]
+def pick_rows_kernel(order_ref, *refs):
+    field_refs = refs[:-1]
+    out_ref = refs[-1]
     group = 8
 
     def body(index, carry):
         start = pl.multiple_of(index * group, group)
         sources = [order_ref[start + row] for row in range(group)]
-        for block in range(blocks):
-            rows = [field_ref[block, pl.ds(source, 1), :] for source in sources]
+        for block, field_ref in enumerate(field_refs):
+            rows = [field_ref[pl.ds(source, 1), :] for source in sources]
             out_ref[block, pl.ds(start, group), :] = jnp.concatenate(rows, axis=0)
         return carry
 
-    lax.fori_loop(0, field_ref.shape[1] // group, body, 0, unroll=2)
+    lax.fori_loop(0, out_ref.shape[1] // group, body, 0, unroll=4)
 
 
-def pick_rows(field, order):
+def pick_rows(fields, order):
+    shape = (len(fields),) + fields[0].shape
     return pl.pallas_call(
         pick_rows_kernel,
-        out_shape=jax.ShapeDtypeStruct(field.shape, field.dtype),
-        in_specs=[pl.BlockSpec(memory_space=pltpu.SMEM), pl.BlockSpec(memory_space=pltpu.VMEM)],
+        out_shape=jax.ShapeDtypeStruct(shape, fields[0].dtype),
+        in_specs=[pl.BlockSpec(memory_space=pltpu.SMEM)] + [pl.BlockSpec(memory_space=pltpu.VMEM)] * len(fields),
         out_specs=pl.BlockSpec(memory_space=pltpu.VMEM),
-        cost_estimate=pl.CostEstimate(flops=0, transcendentals=0, bytes_accessed=2 * field.size * 4),
-    )(order, field)
+        cost_estimate=pl.CostEstimate(flops=0, transcendentals=0, bytes_accessed=2 * len(fields) * fields[0].size * 4),
+    )(order, *fields)
 
 
 def shards(noise, inv_diag, coupling, order):
@@ -153,7 +155,7 @@
         leaving = chain(entering, step == 0)[0]
         entering = entering + lax.ppermute(leaving, "tm", [(sender, sender - 1)])
     finals = chain(entering, False)
-    return pick_rows(jnp.stack(finals, axis=0), order)
+    return pick_rows(finals, order)
 
 
 def solution(mesh):

time: 304 us -> 305 us (level)
  no operation moved by 1% of the time
where the time goes in v2:
time: 305 us; the launch traced here: 304 us
  waiting for transfers between devices  206 us (68%)
  starting transfers between devices  52.5 us (17%)
  matrix products  19.9 us (7%)
  other arithmetic  13.9 us (5%)
  local copies, waits for them, and re-layouts  5.73 us (2%)
  Pallas kernels  5.28 us (2%)
    ppermute x3, waiting for transfers between devices, line_reduce_scatter(): lax.ppermute(tile(me - count + step) + leftward, axis, left_route)  113 us
    ppermute x3, waiting for transfers between devices, line_all_to_all(): lax.ppermute(own_rows(me - distance), axis, [(k, k - distance) for k in r...  34.2 us
    ppermute x3, waiting for transfers between devices, line_all_to_all(): lax.ppermute(own_rows(me + distance), axis, [(k, k + distance) for k in r...  31.2 us
    ppermute x3, waiting for transfers between devices, shards(): entering = entering + lax.ppermute(leaving, 'tm', [(sender, sender - 1)])  24.3 us
    ppermute x3, starting transfers between devices, line_reduce_scatter(): lax.ppermute(tile(me - count + step) + leftward, axis, left_route)  23.3 us
    dot_general x18, matrix products, bdot(): return jnp.dot(left, right, preferred_element_type=jnp.float32)  19.9 us
    ppermute x3, starting transfers between devices, line_all_to_all(): lax.ppermute(own_rows(me - distance), axis, [(k, k - distance) for k in r...  7.67 us
    add x2, other arithmetic, line_reduce_scatter(): tile(me - count + step) + leftward  6.65 us
  transfers between devices with their start and end apart: 21, of which 11 were waited for; matrix products, arithmetic and copies ran while one was open for 6% of the time, Pallas kernels for 0%

profile of v2, /device:TPU:25, one launch (start us, length us, event | category | flops | bytes accessed | tf_op | source)
XLA Modules:
  0.0 304.2 jit_solution(4338862805466416513)
XLA Ops:
  1.9 1.4 collective-permute-start
  3.3 4.0 %collective-permute-start.1 = (f32[2,256,256]{2,1,0:T(8,128)S(1)}, f32[2,256,256]{2,1,0:T(8,128)S(1)}, u32[]{:S(2)}, u32[]{:S(2)}) collective-permute-start(f32[2,256,256]{2,1,0:T(8,128)S(1)} %get-tuple-element.24), channel_id=1, source_target_pairs={{1,0},{2,1},{3,2},{5,4},{6,5},{7,6},{9,8},{10,9},{11,10},{13,12},{... | collective-permute-start | bytes 1572872 | tf_op jit(solution)/shard_map/ppermute | solution.py:94
  10.0 4.1 %collective-permute-start.13 = (f32[2,1024,256]{2,1,0:T(8,128)S(1)}, f32[2,1024,256]{2,1,0:T(8,128)S(1)}, u32[]{:S(2)}, u32[]{:S(2)}) collective-permute-start(f32[2,1024,256]{2,1,0:T(8,128)S(1)} %copy-done.3), channel_id=1, source_target_pairs={{1,0},{2,1},{3,2},{5,4},{6,5},{7,6},{9,8},{10,9},{11,10},{13,12},{... | collective-permute-start | bytes 6291464 | tf_op jit(solution)/shard_map/ppermute | solution.py:76
  14.1 2.6 collective-permute-done
  16.7 2.3 collective-permute-start.3
  20.6 18.5 %collective-permute-done.2 = f32[2,256,256]{2,1,0:T(8,128)S(1)} collective-permute-done((f32[2,256,256]{2,1,0:T(8,128)S(1)}, f32[2,256,256]{2,1,0:T(8,128)S(1)}, u32[]{:S(2)}, u32[]{:S(2)}) %collective-permute-start.2) | collective-permute-done | bytes 524320 | tf_op jit(solution)/shard_map/ppermute | solution.py:93
  40.6 33.2 %collective-permute-done.3 = f32[2,256,256]{2,1,0:T(8,128)S(1)} collective-permute-done((f32[2,256,256]{2,1,0:T(8,128)S(1)}, f32[2,256,256]{2,1,0:T(8,128)S(1)}, u32[]{:S(2)}, u32[]{:S(2)}) %collective-permute-start.3) | collective-permute-done | bytes 524320 | tf_op jit(solution)/shard_map/ppermute | solution.py:94
  73.9 10.1 %collective-permute-done.4 = f32[2,256,256]{2,1,0:T(8,128)S(1)} collective-permute-done((f32[2,256,256]{2,1,0:T(8,128)S(1)}, f32[2,256,256]{2,1,0:T(8,128)S(1)}, u32[]{:S(2)}, u32[]{:S(2)}) %collective-permute-start.4) | collective-permute-done | bytes 524320 | tf_op jit(solution)/shard_map/ppermute | solution.py:93
  92.1 13.7 %collective-permute-start.9 = (f32[2,1024,256]{2,1,0:T(8,128)S(1)}, f32[2,1024,256]{2,1,0:T(8,128)S(1)}, u32[]{:S(2)}, u32[]{:S(2)}) collective-permute-start(f32[2,1024,256]{2,1,0:T(8,128)S(1)} %get-tuple-element.11), channel_id=1, source_target_pairs={{3,2},{7,6},{11,10},{15,14},{19,18},{23,22},{27,26},{31,30}} | collective-permute-start | bytes 6291464 | tf_op jit(solution)/shard_map/ppermute | solution.py:55
  107.9 40.8 %collective-permute-done.9 = f32[2,1024,256]{2,1,0:T(8,128)S(1)} collective-permute-done((f32[2,1024,256]{2,1,0:T(8,128)S(1)}, f32[2,1024,256]{2,1,0:T(8,128)S(1)}, u32[]{:S(2)}, u32[]{:S(2)}) %collective-permute-start.9) | collective-permute-done | bytes 2097184 | tf_op jit(solution)/shard_map/ppermute | solution.py:55
  148.7 2.2 fusion.24
  150.9 4.1 %collective-permute-start.10 = (f32[2,1024,256]{2,1,0:T(8,128)}, f32[2,1024,256]{2,1,0:T(8,128)S(1)}, u32[]{:S(2)}, u32[]{:S(2)}) collective-permute-start(f32[2,1024,256]{2,1,0:T(8,128)} %get-tuple-element.9), channel_id=1, source_target_pairs={{2,1},{3,2},{6,5},{7,6},{10,9},{11,10},{14,13},{15,14},{18,17},{19... | collective-permute-start | bytes 6291464 | tf_op jit(solution)/shard_map/ppermute | solution.py:55
  155.1 2.2 collective-permute-start.7
  160.9 36.4 %collective-permute-done.10 = f32[2,1024,256]{2,1,0:T(8,128)S(1)} collective-permute-done((f32[2,1024,256]{2,1,0:T(8,128)}, f32[2,1024,256]{2,1,0:T(8,128)S(1)}, u32[]{:S(2)}, u32[]{:S(2)}) %collective-permute-start.10) | collective-permute-done | bytes 2097184 | tf_op jit(solution)/shard_map/ppermute | solution.py:55
  198.7 4.4 %fusion.22 = (f32[2,1024,256]{2,1,0:T(8,128)}, f32[2,1024,256]{2,1,0:T(8,128)S(1)}) fusion(f32[2,1024,256]{2,1,0:T(8,128)} %copy-done.2, s32[]{:T(128)S(6)} %select_n.15, f32[1,1024,1024]{2,1,0:T(8,128)S(1)} %fusion.9, f32[1,1024,1024]{2,1,0:T(8,128)S(1)} %fusion.7, f32[2,1024,256]{2,1,0:T(8,128)} %collective-permute-done.7, s32[]{:T(128)S(6)} %select_n.16), kind=kLoop, calls=%fused_computation.45 | loop fusion | flops 2097152 | bytes 16777224 | tf_op jit(solution)/shard_map/add | solution.py:55
  203.1 5.4 %collective-permute-start.11 = (f32[2,1024,256]{2,1,0:T(8,128)}, f32[2,1024,256]{2,1,0:T(8,128)S(1)}, u32[]{:S(2)}, u32[]{:S(2)}) collective-permute-start(f32[2,1024,256]{2,1,0:T(8,128)} %get-tuple-element.7), channel_id=1, source_target_pairs={{1,0},{2,1},{3,2},{5,4},{6,5},{7,6},{9,8},{10,9},{11,10},{13,12},{... | collective-permute-start | bytes 6291464 | tf_op jit(solution)/shard_map/ppermute | solution.py:55
  214.1 35.8 %collective-permute-done.11 = f32[2,1024,256]{2,1,0:T(8,128)S(1)} collective-permute-done((f32[2,1024,256]{2,1,0:T(8,128)}, f32[2,1024,256]{2,1,0:T(8,128)S(1)}, u32[]{:S(2)}, u32[]{:S(2)}) %collective-permute-start.11) | collective-permute-done | bytes 2097184 | tf_op jit(solution)/shard_map/ppermute | solution.py:55
  249.9 3.6 %collective-permute-done.8 = f32[2,1024,256]{2,1,0:T(8,128)S(1)} collective-permute-done((f32[2,1024,256]{2,1,0:T(8,128)S(1)}, f32[2,1024,256]{2,1,0:T(8,128)S(1)}, u32[]{:S(2)}, u32[]{:S(2)}) %collective-permute-start.8) | collective-permute-done | bytes 2097184 | tf_op jit(solution)/shard_map/ppermute | solution.py:54
  261.2 1.5 collective-permute-start.19
  262.8 22.1 %collective-permute-done.19 = f32[1024,256]{1,0:T(8,128)S(1)} collective-permute-done((f32[1024,256]{1,0:T(8,128)S(1)}, f32[1024,256]{1,0:T(8,128)S(1)}, u32[]{:S(2)}, u32[]{:S(2)}) %collective-permute-start.19) | collective-permute-done | bytes 1048608 | tf_op jit(solution)/shard_map/ppermute | solution.py:156
  290.5 2.2 collective-permute-done.20
  294.2 1.8 reduce-precision_convert_fusion.2
  297.2 1.7 fusion.48.refs_0_
  298.9 5.3 %shard_map.46 = f32[2,1024,256]{2,1,0:T(8,128)} custom-call(s32[1024]{0:T(1024)} %order_ref.1, f32[1024,256]{1,0:T(8,128)} %fusion.48.refs_0_, f32[1024,256]{1,0:T(8,128)} %get-tuple-element.36.refs_1_), custom_call_target="tpu_custom_call" | custom-call | bytes 4194304 | tf_op jit(solution)/shard_map/pallas_call | solution.py:118
  (74 shorter events, 44.1 us)
Async XLA Ops:
  1.6 7.1 %copy-start.3 = (f32[2,1024,256]{2,1,0:T(8,128)S(1)}, f32[2,1024,256]{2,1,0:T(8,128)}, u32[]{:S(2)}) copy-start(f32[2,1024,256]{2,1,0:T(8,128)} %param.6) | copy-start | bytes 6291460
  1.9 14.8 %collective-permute-start = (f32[2,256,256]{2,1,0:T(8,128)S(1)}, f32[2,256,256]{2,1,0:T(8,128)S(1)}, u32[]{:S(2)}, u32[]{:S(2)}) collective-permute-start(f32[2,256,256]{2,1,0:T(8,128)S(1)} %get-tuple-element.25), channel_id=1, source_target_pairs={{0,1},{1,2},{2,3},{4,5},{5,6},{6,7},{8,9},{9,10},{10,11},{12,13},{... | collective-permute-start | bytes 1572872 | tf_op jit(solution)/shard_map/ppermute | solution.py:93
  3.3 15.9 %collective-permute-start.1 = (f32[2,256,256]{2,1,0:T(8,128)S(1)}, f32[2,256,256]{2,1,0:T(8,128)S(1)}, u32[]{:S(2)}, u32[]{:S(2)}) collective-permute-start(f32[2,256,256]{2,1,0:T(8,128)S(1)} %get-tuple-element.24), channel_id=1, source_target_pairs={{1,0},{2,1},{3,2},{5,4},{6,5},{7,6},{9,8},{10,9},{11,10},{13,12},{... | collective-permute-start | bytes 1572872 | tf_op jit(solution)/shard_map/ppermute | solution.py:94
  7.4 31.8 %collective-permute-start.2 = (f32[2,256,256]{2,1,0:T(8,128)S(1)}, f32[2,256,256]{2,1,0:T(8,128)S(1)}, u32[]{:S(2)}, u32[]{:S(2)}) collective-permute-start(f32[2,256,256]{2,1,0:T(8,128)S(1)} %get-tuple-element.23), channel_id=1, source_target_pairs={{0,2},{1,3},{4,6},{5,7},{8,10},{9,11},{12,14},{13,15},{16,18},{17,... | collective-permute-start | bytes 1572872 | tf_op jit(solution)/shard_map/ppermute | solution.py:93
  8.7 97.1 %collective-permute-start.12 = (f32[2,1024,256]{2,1,0:T(8,128)S(1)}, f32[2,1024,256]{2,1,0:T(8,128)S(1)}, u32[]{:S(2)}, u32[]{:S(2)}) collective-permute-start(f32[2,1024,256]{2,1,0:T(8,128)S(1)} %copy-done.3), channel_id=1, source_target_pairs={{0,1},{1,2},{2,3},{4,5},{5,6},{6,7},{8,9},{9,10},{10,11},{12,13},{... | collective-permute-start | bytes 6291464 | tf_op jit(solution)/shard_map/ppermute | solution.py:75
  10.0 97.1 %collective-permute-start.13 = (f32[2,1024,256]{2,1,0:T(8,128)S(1)}, f32[2,1024,256]{2,1,0:T(8,128)S(1)}, u32[]{:S(2)}, u32[]{:S(2)}) collective-permute-start(f32[2,1024,256]{2,1,0:T(8,128)S(1)} %copy-done.3), channel_id=1, source_target_pairs={{1,0},{2,1},{3,2},{5,4},{6,5},{7,6},{9,8},{10,9},{11,10},{13,12},{... | collective-permute-start | bytes 6291464 | tf_op jit(solution)/shard_map/ppermute | solution.py:76
  16.7 57.1 %collective-permute-start.3 = (f32[2,256,256]{2,1,0:T(8,128)S(1)}, f32[2,256,256]{2,1,0:T(8,128)S(1)}, u32[]{:S(2)}, u32[]{:S(2)}) collective-permute-start(f32[2,256,256]{2,1,0:T(8,128)S(1)} %get-tuple-element.22), channel_id=1, source_target_pairs={{2,0},{3,1},{6,4},{7,5},{10,8},{11,9},{14,12},{15,13},{18,16},{19,... | collective-permute-start | bytes 1572872 | tf_op jit(solution)/shard_map/ppermute | solution.py:94
  19.2 64.8 %collective-permute-start.4 = (f32[2,256,256]{2,1,0:T(8,128)S(1)}, f32[2,256,256]{2,1,0:T(8,128)S(1)}, u32[]{:S(2)}, u32[]{:S(2)}) collective-permute-start(f32[2,256,256]{2,1,0:T(8,128)S(1)} %get-tuple-element.27), channel_id=1, source_target_pairs={{0,3},{4,7},{8,11},{12,15},{16,19},{20,23},{24,27},{28,31}} | collective-permute-start | bytes 1572872 | tf_op jit(solution)/shard_map/ppermute | solution.py:93
  39.1 45.9 %collective-permute-start.5 = (f32[2,256,256]{2,1,0:T(8,128)S(1)}, f32[2,256,256]{2,1,0:T(8,128)S(1)}, u32[]{:S(2)}, u32[]{:S(2)}) collective-permute-start(f32[2,256,256]{2,1,0:T(8,128)S(1)} %get-tuple-element.21), channel_id=1, source_target_pairs={{3,0},{7,4},{11,8},{15,12},{19,16},{23,20},{27,24},{31,28}} | collective-permute-start | bytes 1572872 | tf_op jit(solution)/shard_map/ppermute | solution.py:94
  85.2 1.6 copy-start
  91.3 16.6 %collective-permute-start.6 = (f32[2,1024,256]{2,1,0:T(8,128)S(1)}, f32[2,1024,256]{2,1,0:T(8,128)S(1)}, u32[]{:S(2)}, u32[]{:S(2)}) collective-permute-start(f32[2,1024,256]{2,1,0:T(8,128)S(1)} %get-tuple-element.12), channel_id=1, source_target_pairs={{0,1},{4,5},{8,9},{12,13},{16,17},{20,21},{24,25},{28,29}} | collective-permute-start | bytes 6291464 | tf_op jit(solution)/shard_map/ppermute | solution.py:54
  92.1 56.6 %collective-permute-start.9 = (f32[2,1024,256]{2,1,0:T(8,128)S(1)}, f32[2,1024,256]{2,1,0:T(8,128)S(1)}, u32[]{:S(2)}, u32[]{:S(2)}) collective-permute-start(f32[2,1024,256]{2,1,0:T(8,128)S(1)} %get-tuple-element.11), channel_id=1, source_target_pairs={{3,2},{7,6},{11,10},{15,14},{19,18},{23,22},{27,26},{31,30}} | collective-permute-start | bytes 6291464 | tf_op jit(solution)/shard_map/ppermute | solution.py:55
  105.8 51.4 %collective-permute-start.14 = (f32[2,1024,256]{2,1,0:T(8,128)S(1)}, f32[2,1024,256]{2,1,0:T(8,128)S(1)}, u32[]{:S(2)}, u32[]{:S(2)}) collective-permute-start(f32[2,1024,256]{2,1,0:T(8,128)S(1)} %collective-permute-done.12), channel_id=1, source_target_pairs={{1,2},{2,3},{5,6},{6,7},{9,10},{10,11},{13,14},{14,15},{17,18},{18... | collective-permute-start | bytes 6291464 | tf_op jit(solution)/shard_map/ppermute | solution.py:75
  107.1 51.4 %collective-permute-start.15 = (f32[2,1024,256]{2,1,0:T(8,128)S(1)}, f32[2,1024,256]{2,1,0:T(8,128)S(1)}, u32[]{:S(2)}, u32[]{:S(2)}) collective-permute-start(f32[2,1024,256]{2,1,0:T(8,128)S(1)} %collective-permute-done.13), channel_id=1, source_target_pairs={{1,0},{2,1},{5,4},{6,5},{9,8},{10,9},{13,12},{14,13},{17,16},{18,1... | collective-permute-start | bytes 6291464 | tf_op jit(solution)/shard_map/ppermute | solution.py:76
  150.9 46.4 %collective-permute-start.10 = (f32[2,1024,256]{2,1,0:T(8,128)}, f32[2,1024,256]{2,1,0:T(8,128)S(1)}, u32[]{:S(2)}, u32[]{:S(2)}) collective-permute-start(f32[2,1024,256]{2,1,0:T(8,128)} %get-tuple-element.9), channel_id=1, source_target_pairs={{2,1},{3,2},{6,5},{7,6},{10,9},{11,10},{14,13},{15,14},{18,17},{19... | collective-permute-start | bytes 6291464 | tf_op jit(solution)/shard_map/ppermute | solution.py:55
  155.1 5.5 %copy-start.4 = (f32[2,1024,256]{2,1,0:T(8,128)S(1)}, f32[2,1024,256]{2,1,0:T(8,128)}, u32[]{:S(2)}) copy-start(f32[2,1024,256]{2,1,0:T(8,128)} %param.6) | copy-start | bytes 6291460
  155.1 43.6 %collective-permute-start.7 = (f32[2,1024,256]{2,1,0:T(8,128)S(1)}, f32[2,1024,256]{2,1,0:T(8,128)}, u32[]{:S(2)}, u32[]{:S(2)}) collective-permute-start(f32[2,1024,256]{2,1,0:T(8,128)S(1)} %get-tuple-element.10), channel_id=1, source_target_pairs={{0,1},{1,2},{4,5},{5,6},{8,9},{9,10},{12,13},{13,14},{16,17},{17,1... | collective-permute-start | bytes 6291464 | tf_op jit(solution)/shard_map/ppermute | solution.py:54
  157.2 55.3 %collective-permute-start.16 = (f32[2,1024,256]{2,1,0:T(8,128)S(1)}, f32[2,1024,256]{2,1,0:T(8,128)S(1)}, u32[]{:S(2)}, u32[]{:S(2)}) collective-permute-start(f32[2,1024,256]{2,1,0:T(8,128)S(1)} %collective-permute-done.14), channel_id=1, source_target_pairs={{2,3},{6,7},{10,11},{14,15},{18,19},{22,23},{26,27},{30,31}} | collective-permute-start | bytes 6291464 | tf_op jit(solution)/shard_map/ppermute | solution.py:75
  158.5 54.6 %collective-permute-start.17 = (f32[2,1024,256]{2,1,0:T(8,128)S(1)}, f32[2,1024,256]{2,1,0:T(8,128)S(1)}, u32[]{:S(2)}, u32[]{:S(2)}) collective-permute-start(f32[2,1024,256]{2,1,0:T(8,128)S(1)} %collective-permute-done.15), channel_id=1, source_target_pairs={{1,0},{5,4},{9,8},{13,12},{17,16},{21,20},{25,24},{29,28}} | collective-permute-start | bytes 6291464 | tf_op jit(solution)/shard_map/ppermute | solution.py:76
  203.1 46.8 %collective-permute-start.11 = (f32[2,1024,256]{2,1,0:T(8,128)}, f32[2,1024,256]{2,1,0:T(8,128)S(1)}, u32[]{:S(2)}, u32[]{:S(2)}) collective-permute-start(f32[2,1024,256]{2,1,0:T(8,128)} %get-tuple-element.7), channel_id=1, source_target_pairs={{1,0},{2,1},{3,2},{5,4},{6,5},{7,6},{9,8},{10,9},{11,10},{13,12},{... | collective-permute-start | bytes 6291464 | tf_op jit(solution)/shard_map/ppermute | solution.py:55
  208.6 45.0 %collective-permute-start.8 = (f32[2,1024,256]{2,1,0:T(8,128)S(1)}, f32[2,1024,256]{2,1,0:T(8,128)S(1)}, u32[]{:S(2)}, u32[]{:S(2)}) collective-permute-start(f32[2,1024,256]{2,1,0:T(8,128)S(1)} %get-tuple-element.8), channel_id=1, source_target_pairs={{0,1},{1,2},{2,3},{4,5},{5,6},{6,7},{8,9},{9,10},{10,11},{12,13},{... | collective-permute-start | bytes 6291464 | tf_op jit(solution)/shard_map/ppermute | solution.py:54
  256.3 0.7 collective-permute-start.18
  261.2 23.6 %collective-permute-start.19 = (f32[1024,256]{1,0:T(8,128)S(1)}, f32[1024,256]{1,0:T(8,128)S(1)}, u32[]{:S(2)}, u32[]{:S(2)}) collective-permute-start(f32[1024,256]{1,0:T(8,128)S(1)} %fusion.56), channel_id=1, source_target_pairs={{8,4},{9,5},{10,6},{11,7},{24,20},{25,21},{26,22},{27,23}} | collective-permute-start | bytes 3145736 | tf_op jit(solution)/shard_map/ppermute | solution.py:156
  289.2 3.6 %collective-permute-start.20 = (f32[1024,256]{1,0:T(8,128)S(1)}, f32[1024,256]{1,0:T(8,128)S(1)}, u32[]{:S(2)}, u32[]{:S(2)}) collective-permute-start(f32[1024,256]{1,0:T(8,128)S(1)} %fusion.52), channel_id=1, source_target_pairs={{4,0},{5,1},{6,2},{7,3},{20,16},{21,17},{22,18},{23,19}} | collective-permute-start | bytes 3145736 | tf_op jit(solution)/shard_map/ppermute | solution.py:156
  (2 other events, 2.9 us)

commit v3 on v1

--- a/solution.py
+++ b/solution.py
@@ -37,7 +37,7 @@
     return both[:, :width] + (both[:, width:] + bdot(small, operand_high))
 
 
-def line_reduce_scatter(partial, axis):
+def line_reduce_scatter(partial, axis, ready=None):
     count = lax.axis_size(axis)
     me = lax.axis_index(axis)
     width = partial.shape[2] // count
@@ -53,7 +53,9 @@
         left_route = [(k, k - 1) for k in range(max(count - step, 1), count)]
         rightward = lax.ppermute(tile(me + count - step) + rightward, axis, right_route)
         leftward = lax.ppermute(tile(me - count + step) + leftward, axis, left_route)
-    return tile(me) + (rightward + leftward)
+    if ready is not None:
+        rightward, leftward, ready = lax.optimization_barrier((rightward, leftward, ready))
+    return tile(me) + (rightward + leftward), ready
 
 
 def add_at(whole, piece, slot, axis):
@@ -131,9 +133,12 @@
     partial = jnp.stack(
         [apply(split(inv_diag[block], 2), noise_rows[block]) for block in range(block_count)], axis=0
     )
-    driven_all = line_reduce_scatter(partial, "cols")
+    coupling_parts = [split(coupling_full[block], 2) for block in range(block_count)]
+    across = coupling_full[block_count - 1]
+    for block in range(block_count - 2, -1, -1):
+        across = apply(coupling_parts[block], across)
+    driven_all, across_parts = line_reduce_scatter(partial, "cols", split(across, 2))
     driven = [driven_all[block] for block in range(block_count)]
-    coupling_parts = [split(coupling_full[block], 2) for block in range(block_count)]
 
     def chain(entering, skip_last):
         carried = entering
@@ -146,11 +151,12 @@
             results[block] = carried
         return results
 
+    local = chain(None, True)[0]
     relays = lax.axis_size("tm")
     entering = jnp.zeros_like(driven[0])
     for step in range(relays - 1):
         sender = relays - 1 - step
-        leaving = chain(entering, step == 0)[0]
+        leaving = local if step == 0 else local + apply(across_parts, entering)
         entering = entering + lax.ppermute(leaving, "tm", [(sender, sender - 1)])
     finals = chain(entering, False)
     return pick_rows(jnp.stack(finals, axis=0), order)

time: 304 us -> 304 us (level)
  waiting for transfers between devices: 206 us -> 194 us
  matrix products: 18 us -> 26.1 us
    ppermute x3, waiting for transfers between devices: 113 us -> 101 us  [line_reduce_scatter(): lax.ppermute(tile(me - count + step) + leftward, axis, left_route)]
    dot_general x18 -> x16, matrix products: 18 us -> 26.1 us  [bdot(): return jnp.dot(left, right, preferred_element_type=jnp.float32)]
  transfers between devices with their start and end apart: 21 -> 21, of which waited for: 11 -> 11; matrix products, arithmetic and copies ran while one was open for 6% -> 10% of each run, Pallas kernels for 0% -> 0%
where the time goes in v3:
time: 304 us; the launch traced here: 303 us
  waiting for transfers between devices  194 us (64%)
  starting transfers between devices  54.4 us (18%)
  matrix products  26.1 us (9%)
  other arithmetic  18.3 us (6%)
  Pallas kernels  5.24 us (2%)
  local copies, waits for them, and re-layouts  4.42 us (1%)
    ppermute x3, waiting for transfers between devices, line_reduce_scatter(): lax.ppermute(tile(me - count + step) + leftward, axis, left_route)  101 us
    ppermute x3, waiting for transfers between devices, line_all_to_all(): lax.ppermute(own_rows(me - distance), axis, [(k, k - distance) for k in r...  34.1 us
    ppermute x3, waiting for transfers between devices, line_all_to_all(): lax.ppermute(own_rows(me + distance), axis, [(k, k + distance) for k in r...  31.1 us
    dot_general x16, matrix products, bdot(): return jnp.dot(left, right, preferred_element_type=jnp.float32)  26.1 us
    ppermute x3, starting transfers between devices, line_reduce_scatter(): lax.ppermute(tile(me - count + step) + leftward, axis, left_route)  25.1 us
    ppermute x3, waiting for transfers between devices, shards(): entering = entering + lax.ppermute(leaving, 'tm', [(sender, sender - 1)])  24.3 us
    ppermute x3, starting transfers between devices, line_all_to_all(): lax.ppermute(own_rows(me - distance), axis, [(k, k - distance) for k in r...  7.67 us
    add x2, other arithmetic, line_reduce_scatter(): tile(me - count + step) + leftward  7.29 us
  transfers between devices with their start and end apart: 21, of which 11 were waited for; matrix products, arithmetic and copies ran while one was open for 10% of the time, Pallas kernels for 0%

profile of v3, /device:TPU:25, one launch (start us, length us, event | category | flops | bytes accessed | tf_op | source)
XLA Modules:
  0.0 303.3 jit_solution(7241445002633248724)
XLA Ops:
  3.3 4.0 %collective-permute-start.1 = (f32[2,256,256]{2,1,0:T(8,128)S(1)}, f32[2,256,256]{2,1,0:T(8,128)S(1)}, u32[]{:S(2)}, u32[]{:S(2)}) collective-permute-start(f32[2,256,256]{2,1,0:T(8,128)S(1)} %get-tuple-element.38), channel_id=1, source_target_pairs={{1,0},{2,1},{3,2},{5,4},{6,5},{7,6},{9,8},{10,9},{11,10},{13,12},{... | collective-permute-start | bytes 1572872 | tf_op jit(solution)/shard_map/ppermute | solution.py:96
  10.0 4.1 %collective-permute-start.13 = (f32[2,1024,256]{2,1,0:T(8,128)S(1)}, f32[2,1024,256]{2,1,0:T(8,128)S(1)}, u32[]{:S(2)}, u32[]{:S(2)}) collective-permute-start(f32[2,1024,256]{2,1,0:T(8,128)S(1)} %copy-done.2), channel_id=1, source_target_pairs={{1,0},{2,1},{3,2},{5,4},{6,5},{7,6},{9,8},{10,9},{11,10},{13,12},{... | collective-permute-start | bytes 6291464 | tf_op jit(solution)/shard_map/ppermute | solution.py:78
  14.1 2.6 collective-permute-done
  16.7 2.3 collective-permute-start.3
  20.6 18.5 %collective-permute-done.2 = f32[2,256,256]{2,1,0:T(8,128)S(1)} collective-permute-done((f32[2,256,256]{2,1,0:T(8,128)S(1)}, f32[2,256,256]{2,1,0:T(8,128)S(1)}, u32[]{:S(2)}, u32[]{:S(2)}) %collective-permute-start.2) | collective-permute-done | bytes 524320 | tf_op jit(solution)/shard_map/ppermute | solution.py:95
  40.6 33.2 %collective-permute-done.3 = f32[2,256,256]{2,1,0:T(8,128)S(1)} collective-permute-done((f32[2,256,256]{2,1,0:T(8,128)S(1)}, f32[2,256,256]{2,1,0:T(8,128)S(1)}, u32[]{:S(2)}, u32[]{:S(2)}) %collective-permute-start.3) | collective-permute-done | bytes 524320 | tf_op jit(solution)/shard_map/ppermute | solution.py:96
  73.9 10.0 %collective-permute-done.4 = f32[2,256,256]{2,1,0:T(8,128)S(1)} collective-permute-done((f32[2,256,256]{2,1,0:T(8,128)S(1)}, f32[2,256,256]{2,1,0:T(8,128)S(1)}, u32[]{:S(2)}, u32[]{:S(2)}) %collective-permute-start.4) | collective-permute-done | bytes 524320 | tf_op jit(solution)/shard_map/ppermute | solution.py:95
  92.1 13.7 %collective-permute-start.9 = (f32[2,1024,256]{2,1,0:T(8,128)S(1)}, f32[2,1024,256]{2,1,0:T(8,128)S(1)}, u32[]{:S(2)}, u32[]{:S(2)}) collective-permute-start(f32[2,1024,256]{2,1,0:T(8,128)S(1)} %get-tuple-element.23), channel_id=1, source_target_pairs={{3,2},{7,6},{11,10},{15,14},{19,18},{23,22},{27,26},{31,30}} | collective-permute-start | bytes 6291464 | tf_op jit(solution)/shard_map/ppermute | solution.py:55
  107.9 40.8 %collective-permute-done.9 = f32[2,1024,256]{2,1,0:T(8,128)S(1)} collective-permute-done((f32[2,1024,256]{2,1,0:T(8,128)S(1)}, f32[2,1024,256]{2,1,0:T(8,128)S(1)}, u32[]{:S(2)}, u32[]{:S(2)}) %collective-permute-start.9) | collective-permute-done | bytes 2097184 | tf_op jit(solution)/shard_map/ppermute | solution.py:55
  148.7 2.8 fusion.34
  151.5 4.3 %collective-permute-start.10 = (f32[2,1024,256]{2,1,0:T(8,128)}, f32[2,1024,256]{2,1,0:T(8,128)S(1)}, u32[]{:S(2)}, u32[]{:S(2)}) collective-permute-start(f32[2,1024,256]{2,1,0:T(8,128)} %get-tuple-element.21), channel_id=1, source_target_pairs={{2,1},{3,2},{6,5},{7,6},{10,9},{11,10},{14,13},{15,14},{18,17},{19... | collective-permute-start | bytes 6291464 | tf_op jit(solution)/shard_map/ppermute | solution.py:55
  155.8 2.1 collective-permute-start.7
  164.1 34.0 %collective-permute-done.10 = f32[2,1024,256]{2,1,0:T(8,128)S(1)} collective-permute-done((f32[2,1024,256]{2,1,0:T(8,128)}, f32[2,1024,256]{2,1,0:T(8,128)S(1)}, u32[]{:S(2)}, u32[]{:S(2)}) %collective-permute-start.10) | collective-permute-done | bytes 2097184 | tf_op jit(solution)/shard_map/ppermute | solution.py:55
  198.1 4.5 %fusion.32 = (f32[2,1024,256]{2,1,0:T(8,128)}, f32[2,1024,256]{2,1,0:T(8,128)}) fusion(f32[2,1024,256]{2,1,0:T(8,128)S(1)} %collective-permute-done.10, s32[]{:T(128)S(6)} %select_n.15, f32[1,1024,1024]{2,1,0:T(8,128)S(1)} %fusion.12, f32[1,1024,1024]{2,1,0:T(8,128)S(1)} %fusion.10, f32[2,1024,256]{2,1,0:T(8,128)} %collective-permute-done.7, s32[]{:T(128)S(6)} %select_n.16), kind=kLoop, calls=%fused_computation.57 | loop fusion | flops 2097152 | bytes 16777224 | tf_op jit(solution)/shard_map/add | solution.py:55
  202.6 7.1 %collective-permute-start.11 = (f32[2,1024,256]{2,1,0:T(8,128)}, f32[2,1024,256]{2,1,0:T(8,128)S(1)}, u32[]{:S(2)}, u32[]{:S(2)}) collective-permute-start(f32[2,1024,256]{2,1,0:T(8,128)} %get-tuple-element.19), channel_id=1, source_target_pairs={{1,0},{2,1},{3,2},{5,4},{6,5},{7,6},{9,8},{10,9},{11,10},{13,12},{... | collective-permute-start | bytes 6291464 | tf_op jit(solution)/shard_map/ppermute | solution.py:55
  213.3 7.0 %fusion.13 = f32[1024,2048]{1,0:T(8,128)} fusion(bf16[1024,1024]{1,0:T(8,128)(2,1)S(1)} %get-tuple-element.18, bf16[1024,1024]{1,0:T(8,128)(2,1)S(1)} %get-tuple-element.17, f32[2,1024,1024]{2,1,0:T(8,128)S(1)} %add_dynamic-update-slice_fusion), kind=kOutput, calls=%fused_computation.39 | convolution fusion | flops 4305453056 | bytes 16777216 | tf_op jit(solution)/shard_map/dot_general | solution.py:29
  220.2 5.0 %fusion.5 = (bf16[1024,1024]{1,0:T(8,128)(2,1)S(1)}, bf16[1024,1024]{1,0:T(8,128)(2,1)S(1)}) fusion(f32[2,1024,1024]{2,1,0:T(8,128)S(1)} %add_dynamic-update-slice_fusion, f32[1024,2048]{1,0:T(8,128)} %fusion.13), kind=kOutput, calls=%fused_computation.28 | convolution fusion | flops 2161115136 | bytes 20971520 | tf_op jit(solution)/shard_map/dot_general | solution.py:29
  225.2 25.9 %collective-permute-done.11 = f32[2,1024,256]{2,1,0:T(8,128)S(1)} collective-permute-done((f32[2,1024,256]{2,1,0:T(8,128)}, f32[2,1024,256]{2,1,0:T(8,128)S(1)}, u32[]{:S(2)}, u32[]{:S(2)}) %collective-permute-start.11) | collective-permute-done | bytes 2097184 | tf_op jit(solution)/shard_map/ppermute | solution.py:55
  251.1 4.0 %collective-permute-done.8 = f32[2,1024,256]{2,1,0:T(8,128)} collective-permute-done((f32[2,1024,256]{2,1,0:T(8,128)}, f32[2,1024,256]{2,1,0:T(8,128)}, u32[]{:S(2)}, u32[]{:S(2)}) %collective-permute-start.8) | collective-permute-done | bytes 2097184 | tf_op jit(solution)/shard_map/ppermute | solution.py:54
  255.1 2.4 fusion.25
  264.2 22.1 %collective-permute-done.19 = f32[1024,256]{1,0:T(8,128)S(1)} collective-permute-done((f32[1024,256]{1,0:T(8,128)S(1)}, f32[1024,256]{1,0:T(8,128)S(1)}, u32[]{:S(2)}, u32[]{:S(2)}) %collective-permute-start.19) | collective-permute-done | bytes 1048608 | tf_op jit(solution)/shard_map/ppermute | solution.py:160
  290.0 2.2 collective-permute-done.20
  296.5 1.5 pad_maximum_fusion.field_ref
  298.0 5.2 %shard_map.46 = f32[2,1024,256]{2,1,0:T(8,128)} custom-call(s32[1024]{0:T(1024)} %order_ref.1, f32[2,1024,256]{2,1,0:T(8,128)} %pad_maximum_fusion.field_ref), custom_call_target="tpu_custom_call" | custom-call | bytes 4194304 | tf_op jit(solution)/shard_map/pallas_call | solution.py:118
  (72 shorter events, 43.3 us)
Async XLA Ops:
  1.6 7.1 %copy-start.2 = (f32[2,1024,256]{2,1,0:T(8,128)S(1)}, f32[2,1024,256]{2,1,0:T(8,128)}, u32[]{:S(2)}) copy-start(f32[2,1024,256]{2,1,0:T(8,128)} %param.6) | copy-start | bytes 6291460
  1.9 14.8 %collective-permute-start = (f32[2,256,256]{2,1,0:T(8,128)S(1)}, f32[2,256,256]{2,1,0:T(8,128)S(1)}, u32[]{:S(2)}, u32[]{:S(2)}) collective-permute-start(f32[2,256,256]{2,1,0:T(8,128)S(1)} %get-tuple-element.39), channel_id=1, source_target_pairs={{0,1},{1,2},{2,3},{4,5},{5,6},{6,7},{8,9},{9,10},{10,11},{12,13},{... | collective-permute-start | bytes 1572872 | tf_op jit(solution)/shard_map/ppermute | solution.py:95
  3.3 15.9 %collective-permute-start.1 = (f32[2,256,256]{2,1,0:T(8,128)S(1)}, f32[2,256,256]{2,1,0:T(8,128)S(1)}, u32[]{:S(2)}, u32[]{:S(2)}) collective-permute-start(f32[2,256,256]{2,1,0:T(8,128)S(1)} %get-tuple-element.38), channel_id=1, source_target_pairs={{1,0},{2,1},{3,2},{5,4},{6,5},{7,6},{9,8},{10,9},{11,10},{13,12},{... | collective-permute-start | bytes 1572872 | tf_op jit(solution)/shard_map/ppermute | solution.py:96
  7.4 31.8 %collective-permute-start.2 = (f32[2,256,256]{2,1,0:T(8,128)S(1)}, f32[2,256,256]{2,1,0:T(8,128)S(1)}, u32[]{:S(2)}, u32[]{:S(2)}) collective-permute-start(f32[2,256,256]{2,1,0:T(8,128)S(1)} %get-tuple-element.37), channel_id=1, source_target_pairs={{0,2},{1,3},{4,6},{5,7},{8,10},{9,11},{12,14},{13,15},{16,18},{17,... | collective-permute-start | bytes 1572872 | tf_op jit(solution)/shard_map/ppermute | solution.py:95
  8.7 97.1 %collective-permute-start.12 = (f32[2,1024,256]{2,1,0:T(8,128)S(1)}, f32[2,1024,256]{2,1,0:T(8,128)S(1)}, u32[]{:S(2)}, u32[]{:S(2)}) collective-permute-start(f32[2,1024,256]{2,1,0:T(8,128)S(1)} %copy-done.2), channel_id=1, source_target_pairs={{0,1},{1,2},{2,3},{4,5},{5,6},{6,7},{8,9},{9,10},{10,11},{12,13},{... | collective-permute-start | bytes 6291464 | tf_op jit(solution)/shard_map/ppermute | solution.py:77
  10.0 97.1 %collective-permute-start.13 = (f32[2,1024,256]{2,1,0:T(8,128)S(1)}, f32[2,1024,256]{2,1,0:T(8,128)S(1)}, u32[]{:S(2)}, u32[]{:S(2)}) collective-permute-start(f32[2,1024,256]{2,1,0:T(8,128)S(1)} %copy-done.2), channel_id=1, source_target_pairs={{1,0},{2,1},{3,2},{5,4},{6,5},{7,6},{9,8},{10,9},{11,10},{13,12},{... | collective-permute-start | bytes 6291464 | tf_op jit(solution)/shard_map/ppermute | solution.py:78
  16.7 57.1 %collective-permute-start.3 = (f32[2,256,256]{2,1,0:T(8,128)S(1)}, f32[2,256,256]{2,1,0:T(8,128)S(1)}, u32[]{:S(2)}, u32[]{:S(2)}) collective-permute-start(f32[2,256,256]{2,1,0:T(8,128)S(1)} %get-tuple-element.36), channel_id=1, source_target_pairs={{2,0},{3,1},{6,4},{7,5},{10,8},{11,9},{14,12},{15,13},{18,16},{19,... | collective-permute-start | bytes 1572872 | tf_op jit(solution)/shard_map/ppermute | solution.py:96
  19.2 64.8 %collective-permute-start.4 = (f32[2,256,256]{2,1,0:T(8,128)S(1)}, f32[2,256,256]{2,1,0:T(8,128)S(1)}, u32[]{:S(2)}, u32[]{:S(2)}) collective-permute-start(f32[2,256,256]{2,1,0:T(8,128)S(1)} %get-tuple-element.41), channel_id=1, source_target_pairs={{0,3},{4,7},{8,11},{12,15},{16,19},{20,23},{24,27},{28,31}} | collective-permute-start | bytes 1572872 | tf_op jit(solution)/shard_map/ppermute | solution.py:95
  39.1 45.9 %collective-permute-start.5 = (f32[2,256,256]{2,1,0:T(8,128)S(1)}, f32[2,256,256]{2,1,0:T(8,128)S(1)}, u32[]{:S(2)}, u32[]{:S(2)}) collective-permute-start(f32[2,256,256]{2,1,0:T(8,128)S(1)} %get-tuple-element.35), channel_id=1, source_target_pairs={{3,0},{7,4},{11,8},{15,12},{19,16},{23,20},{27,24},{31,28}} | collective-permute-start | bytes 1572872 | tf_op jit(solution)/shard_map/ppermute | solution.py:96
  85.2 1.6 copy-start
  91.3 16.6 %collective-permute-start.6 = (f32[2,1024,256]{2,1,0:T(8,128)S(1)}, f32[2,1024,256]{2,1,0:T(8,128)S(1)}, u32[]{:S(2)}, u32[]{:S(2)}) collective-permute-start(f32[2,1024,256]{2,1,0:T(8,128)S(1)} %get-tuple-element.24), channel_id=1, source_target_pairs={{0,1},{4,5},{8,9},{12,13},{16,17},{20,21},{24,25},{28,29}} | collective-permute-start | bytes 6291464 | tf_op jit(solution)/shard_map/ppermute | solution.py:54
  92.1 56.6 %collective-permute-start.9 = (f32[2,1024,256]{2,1,0:T(8,128)S(1)}, f32[2,1024,256]{2,1,0:T(8,128)S(1)}, u32[]{:S(2)}, u32[]{:S(2)}) collective-permute-start(f32[2,1024,256]{2,1,0:T(8,128)S(1)} %get-tuple-element.23), channel_id=1, source_target_pairs={{3,2},{7,6},{11,10},{15,14},{19,18},{23,22},{27,26},{31,30}} | collective-permute-start | bytes 6291464 | tf_op jit(solution)/shard_map/ppermute | solution.py:55
  105.8 52.2 %collective-permute-start.14 = (f32[2,1024,256]{2,1,0:T(8,128)S(1)}, f32[2,1024,256]{2,1,0:T(8,128)S(1)}, u32[]{:S(2)}, u32[]{:S(2)}) collective-permute-start(f32[2,1024,256]{2,1,0:T(8,128)S(1)} %collective-permute-done.12), channel_id=1, source_target_pairs={{1,2},{2,3},{5,6},{6,7},{9,10},{10,11},{13,14},{14,15},{17,18},{18... | collective-permute-start | bytes 6291464 | tf_op jit(solution)/shard_map/ppermute | solution.py:77
  107.1 52.2 %collective-permute-start.15 = (f32[2,1024,256]{2,1,0:T(8,128)S(1)}, f32[2,1024,256]{2,1,0:T(8,128)S(1)}, u32[]{:S(2)}, u32[]{:S(2)}) collective-permute-start(f32[2,1024,256]{2,1,0:T(8,128)S(1)} %collective-permute-done.13), channel_id=1, source_target_pairs={{1,0},{2,1},{5,4},{6,5},{9,8},{10,9},{13,12},{14,13},{17,16},{18,1... | collective-permute-start | bytes 6291464 | tf_op jit(solution)/shard_map/ppermute | solution.py:78
  151.5 46.6 %collective-permute-start.10 = (f32[2,1024,256]{2,1,0:T(8,128)}, f32[2,1024,256]{2,1,0:T(8,128)S(1)}, u32[]{:S(2)}, u32[]{:S(2)}) collective-permute-start(f32[2,1024,256]{2,1,0:T(8,128)} %get-tuple-element.21), channel_id=1, source_target_pairs={{2,1},{3,2},{6,5},{7,6},{10,9},{11,10},{14,13},{15,14},{18,17},{19... | collective-permute-start | bytes 6291464 | tf_op jit(solution)/shard_map/ppermute | solution.py:55
  155.8 5.5 %copy-start.3 = (f32[2,1024,256]{2,1,0:T(8,128)S(1)}, f32[2,1024,256]{2,1,0:T(8,128)}, u32[]{:S(2)}) copy-start(f32[2,1024,256]{2,1,0:T(8,128)} %param.6) | copy-start | bytes 6291460
  155.8 42.3 %collective-permute-start.7 = (f32[2,1024,256]{2,1,0:T(8,128)}, f32[2,1024,256]{2,1,0:T(8,128)}, u32[]{:S(2)}, u32[]{:S(2)}) collective-permute-start(f32[2,1024,256]{2,1,0:T(8,128)} %get-tuple-element.22), channel_id=1, source_target_pairs={{0,1},{1,2},{4,5},{5,6},{8,9},{9,10},{12,13},{13,14},{16,17},{17,1... | collective-permute-start | bytes 6291464 | tf_op jit(solution)/shard_map/ppermute | solution.py:54
  158.0 53.1 %collective-permute-start.16 = (f32[2,1024,256]{2,1,0:T(8,128)S(1)}, f32[2,1024,256]{2,1,0:T(8,128)S(1)}, u32[]{:S(2)}, u32[]{:S(2)}) collective-permute-start(f32[2,1024,256]{2,1,0:T(8,128)S(1)} %collective-permute-done.14), channel_id=1, source_target_pairs={{2,3},{6,7},{10,11},{14,15},{18,19},{22,23},{26,27},{30,31}} | collective-permute-start | bytes 6291464 | tf_op jit(solution)/shard_map/ppermute | solution.py:77
  159.3 52.3 %collective-permute-start.17 = (f32[2,1024,256]{2,1,0:T(8,128)S(1)}, f32[2,1024,256]{2,1,0:T(8,128)S(1)}, u32[]{:S(2)}, u32[]{:S(2)}) collective-permute-start(f32[2,1024,256]{2,1,0:T(8,128)S(1)} %collective-permute-done.15), channel_id=1, source_target_pairs={{1,0},{5,4},{9,8},{13,12},{17,16},{21,20},{25,24},{29,28}} | collective-permute-start | bytes 6291464 | tf_op jit(solution)/shard_map/ppermute | solution.py:78
  202.6 48.5 %collective-permute-start.11 = (f32[2,1024,256]{2,1,0:T(8,128)}, f32[2,1024,256]{2,1,0:T(8,128)S(1)}, u32[]{:S(2)}, u32[]{:S(2)}) collective-permute-start(f32[2,1024,256]{2,1,0:T(8,128)} %get-tuple-element.19), channel_id=1, source_target_pairs={{1,0},{2,1},{3,2},{5,4},{6,5},{7,6},{9,8},{10,9},{11,10},{13,12},{... | collective-permute-start | bytes 6291464 | tf_op jit(solution)/shard_map/ppermute | solution.py:55
  209.7 45.3 %collective-permute-start.8 = (f32[2,1024,256]{2,1,0:T(8,128)}, f32[2,1024,256]{2,1,0:T(8,128)}, u32[]{:S(2)}, u32[]{:S(2)}) collective-permute-start(f32[2,1024,256]{2,1,0:T(8,128)} %get-tuple-element.20), channel_id=1, source_target_pairs={{0,1},{1,2},{2,3},{4,5},{5,6},{6,7},{8,9},{9,10},{10,11},{12,13},{... | collective-permute-start | bytes 6291464 | tf_op jit(solution)/shard_map/ppermute | solution.py:54
  259.7 1.0 collective-permute-start.18
  262.9 23.4 %collective-permute-start.19 = (f32[1024,256]{1,0:T(8,128)S(1)}, f32[1024,256]{1,0:T(8,128)S(1)}, u32[]{:S(2)}, u32[]{:S(2)}) collective-permute-start(f32[1024,256]{1,0:T(8,128)S(1)} %fusion.63), channel_id=1, source_target_pairs={{8,4},{9,5},{10,6},{11,7},{24,20},{25,21},{26,22},{27,23}} | collective-permute-start | bytes 3145736 | tf_op jit(solution)/shard_map/ppermute | solution.py:160
  288.7 3.6 %collective-permute-start.20 = (f32[1024,256]{1,0:T(8,128)S(1)}, f32[1024,256]{1,0:T(8,128)S(1)}, u32[]{:S(2)}, u32[]{:S(2)}) collective-permute-start(f32[1024,256]{1,0:T(8,128)S(1)} %fusion.61), channel_id=1, source_target_pairs={{4,0},{5,1},{6,2},{7,3},{20,16},{21,17},{22,18},{23,19}} | collective-permute-start | bytes 3145736 | tf_op jit(solution)/shard_map/ppermute | solution.py:160
  (1 other events, 1.6 us)

commit v4 on v3

--- a/solution.py
+++ b/solution.py
@@ -100,28 +100,32 @@
 
 
 def pick_rows_kernel(order_ref, field_ref, out_ref):
-    blocks = field_ref.shape[0]
+    blocks = out_ref.shape[0]
+    width = out_ref.shape[2]
     group = 8
 
     def body(index, carry):
         start = pl.multiple_of(index * group, group)
-        sources = [order_ref[start + row] for row in range(group)]
+        rows = jnp.concatenate(
+            [field_ref[pl.ds(order_ref[start + row], 1), :] for row in range(group)], axis=0
+        )
         for block in range(blocks):
-            rows = [field_ref[block, pl.ds(source, 1), :] for source in sources]
-            out_ref[block, pl.ds(start, group), :] = jnp.concatenate(rows, axis=0)
+            out_ref[block, pl.ds(start, group), :] = rows[:, block * width:(block + 1) * width]
         return carry
 
-    lax.fori_loop(0, field_ref.shape[1] // group, body, 0, unroll=2)
+    lax.fori_loop(0, out_ref.shape[1] // group, body, 0, unroll=2)
 
 
-def pick_rows(field, order):
+def pick_rows(fields, order):
+    side_by_side = jnp.concatenate(fields, axis=1)
+    shape = (len(fields),) + fields[0].shape
     return pl.pallas_call(
         pick_rows_kernel,
-        out_shape=jax.ShapeDtypeStruct(field.shape, field.dtype),
+        out_shape=jax.ShapeDtypeStruct(shape, fields[0].dtype),
         in_specs=[pl.BlockSpec(memory_space=pltpu.SMEM), pl.BlockSpec(memory_space=pltpu.VMEM)],
         out_specs=pl.BlockSpec(memory_space=pltpu.VMEM),
-        cost_estimate=pl.CostEstimate(flops=0, transcendentals=0, bytes_accessed=2 * field.size * 4),
-    )(order, field)
+        cost_estimate=pl.CostEstimate(flops=0, transcendentals=0, bytes_accessed=2 * side_by_side.size * 4),
+    )(order, side_by_side)
 
 
 def shards(noise, inv_diag, coupling, order):
@@ -159,7 +163,7 @@
         leaving = local if step == 0 else local + apply(across_parts, entering)
         entering = entering + lax.ppermute(leaving, "tm", [(sender, sender - 1)])
     finals = chain(entering, False)
-    return pick_rows(jnp.stack(finals, axis=0), order)
+    return pick_rows(finals, order)
 
 
 def solution(mesh):

time: 304 us -> 304 us (level)
  no operation moved by 1% of the time
where the time goes in v4:
time: 304 us
  waiting for transfers between devices  194 us (64%)
  starting transfers between devices  54.4 us (18%)
  matrix products  26.1 us (9%)
  other arithmetic  18.5 us (6%)
  Pallas kernels  5.31 us (2%)
  local copies, waits for them, and re-layouts  4.42 us (1%)
    ppermute x3, waiting for transfers between devices, line_reduce_scatter(): lax.ppermute(tile(me - count + step) + leftward, axis, left_route)  101 us
    ppermute x3, waiting for transfers between devices, line_all_to_all(): lax.ppermute(own_rows(me - distance), axis, [(k, k - distance) for k in r...  34.1 us
    ppermute x3, waiting for transfers between devices, line_all_to_all(): lax.ppermute(own_rows(me + distance), axis, [(k, k + distance) for k in r...  31.1 us
    dot_general x16, matrix products, bdot(): return jnp.dot(left, right, preferred_element_type=jnp.float32)  26.1 us
    ppermute x3, starting transfers between devices, line_reduce_scatter(): lax.ppermute(tile(me - count + step) + leftward, axis, left_route)  25.1 us
    ppermute x3, waiting for transfers between devices, shards(): entering = entering + lax.ppermute(leaving, 'tm', [(sender, sender - 1)])  24.3 us
    ppermute x3, starting transfers between devices, line_all_to_all(): lax.ppermute(own_rows(me - distance), axis, [(k, k - distance) for k in r...  7.67 us
    add x2, other arithmetic, line_reduce_scatter(): tile(me - count + step) + leftward  7.29 us
  transfers between devices with their start and end apart: 21, of which 11 were waited for; matrix products, arithmetic and copies ran while one was open for 10% of the time, Pallas kernels for 0%

profile of v4, /device:TPU:25, one launch (start us, length us, event | category | flops | bytes accessed | tf_op | source)
XLA Modules:
  0.0 303.5 jit_solution(11244281638735627856)
XLA Ops:
  3.3 4.0 %collective-permute-start.1 = (f32[2,256,256]{2,1,0:T(8,128)S(1)}, f32[2,256,256]{2,1,0:T(8,128)S(1)}, u32[]{:S(2)}, u32[]{:S(2)}) collective-permute-start(f32[2,256,256]{2,1,0:T(8,128)S(1)} %get-tuple-element.38), channel_id=1, source_target_pairs={{1,0},{2,1},{3,2},{5,4},{6,5},{7,6},{9,8},{10,9},{11,10},{13,12},{... | collective-permute-start | bytes 1572872 | tf_op jit(solution)/shard_map/ppermute | solution.py:96
  10.0 4.1 %collective-permute-start.13 = (f32[2,1024,256]{2,1,0:T(8,128)S(1)}, f32[2,1024,256]{2,1,0:T(8,128)S(1)}, u32[]{:S(2)}, u32[]{:S(2)}) collective-permute-start(f32[2,1024,256]{2,1,0:T(8,128)S(1)} %copy-done.2), channel_id=1, source_target_pairs={{1,0},{2,1},{3,2},{5,4},{6,5},{7,6},{9,8},{10,9},{11,10},{13,12},{... | collective-permute-start | bytes 6291464 | tf_op jit(solution)/shard_map/ppermute | solution.py:78
  14.1 2.6 collective-permute-done
  16.7 2.3 collective-permute-start.3
  20.6 18.5 %collective-permute-done.2 = f32[2,256,256]{2,1,0:T(8,128)S(1)} collective-permute-done((f32[2,256,256]{2,1,0:T(8,128)S(1)}, f32[2,256,256]{2,1,0:T(8,128)S(1)}, u32[]{:S(2)}, u32[]{:S(2)}) %collective-permute-start.2) | collective-permute-done | bytes 524320 | tf_op jit(solution)/shard_map/ppermute | solution.py:95
  40.6 33.2 %collective-permute-done.3 = f32[2,256,256]{2,1,0:T(8,128)S(1)} collective-permute-done((f32[2,256,256]{2,1,0:T(8,128)S(1)}, f32[2,256,256]{2,1,0:T(8,128)S(1)}, u32[]{:S(2)}, u32[]{:S(2)}) %collective-permute-start.3) | collective-permute-done | bytes 524320 | tf_op jit(solution)/shard_map/ppermute | solution.py:96
  73.9 10.0 %collective-permute-done.4 = f32[2,256,256]{2,1,0:T(8,128)S(1)} collective-permute-done((f32[2,256,256]{2,1,0:T(8,128)S(1)}, f32[2,256,256]{2,1,0:T(8,128)S(1)}, u32[]{:S(2)}, u32[]{:S(2)}) %collective-permute-start.4) | collective-permute-done | bytes 524320 | tf_op jit(solution)/shard_map/ppermute | solution.py:95
  92.1 13.7 %collective-permute-start.9 = (f32[2,1024,256]{2,1,0:T(8,128)S(1)}, f32[2,1024,256]{2,1,0:T(8,128)S(1)}, u32[]{:S(2)}, u32[]{:S(2)}) collective-permute-start(f32[2,1024,256]{2,1,0:T(8,128)S(1)} %get-tuple-element.23), channel_id=1, source_target_pairs={{3,2},{7,6},{11,10},{15,14},{19,18},{23,22},{27,26},{31,30}} | collective-permute-start | bytes 6291464 | tf_op jit(solution)/shard_map/ppermute | solution.py:55
  107.9 40.8 %collective-permute-done.9 = f32[2,1024,256]{2,1,0:T(8,128)S(1)} collective-permute-done((f32[2,1024,256]{2,1,0:T(8,128)S(1)}, f32[2,1024,256]{2,1,0:T(8,128)S(1)}, u32[]{:S(2)}, u32[]{:S(2)}) %collective-permute-start.9) | collective-permute-done | bytes 2097184 | tf_op jit(solution)/shard_map/ppermute | solution.py:55
  148.7 2.8 fusion.34
  151.5 4.3 %collective-permute-start.10 = (f32[2,1024,256]{2,1,0:T(8,128)}, f32[2,1024,256]{2,1,0:T(8,128)S(1)}, u32[]{:S(2)}, u32[]{:S(2)}) collective-permute-start(f32[2,1024,256]{2,1,0:T(8,128)} %get-tuple-element.21), channel_id=1, source_target_pairs={{2,1},{3,2},{6,5},{7,6},{10,9},{11,10},{14,13},{15,14},{18,17},{19... | collective-permute-start | bytes 6291464 | tf_op jit(solution)/shard_map/ppermute | solution.py:55
  155.8 2.1 collective-permute-start.7
  164.1 34.0 %collective-permute-done.10 = f32[2,1024,256]{2,1,0:T(8,128)S(1)} collective-permute-done((f32[2,1024,256]{2,1,0:T(8,128)}, f32[2,1024,256]{2,1,0:T(8,128)S(1)}, u32[]{:S(2)}, u32[]{:S(2)}) %collective-permute-start.10) | collective-permute-done | bytes 2097184 | tf_op jit(solution)/shard_map/ppermute | solution.py:55
  198.1 4.5 %fusion.32 = (f32[2,1024,256]{2,1,0:T(8,128)}, f32[2,1024,256]{2,1,0:T(8,128)}) fusion(f32[2,1024,256]{2,1,0:T(8,128)S(1)} %collective-permute-done.10, s32[]{:T(128)S(6)} %select_n.15, f32[1,1024,1024]{2,1,0:T(8,128)S(1)} %fusion.12, f32[1,1024,1024]{2,1,0:T(8,128)S(1)} %fusion.10, f32[2,1024,256]{2,1,0:T(8,128)} %collective-permute-done.7, s32[]{:T(128)S(6)} %select_n.16), kind=kLoop, calls=%fused_computation.57 | loop fusion | flops 2097152 | bytes 16777224 | tf_op jit(solution)/shard_map/add | solution.py:55
  202.6 7.1 %collective-permute-start.11 = (f32[2,1024,256]{2,1,0:T(8,128)}, f32[2,1024,256]{2,1,0:T(8,128)S(1)}, u32[]{:S(2)}, u32[]{:S(2)}) collective-permute-start(f32[2,1024,256]{2,1,0:T(8,128)} %get-tuple-element.19), channel_id=1, source_target_pairs={{1,0},{2,1},{3,2},{5,4},{6,5},{7,6},{9,8},{10,9},{11,10},{13,12},{... | collective-permute-start | bytes 6291464 | tf_op jit(solution)/shard_map/ppermute | solution.py:55
  213.3 7.0 %fusion.13 = f32[1024,2048]{1,0:T(8,128)} fusion(bf16[1024,1024]{1,0:T(8,128)(2,1)S(1)} %get-tuple-element.18, bf16[1024,1024]{1,0:T(8,128)(2,1)S(1)} %get-tuple-element.17, f32[2,1024,1024]{2,1,0:T(8,128)S(1)} %add_dynamic-update-slice_fusion), kind=kOutput, calls=%fused_computation.39 | convolution fusion | flops 4305453056 | bytes 16777216 | tf_op jit(solution)/shard_map/dot_general | solution.py:29
  220.2 5.0 %fusion.5 = (bf16[1024,1024]{1,0:T(8,128)(2,1)S(1)}, bf16[1024,1024]{1,0:T(8,128)(2,1)S(1)}) fusion(f32[2,1024,1024]{2,1,0:T(8,128)S(1)} %add_dynamic-update-slice_fusion, f32[1024,2048]{1,0:T(8,128)} %fusion.13), kind=kOutput, calls=%fused_computation.28 | convolution fusion | flops 2161115136 | bytes 20971520 | tf_op jit(solution)/shard_map/dot_general | solution.py:29
  225.2 25.9 %collective-permute-done.11 = f32[2,1024,256]{2,1,0:T(8,128)S(1)} collective-permute-done((f32[2,1024,256]{2,1,0:T(8,128)}, f32[2,1024,256]{2,1,0:T(8,128)S(1)}, u32[]{:S(2)}, u32[]{:S(2)}) %collective-permute-start.11) | collective-permute-done | bytes 2097184 | tf_op jit(solution)/shard_map/ppermute | solution.py:55
  251.1 4.0 %collective-permute-done.8 = f32[2,1024,256]{2,1,0:T(8,128)} collective-permute-done((f32[2,1024,256]{2,1,0:T(8,128)}, f32[2,1024,256]{2,1,0:T(8,128)}, u32[]{:S(2)}, u32[]{:S(2)}) %collective-permute-start.8) | collective-permute-done | bytes 2097184 | tf_op jit(solution)/shard_map/ppermute | solution.py:54
  255.1 2.4 fusion.25
  264.2 22.1 %collective-permute-done.19 = f32[1024,256]{1,0:T(8,128)S(1)} collective-permute-done((f32[1024,256]{1,0:T(8,128)S(1)}, f32[1024,256]{1,0:T(8,128)S(1)}, u32[]{:S(2)}, u32[]{:S(2)}) %collective-permute-start.19) | collective-permute-done | bytes 1048608 | tf_op jit(solution)/shard_map/ppermute | solution.py:164
  290.0 2.2 collective-permute-done.20
  296.5 1.7 pad_maximum_fusion.field_ref
  298.2 5.3 %shard_map.46 = f32[2,1024,256]{2,1,0:T(8,128)} custom-call(s32[1024]{0:T(1024)} %order_ref.1, f32[1024,512]{1,0:T(8,128)} %pad_maximum_fusion.field_ref), custom_call_target="tpu_custom_call" | custom-call | bytes 4194304 | tf_op jit(solution)/shard_map/pallas_call | solution.py:122
  (72 shorter events, 43.3 us)
Async XLA Ops:
  1.6 7.1 %copy-start.2 = (f32[2,1024,256]{2,1,0:T(8,128)S(1)}, f32[2,1024,256]{2,1,0:T(8,128)}, u32[]{:S(2)}) copy-start(f32[2,1024,256]{2,1,0:T(8,128)} %param.6) | copy-start | bytes 6291460
  1.9 14.8 %collective-permute-start = (f32[2,256,256]{2,1,0:T(8,128)S(1)}, f32[2,256,256]{2,1,0:T(8,128)S(1)}, u32[]{:S(2)}, u32[]{:S(2)}) collective-permute-start(f32[2,256,256]{2,1,0:T(8,128)S(1)} %get-tuple-element.39), channel_id=1, source_target_pairs={{0,1},{1,2},{2,3},{4,5},{5,6},{6,7},{8,9},{9,10},{10,11},{12,13},{... | collective-permute-start | bytes 1572872 | tf_op jit(solution)/shard_map/ppermute | solution.py:95
  3.3 15.9 %collective-permute-start.1 = (f32[2,256,256]{2,1,0:T(8,128)S(1)}, f32[2,256,256]{2,1,0:T(8,128)S(1)}, u32[]{:S(2)}, u32[]{:S(2)}) collective-permute-start(f32[2,256,256]{2,1,0:T(8,128)S(1)} %get-tuple-element.38), channel_id=1, source_target_pairs={{1,0},{2,1},{3,2},{5,4},{6,5},{7,6},{9,8},{10,9},{11,10},{13,12},{... | collective-permute-start | bytes 1572872 | tf_op jit(solution)/shard_map/ppermute | solution.py:96
  7.4 31.8 %collective-permute-start.2 = (f32[2,256,256]{2,1,0:T(8,128)S(1)}, f32[2,256,256]{2,1,0:T(8,128)S(1)}, u32[]{:S(2)}, u32[]{:S(2)}) collective-permute-start(f32[2,256,256]{2,1,0:T(8,128)S(1)} %get-tuple-element.37), channel_id=1, source_target_pairs={{0,2},{1,3},{4,6},{5,7},{8,10},{9,11},{12,14},{13,15},{16,18},{17,... | collective-permute-start | bytes 1572872 | tf_op jit(solution)/shard_map/ppermute | solution.py:95
  8.7 97.1 %collective-permute-start.12 = (f32[2,1024,256]{2,1,0:T(8,128)S(1)}, f32[2,1024,256]{2,1,0:T(8,128)S(1)}, u32[]{:S(2)}, u32[]{:S(2)}) collective-permute-start(f32[2,1024,256]{2,1,0:T(8,128)S(1)} %copy-done.2), channel_id=1, source_target_pairs={{0,1},{1,2},{2,3},{4,5},{5,6},{6,7},{8,9},{9,10},{10,11},{12,13},{... | collective-permute-start | bytes 6291464 | tf_op jit(solution)/shard_map/ppermute | solution.py:77
  10.0 97.1 %collective-permute-start.13 = (f32[2,1024,256]{2,1,0:T(8,128)S(1)}, f32[2,1024,256]{2,1,0:T(8,128)S(1)}, u32[]{:S(2)}, u32[]{:S(2)}) collective-permute-start(f32[2,1024,256]{2,1,0:T(8,128)S(1)} %copy-done.2), channel_id=1, source_target_pairs={{1,0},{2,1},{3,2},{5,4},{6,5},{7,6},{9,8},{10,9},{11,10},{13,12},{... | collective-permute-start | bytes 6291464 | tf_op jit(solution)/shard_map/ppermute | solution.py:78
  16.7 57.1 %collective-permute-start.3 = (f32[2,256,256]{2,1,0:T(8,128)S(1)}, f32[2,256,256]{2,1,0:T(8,128)S(1)}, u32[]{:S(2)}, u32[]{:S(2)}) collective-permute-start(f32[2,256,256]{2,1,0:T(8,128)S(1)} %get-tuple-element.36), channel_id=1, source_target_pairs={{2,0},{3,1},{6,4},{7,5},{10,8},{11,9},{14,12},{15,13},{18,16},{19,... | collective-permute-start | bytes 1572872 | tf_op jit(solution)/shard_map/ppermute | solution.py:96
  19.2 64.8 %collective-permute-start.4 = (f32[2,256,256]{2,1,0:T(8,128)S(1)}, f32[2,256,256]{2,1,0:T(8,128)S(1)}, u32[]{:S(2)}, u32[]{:S(2)}) collective-permute-start(f32[2,256,256]{2,1,0:T(8,128)S(1)} %get-tuple-element.41), channel_id=1, source_target_pairs={{0,3},{4,7},{8,11},{12,15},{16,19},{20,23},{24,27},{28,31}} | collective-permute-start | bytes 1572872 | tf_op jit(solution)/shard_map/ppermute | solution.py:95
  39.1 45.9 %collective-permute-start.5 = (f32[2,256,256]{2,1,0:T(8,128)S(1)}, f32[2,256,256]{2,1,0:T(8,128)S(1)}, u32[]{:S(2)}, u32[]{:S(2)}) collective-permute-start(f32[2,256,256]{2,1,0:T(8,128)S(1)} %get-tuple-element.35), channel_id=1, source_target_pairs={{3,0},{7,4},{11,8},{15,12},{19,16},{23,20},{27,24},{31,28}} | collective-permute-start | bytes 1572872 | tf_op jit(solution)/shard_map/ppermute | solution.py:96
  85.2 1.6 copy-start
  91.3 16.6 %collective-permute-start.6 = (f32[2,1024,256]{2,1,0:T(8,128)S(1)}, f32[2,1024,256]{2,1,0:T(8,128)S(1)}, u32[]{:S(2)}, u32[]{:S(2)}) collective-permute-start(f32[2,1024,256]{2,1,0:T(8,128)S(1)} %get-tuple-element.24), channel_id=1, source_target_pairs={{0,1},{4,5},{8,9},{12,13},{16,17},{20,21},{24,25},{28,29}} | collective-permute-start | bytes 6291464 | tf_op jit(solution)/shard_map/ppermute | solution.py:54
  92.1 56.6 %collective-permute-start.9 = (f32[2,1024,256]{2,1,0:T(8,128)S(1)}, f32[2,1024,256]{2,1,0:T(8,128)S(1)}, u32[]{:S(2)}, u32[]{:S(2)}) collective-permute-start(f32[2,1024,256]{2,1,0:T(8,128)S(1)} %get-tuple-element.23), channel_id=1, source_target_pairs={{3,2},{7,6},{11,10},{15,14},{19,18},{23,22},{27,26},{31,30}} | collective-permute-start | bytes 6291464 | tf_op jit(solution)/shard_map/ppermute | solution.py:55
  105.8 52.2 %collective-permute-start.14 = (f32[2,1024,256]{2,1,0:T(8,128)S(1)}, f32[2,1024,256]{2,1,0:T(8,128)S(1)}, u32[]{:S(2)}, u32[]{:S(2)}) collective-permute-start(f32[2,1024,256]{2,1,0:T(8,128)S(1)} %collective-permute-done.12), channel_id=1, source_target_pairs={{1,2},{2,3},{5,6},{6,7},{9,10},{10,11},{13,14},{14,15},{17,18},{18... | collective-permute-start | bytes 6291464 | tf_op jit(solution)/shard_map/ppermute | solution.py:77
  107.1 52.2 %collective-permute-start.15 = (f32[2,1024,256]{2,1,0:T(8,128)S(1)}, f32[2,1024,256]{2,1,0:T(8,128)S(1)}, u32[]{:S(2)}, u32[]{:S(2)}) collective-permute-start(f32[2,1024,256]{2,1,0:T(8,128)S(1)} %collective-permute-done.13), channel_id=1, source_target_pairs={{1,0},{2,1},{5,4},{6,5},{9,8},{10,9},{13,12},{14,13},{17,16},{18,1... | collective-permute-start | bytes 6291464 | tf_op jit(solution)/shard_map/ppermute | solution.py:78
  151.5 46.6 %collective-permute-start.10 = (f32[2,1024,256]{2,1,0:T(8,128)}, f32[2,1024,256]{2,1,0:T(8,128)S(1)}, u32[]{:S(2)}, u32[]{:S(2)}) collective-permute-start(f32[2,1024,256]{2,1,0:T(8,128)} %get-tuple-element.21), channel_id=1, source_target_pairs={{2,1},{3,2},{6,5},{7,6},{10,9},{11,10},{14,13},{15,14},{18,17},{19... | collective-permute-start | bytes 6291464 | tf_op jit(solution)/shard_map/ppermute | solution.py:55
  155.8 5.5 %copy-start.3 = (f32[2,1024,256]{2,1,0:T(8,128)S(1)}, f32[2,1024,256]{2,1,0:T(8,128)}, u32[]{:S(2)}) copy-start(f32[2,1024,256]{2,1,0:T(8,128)} %param.6) | copy-start | bytes 6291460
  155.8 42.3 %collective-permute-start.7 = (f32[2,1024,256]{2,1,0:T(8,128)}, f32[2,1024,256]{2,1,0:T(8,128)}, u32[]{:S(2)}, u32[]{:S(2)}) collective-permute-start(f32[2,1024,256]{2,1,0:T(8,128)} %get-tuple-element.22), channel_id=1, source_target_pairs={{0,1},{1,2},{4,5},{5,6},{8,9},{9,10},{12,13},{13,14},{16,17},{17,1... | collective-permute-start | bytes 6291464 | tf_op jit(solution)/shard_map/ppermute | solution.py:54
  158.0 53.1 %collective-permute-start.16 = (f32[2,1024,256]{2,1,0:T(8,128)S(1)}, f32[2,1024,256]{2,1,0:T(8,128)S(1)}, u32[]{:S(2)}, u32[]{:S(2)}) collective-permute-start(f32[2,1024,256]{2,1,0:T(8,128)S(1)} %collective-permute-done.14), channel_id=1, source_target_pairs={{2,3},{6,7},{10,11},{14,15},{18,19},{22,23},{26,27},{30,31}} | collective-permute-start | bytes 6291464 | tf_op jit(solution)/shard_map/ppermute | solution.py:77
  159.3 52.3 %collective-permute-start.17 = (f32[2,1024,256]{2,1,0:T(8,128)S(1)}, f32[2,1024,256]{2,1,0:T(8,128)S(1)}, u32[]{:S(2)}, u32[]{:S(2)}) collective-permute-start(f32[2,1024,256]{2,1,0:T(8,128)S(1)} %collective-permute-done.15), channel_id=1, source_target_pairs={{1,0},{5,4},{9,8},{13,12},{17,16},{21,20},{25,24},{29,28}} | collective-permute-start | bytes 6291464 | tf_op jit(solution)/shard_map/ppermute | solution.py:78
  202.6 48.5 %collective-permute-start.11 = (f32[2,1024,256]{2,1,0:T(8,128)}, f32[2,1024,256]{2,1,0:T(8,128)S(1)}, u32[]{:S(2)}, u32[]{:S(2)}) collective-permute-start(f32[2,1024,256]{2,1,0:T(8,128)} %get-tuple-element.19), channel_id=1, source_target_pairs={{1,0},{2,1},{3,2},{5,4},{6,5},{7,6},{9,8},{10,9},{11,10},{13,12},{... | collective-permute-start | bytes 6291464 | tf_op jit(solution)/shard_map/ppermute | solution.py:55
  209.7 45.3 %collective-permute-start.8 = (f32[2,1024,256]{2,1,0:T(8,128)}, f32[2,1024,256]{2,1,0:T(8,128)}, u32[]{:S(2)}, u32[]{:S(2)}) collective-permute-start(f32[2,1024,256]{2,1,0:T(8,128)} %get-tuple-element.20), channel_id=1, source_target_pairs={{0,1},{1,2},{2,3},{4,5},{5,6},{6,7},{8,9},{9,10},{10,11},{12,13},{... | collective-permute-start | bytes 6291464 | tf_op jit(solution)/shard_map/ppermute | solution.py:54
  259.7 1.0 collective-permute-start.18
  262.9 23.4 %collective-permute-start.19 = (f32[1024,256]{1,0:T(8,128)S(1)}, f32[1024,256]{1,0:T(8,128)S(1)}, u32[]{:S(2)}, u32[]{:S(2)}) collective-permute-start(f32[1024,256]{1,0:T(8,128)S(1)} %fusion.62), channel_id=1, source_target_pairs={{8,4},{9,5},{10,6},{11,7},{24,20},{25,21},{26,22},{27,23}} | collective-permute-start | bytes 3145736 | tf_op jit(solution)/shard_map/ppermute | solution.py:164
  288.7 3.6 %collective-permute-start.20 = (f32[1024,256]{1,0:T(8,128)S(1)}, f32[1024,256]{1,0:T(8,128)S(1)}, u32[]{:S(2)}, u32[]{:S(2)}) collective-permute-start(f32[1024,256]{1,0:T(8,128)S(1)} %fusion.60), channel_id=1, source_target_pairs={{4,0},{5,1},{6,2},{7,3},{20,16},{21,17},{22,18},{23,19}} | collective-permute-start | bytes 3145736 | tf_op jit(solution)/shard_map/ppermute | solution.py:164
  (1 other events, 1.6 us)

commit v5 on v3

--- a/solution.py
+++ b/solution.py
@@ -111,7 +111,7 @@
             out_ref[block, pl.ds(start, group), :] = jnp.concatenate(rows, axis=0)
         return carry
 
-    lax.fori_loop(0, field_ref.shape[1] // group, body, 0, unroll=2)
+    lax.fori_loop(0, field_ref.shape[1] // group, body, 0, unroll=8)
 
 
 def pick_rows(field, order):

time: 304 us -> 304 us (level)
  no operation moved by 1% of the time
where the time goes in v5:
time: 304 us; the launch traced here: 303 us
  waiting for transfers between devices  194 us (64%)
  starting transfers between devices  54.4 us (18%)
  matrix products  26.1 us (9%)
  other arithmetic  18.3 us (6%)
  Pallas kernels  5 us (2%)
  local copies, waits for them, and re-layouts  4.42 us (1%)
    ppermute x3, waiting for transfers between devices, line_reduce_scatter(): lax.ppermute(tile(me - count + step) + leftward, axis, left_route)  101 us
    ppermute x3, waiting for transfers between devices, line_all_to_all(): lax.ppermute(own_rows(me - distance), axis, [(k, k - distance) for k in r...  34.1 us
    ppermute x3, waiting for transfers between devices, line_all_to_all(): lax.ppermute(own_rows(me + distance), axis, [(k, k + distance) for k in r...  31.1 us
    dot_general x16, matrix products, bdot(): return jnp.dot(left, right, preferred_element_type=jnp.float32)  26.1 us
    ppermute x3, starting transfers between devices, line_reduce_scatter(): lax.ppermute(tile(me - count + step) + leftward, axis, left_route)  25.1 us
    ppermute x3, waiting for transfers between devices, shards(): entering = entering + lax.ppermute(leaving, 'tm', [(sender, sender - 1)])  24.3 us
    ppermute x3, starting transfers between devices, line_all_to_all(): lax.ppermute(own_rows(me - distance), axis, [(k, k - distance) for k in r...  7.67 us
    add x2, other arithmetic, line_reduce_scatter(): tile(me - count + step) + leftward  7.29 us
  transfers between devices with their start and end apart: 21, of which 11 were waited for; matrix products, arithmetic and copies ran while one was open for 10% of the time, Pallas kernels for 0%

profile of v5, /device:TPU:25, one launch (start us, length us, event | category | flops | bytes accessed | tf_op | source)
XLA Modules:
  0.0 303.0 jit_solution(13381623281410985799)
XLA Ops:
  3.3 4.0 %collective-permute-start.1 = (f32[2,256,256]{2,1,0:T(8,128)S(1)}, f32[2,256,256]{2,1,0:T(8,128)S(1)}, u32[]{:S(2)}, u32[]{:S(2)}) collective-permute-start(f32[2,256,256]{2,1,0:T(8,128)S(1)} %get-tuple-element.38), channel_id=1, source_target_pairs={{1,0},{2,1},{3,2},{5,4},{6,5},{7,6},{9,8},{10,9},{11,10},{13,12},{... | collective-permute-start | bytes 1572872 | tf_op jit(solution)/shard_map/ppermute | solution.py:96
  10.0 4.1 %collective-permute-start.13 = (f32[2,1024,256]{2,1,0:T(8,128)S(1)}, f32[2,1024,256]{2,1,0:T(8,128)S(1)}, u32[]{:S(2)}, u32[]{:S(2)}) collective-permute-start(f32[2,1024,256]{2,1,0:T(8,128)S(1)} %copy-done.2), channel_id=1, source_target_pairs={{1,0},{2,1},{3,2},{5,4},{6,5},{7,6},{9,8},{10,9},{11,10},{13,12},{... | collective-permute-start | bytes 6291464 | tf_op jit(solution)/shard_map/ppermute | solution.py:78
  14.1 2.6 collective-permute-done
  16.7 2.3 collective-permute-start.3
  20.6 18.5 %collective-permute-done.2 = f32[2,256,256]{2,1,0:T(8,128)S(1)} collective-permute-done((f32[2,256,256]{2,1,0:T(8,128)S(1)}, f32[2,256,256]{2,1,0:T(8,128)S(1)}, u32[]{:S(2)}, u32[]{:S(2)}) %collective-permute-start.2) | collective-permute-done | bytes 524320 | tf_op jit(solution)/shard_map/ppermute | solution.py:95
  40.6 33.2 %collective-permute-done.3 = f32[2,256,256]{2,1,0:T(8,128)S(1)} collective-permute-done((f32[2,256,256]{2,1,0:T(8,128)S(1)}, f32[2,256,256]{2,1,0:T(8,128)S(1)}, u32[]{:S(2)}, u32[]{:S(2)}) %collective-permute-start.3) | collective-permute-done | bytes 524320 | tf_op jit(solution)/shard_map/ppermute | solution.py:96
  73.9 10.0 %collective-permute-done.4 = f32[2,256,256]{2,1,0:T(8,128)S(1)} collective-permute-done((f32[2,256,256]{2,1,0:T(8,128)S(1)}, f32[2,256,256]{2,1,0:T(8,128)S(1)}, u32[]{:S(2)}, u32[]{:S(2)}) %collective-permute-start.4) | collective-permute-done | bytes 524320 | tf_op jit(solution)/shard_map/ppermute | solution.py:95
  92.1 13.7 %collective-permute-start.9 = (f32[2,1024,256]{2,1,0:T(8,128)S(1)}, f32[2,1024,256]{2,1,0:T(8,128)S(1)}, u32[]{:S(2)}, u32[]{:S(2)}) collective-permute-start(f32[2,1024,256]{2,1,0:T(8,128)S(1)} %get-tuple-element.23), channel_id=1, source_target_pairs={{3,2},{7,6},{11,10},{15,14},{19,18},{23,22},{27,26},{31,30}} | collective-permute-start | bytes 6291464 | tf_op jit(solution)/shard_map/ppermute | solution.py:55
  107.9 40.8 %collective-permute-done.9 = f32[2,1024,256]{2,1,0:T(8,128)S(1)} collective-permute-done((f32[2,1024,256]{2,1,0:T(8,128)S(1)}, f32[2,1024,256]{2,1,0:T(8,128)S(1)}, u32[]{:S(2)}, u32[]{:S(2)}) %collective-permute-start.9) | collective-permute-done | bytes 2097184 | tf_op jit(solution)/shard_map/ppermute | solution.py:55
  148.7 2.8 fusion.34
  151.5 4.3 %collective-permute-start.10 = (f32[2,1024,256]{2,1,0:T(8,128)}, f32[2,1024,256]{2,1,0:T(8,128)S(1)}, u32[]{:S(2)}, u32[]{:S(2)}) collective-permute-start(f32[2,1024,256]{2,1,0:T(8,128)} %get-tuple-element.21), channel_id=1, source_target_pairs={{2,1},{3,2},{6,5},{7,6},{10,9},{11,10},{14,13},{15,14},{18,17},{19... | collective-permute-start | bytes 6291464 | tf_op jit(solution)/shard_map/ppermute | solution.py:55
  155.8 2.1 collective-permute-start.7
  164.1 34.0 %collective-permute-done.10 = f32[2,1024,256]{2,1,0:T(8,128)S(1)} collective-permute-done((f32[2,1024,256]{2,1,0:T(8,128)}, f32[2,1024,256]{2,1,0:T(8,128)S(1)}, u32[]{:S(2)}, u32[]{:S(2)}) %collective-permute-start.10) | collective-permute-done | bytes 2097184 | tf_op jit(solution)/shard_map/ppermute | solution.py:55
  198.1 4.5 %fusion.32 = (f32[2,1024,256]{2,1,0:T(8,128)}, f32[2,1024,256]{2,1,0:T(8,128)}) fusion(f32[2,1024,256]{2,1,0:T(8,128)S(1)} %collective-permute-done.10, s32[]{:T(128)S(6)} %select_n.15, f32[1,1024,1024]{2,1,0:T(8,128)S(1)} %fusion.12, f32[1,1024,1024]{2,1,0:T(8,128)S(1)} %fusion.10, f32[2,1024,256]{2,1,0:T(8,128)} %collective-permute-done.7, s32[]{:T(128)S(6)} %select_n.16), kind=kLoop, calls=%fused_computation.57 | loop fusion | flops 2097152 | bytes 16777224 | tf_op jit(solution)/shard_map/add | solution.py:55
  202.6 7.1 %collective-permute-start.11 = (f32[2,1024,256]{2,1,0:T(8,128)}, f32[2,1024,256]{2,1,0:T(8,128)S(1)}, u32[]{:S(2)}, u32[]{:S(2)}) collective-permute-start(f32[2,1024,256]{2,1,0:T(8,128)} %get-tuple-element.19), channel_id=1, source_target_pairs={{1,0},{2,1},{3,2},{5,4},{6,5},{7,6},{9,8},{10,9},{11,10},{13,12},{... | collective-permute-start | bytes 6291464 | tf_op jit(solution)/shard_map/ppermute | solution.py:55
  213.3 7.0 %fusion.13 = f32[1024,2048]{1,0:T(8,128)} fusion(bf16[1024,1024]{1,0:T(8,128)(2,1)S(1)} %get-tuple-element.18, bf16[1024,1024]{1,0:T(8,128)(2,1)S(1)} %get-tuple-element.17, f32[2,1024,1024]{2,1,0:T(8,128)S(1)} %add_dynamic-update-slice_fusion), kind=kOutput, calls=%fused_computation.39 | convolution fusion | flops 4305453056 | bytes 16777216 | tf_op jit(solution)/shard_map/dot_general | solution.py:29
  220.2 5.0 %fusion.5 = (bf16[1024,1024]{1,0:T(8,128)(2,1)S(1)}, bf16[1024,1024]{1,0:T(8,128)(2,1)S(1)}) fusion(f32[2,1024,1024]{2,1,0:T(8,128)S(1)} %add_dynamic-update-slice_fusion, f32[1024,2048]{1,0:T(8,128)} %fusion.13), kind=kOutput, calls=%fused_computation.28 | convolution fusion | flops 2161115136 | bytes 20971520 | tf_op jit(solution)/shard_map/dot_general | solution.py:29
  225.2 25.9 %collective-permute-done.11 = f32[2,1024,256]{2,1,0:T(8,128)S(1)} collective-permute-done((f32[2,1024,256]{2,1,0:T(8,128)}, f32[2,1024,256]{2,1,0:T(8,128)S(1)}, u32[]{:S(2)}, u32[]{:S(2)}) %collective-permute-start.11) | collective-permute-done | bytes 2097184 | tf_op jit(solution)/shard_map/ppermute | solution.py:55
  251.1 4.0 %collective-permute-done.8 = f32[2,1024,256]{2,1,0:T(8,128)} collective-permute-done((f32[2,1024,256]{2,1,0:T(8,128)}, f32[2,1024,256]{2,1,0:T(8,128)}, u32[]{:S(2)}, u32[]{:S(2)}) %collective-permute-start.8) | collective-permute-done | bytes 2097184 | tf_op jit(solution)/shard_map/ppermute | solution.py:54
  255.1 2.4 fusion.25
  264.2 22.1 %collective-permute-done.19 = f32[1024,256]{1,0:T(8,128)S(1)} collective-permute-done((f32[1024,256]{1,0:T(8,128)S(1)}, f32[1024,256]{1,0:T(8,128)S(1)}, u32[]{:S(2)}, u32[]{:S(2)}) %collective-permute-start.19) | collective-permute-done | bytes 1048608 | tf_op jit(solution)/shard_map/ppermute | solution.py:160
  290.0 2.2 collective-permute-done.20
  296.5 1.5 pad_maximum_fusion.field_ref
  298.0 5.0 %shard_map.46 = f32[2,1024,256]{2,1,0:T(8,128)} custom-call(s32[1024]{0:T(1024)} %order_ref.1, f32[2,1024,256]{2,1,0:T(8,128)} %pad_maximum_fusion.field_ref), custom_call_target="tpu_custom_call" | custom-call | bytes 4194304 | tf_op jit(solution)/shard_map/pallas_call | solution.py:118
  (72 shorter events, 43.3 us)
Async XLA Ops:
  1.6 7.1 %copy-start.2 = (f32[2,1024,256]{2,1,0:T(8,128)S(1)}, f32[2,1024,256]{2,1,0:T(8,128)}, u32[]{:S(2)}) copy-start(f32[2,1024,256]{2,1,0:T(8,128)} %param.6) | copy-start | bytes 6291460
  1.9 14.8 %collective-permute-start = (f32[2,256,256]{2,1,0:T(8,128)S(1)}, f32[2,256,256]{2,1,0:T(8,128)S(1)}, u32[]{:S(2)}, u32[]{:S(2)}) collective-permute-start(f32[2,256,256]{2,1,0:T(8,128)S(1)} %get-tuple-element.39), channel_id=1, source_target_pairs={{0,1},{1,2},{2,3},{4,5},{5,6},{6,7},{8,9},{9,10},{10,11},{12,13},{... | collective-permute-start | bytes 1572872 | tf_op jit(solution)/shard_map/ppermute | solution.py:95
  3.3 15.9 %collective-permute-start.1 = (f32[2,256,256]{2,1,0:T(8,128)S(1)}, f32[2,256,256]{2,1,0:T(8,128)S(1)}, u32[]{:S(2)}, u32[]{:S(2)}) collective-permute-start(f32[2,256,256]{2,1,0:T(8,128)S(1)} %get-tuple-element.38), channel_id=1, source_target_pairs={{1,0},{2,1},{3,2},{5,4},{6,5},{7,6},{9,8},{10,9},{11,10},{13,12},{... | collective-permute-start | bytes 1572872 | tf_op jit(solution)/shard_map/ppermute | solution.py:96
  7.4 31.8 %collective-permute-start.2 = (f32[2,256,256]{2,1,0:T(8,128)S(1)}, f32[2,256,256]{2,1,0:T(8,128)S(1)}, u32[]{:S(2)}, u32[]{:S(2)}) collective-permute-start(f32[2,256,256]{2,1,0:T(8,128)S(1)} %get-tuple-element.37), channel_id=1, source_target_pairs={{0,2},{1,3},{4,6},{5,7},{8,10},{9,11},{12,14},{13,15},{16,18},{17,... | collective-permute-start | bytes 1572872 | tf_op jit(solution)/shard_map/ppermute | solution.py:95
  8.7 97.1 %collective-permute-start.12 = (f32[2,1024,256]{2,1,0:T(8,128)S(1)}, f32[2,1024,256]{2,1,0:T(8,128)S(1)}, u32[]{:S(2)}, u32[]{:S(2)}) collective-permute-start(f32[2,1024,256]{2,1,0:T(8,128)S(1)} %copy-done.2), channel_id=1, source_target_pairs={{0,1},{1,2},{2,3},{4,5},{5,6},{6,7},{8,9},{9,10},{10,11},{12,13},{... | collective-permute-start | bytes 6291464 | tf_op jit(solution)/shard_map/ppermute | solution.py:77
  10.0 97.1 %collective-permute-start.13 = (f32[2,1024,256]{2,1,0:T(8,128)S(1)}, f32[2,1024,256]{2,1,0:T(8,128)S(1)}, u32[]{:S(2)}, u32[]{:S(2)}) collective-permute-start(f32[2,1024,256]{2,1,0:T(8,128)S(1)} %copy-done.2), channel_id=1, source_target_pairs={{1,0},{2,1},{3,2},{5,4},{6,5},{7,6},{9,8},{10,9},{11,10},{13,12},{... | collective-permute-start | bytes 6291464 | tf_op jit(solution)/shard_map/ppermute | solution.py:78
  16.7 57.1 %collective-permute-start.3 = (f32[2,256,256]{2,1,0:T(8,128)S(1)}, f32[2,256,256]{2,1,0:T(8,128)S(1)}, u32[]{:S(2)}, u32[]{:S(2)}) collective-permute-start(f32[2,256,256]{2,1,0:T(8,128)S(1)} %get-tuple-element.36), channel_id=1, source_target_pairs={{2,0},{3,1},{6,4},{7,5},{10,8},{11,9},{14,12},{15,13},{18,16},{19,... | collective-permute-start | bytes 1572872 | tf_op jit(solution)/shard_map/ppermute | solution.py:96
  19.2 64.8 %collective-permute-start.4 = (f32[2,256,256]{2,1,0:T(8,128)S(1)}, f32[2,256,256]{2,1,0:T(8,128)S(1)}, u32[]{:S(2)}, u32[]{:S(2)}) collective-permute-start(f32[2,256,256]{2,1,0:T(8,128)S(1)} %get-tuple-element.41), channel_id=1, source_target_pairs={{0,3},{4,7},{8,11},{12,15},{16,19},{20,23},{24,27},{28,31}} | collective-permute-start | bytes 1572872 | tf_op jit(solution)/shard_map/ppermute | solution.py:95
  39.1 45.9 %collective-permute-start.5 = (f32[2,256,256]{2,1,0:T(8,128)S(1)}, f32[2,256,256]{2,1,0:T(8,128)S(1)}, u32[]{:S(2)}, u32[]{:S(2)}) collective-permute-start(f32[2,256,256]{2,1,0:T(8,128)S(1)} %get-tuple-element.35), channel_id=1, source_target_pairs={{3,0},{7,4},{11,8},{15,12},{19,16},{23,20},{27,24},{31,28}} | collective-permute-start | bytes 1572872 | tf_op jit(solution)/shard_map/ppermute | solution.py:96
  85.2 1.6 copy-start
  91.3 16.6 %collective-permute-start.6 = (f32[2,1024,256]{2,1,0:T(8,128)S(1)}, f32[2,1024,256]{2,1,0:T(8,128)S(1)}, u32[]{:S(2)}, u32[]{:S(2)}) collective-permute-start(f32[2,1024,256]{2,1,0:T(8,128)S(1)} %get-tuple-element.24), channel_id=1, source_target_pairs={{0,1},{4,5},{8,9},{12,13},{16,17},{20,21},{24,25},{28,29}} | collective-permute-start | bytes 6291464 | tf_op jit(solution)/shard_map/ppermute | solution.py:54
  92.1 56.6 %collective-permute-start.9 = (f32[2,1024,256]{2,1,0:T(8,128)S(1)}, f32[2,1024,256]{2,1,0:T(8,128)S(1)}, u32[]{:S(2)}, u32[]{:S(2)}) collective-permute-start(f32[2,1024,256]{2,1,0:T(8,128)S(1)} %get-tuple-element.23), channel_id=1, source_target_pairs={{3,2},{7,6},{11,10},{15,14},{19,18},{23,22},{27,26},{31,30}} | collective-permute-start | bytes 6291464 | tf_op jit(solution)/shard_map/ppermute | solution.py:55
  105.8 52.2 %collective-permute-start.14 = (f32[2,1024,256]{2,1,0:T(8,128)S(1)}, f32[2,1024,256]{2,1,0:T(8,128)S(1)}, u32[]{:S(2)}, u32[]{:S(2)}) collective-permute-start(f32[2,1024,256]{2,1,0:T(8,128)S(1)} %collective-permute-done.12), channel_id=1, source_target_pairs={{1,2},{2,3},{5,6},{6,7},{9,10},{10,11},{13,14},{14,15},{17,18},{18... | collective-permute-start | bytes 6291464 | tf_op jit(solution)/shard_map/ppermute | solution.py:77
  107.1 52.2 %collective-permute-start.15 = (f32[2,1024,256]{2,1,0:T(8,128)S(1)}, f32[2,1024,256]{2,1,0:T(8,128)S(1)}, u32[]{:S(2)}, u32[]{:S(2)}) collective-permute-start(f32[2,1024,256]{2,1,0:T(8,128)S(1)} %collective-permute-done.13), channel_id=1, source_target_pairs={{1,0},{2,1},{5,4},{6,5},{9,8},{10,9},{13,12},{14,13},{17,16},{18,1... | collective-permute-start | bytes 6291464 | tf_op jit(solution)/shard_map/ppermute | solution.py:78
  151.5 46.6 %collective-permute-start.10 = (f32[2,1024,256]{2,1,0:T(8,128)}, f32[2,1024,256]{2,1,0:T(8,128)S(1)}, u32[]{:S(2)}, u32[]{:S(2)}) collective-permute-start(f32[2,1024,256]{2,1,0:T(8,128)} %get-tuple-element.21), channel_id=1, source_target_pairs={{2,1},{3,2},{6,5},{7,6},{10,9},{11,10},{14,13},{15,14},{18,17},{19... | collective-permute-start | bytes 6291464 | tf_op jit(solution)/shard_map/ppermute | solution.py:55
  155.8 5.5 %copy-start.3 = (f32[2,1024,256]{2,1,0:T(8,128)S(1)}, f32[2,1024,256]{2,1,0:T(8,128)}, u32[]{:S(2)}) copy-start(f32[2,1024,256]{2,1,0:T(8,128)} %param.6) | copy-start | bytes 6291460
  155.8 42.3 %collective-permute-start.7 = (f32[2,1024,256]{2,1,0:T(8,128)}, f32[2,1024,256]{2,1,0:T(8,128)}, u32[]{:S(2)}, u32[]{:S(2)}) collective-permute-start(f32[2,1024,256]{2,1,0:T(8,128)} %get-tuple-element.22), channel_id=1, source_target_pairs={{0,1},{1,2},{4,5},{5,6},{8,9},{9,10},{12,13},{13,14},{16,17},{17,1... | collective-permute-start | bytes 6291464 | tf_op jit(solution)/shard_map/ppermute | solution.py:54
  158.0 53.1 %collective-permute-start.16 = (f32[2,1024,256]{2,1,0:T(8,128)S(1)}, f32[2,1024,256]{2,1,0:T(8,128)S(1)}, u32[]{:S(2)}, u32[]{:S(2)}) collective-permute-start(f32[2,1024,256]{2,1,0:T(8,128)S(1)} %collective-permute-done.14), channel_id=1, source_target_pairs={{2,3},{6,7},{10,11},{14,15},{18,19},{22,23},{26,27},{30,31}} | collective-permute-start | bytes 6291464 | tf_op jit(solution)/shard_map/ppermute | solution.py:77
  159.3 52.3 %collective-permute-start.17 = (f32[2,1024,256]{2,1,0:T(8,128)S(1)}, f32[2,1024,256]{2,1,0:T(8,128)S(1)}, u32[]{:S(2)}, u32[]{:S(2)}) collective-permute-start(f32[2,1024,256]{2,1,0:T(8,128)S(1)} %collective-permute-done.15), channel_id=1, source_target_pairs={{1,0},{5,4},{9,8},{13,12},{17,16},{21,20},{25,24},{29,28}} | collective-permute-start | bytes 6291464 | tf_op jit(solution)/shard_map/ppermute | solution.py:78
  202.6 48.5 %collective-permute-start.11 = (f32[2,1024,256]{2,1,0:T(8,128)}, f32[2,1024,256]{2,1,0:T(8,128)S(1)}, u32[]{:S(2)}, u32[]{:S(2)}) collective-permute-start(f32[2,1024,256]{2,1,0:T(8,128)} %get-tuple-element.19), channel_id=1, source_target_pairs={{1,0},{2,1},{3,2},{5,4},{6,5},{7,6},{9,8},{10,9},{11,10},{13,12},{... | collective-permute-start | bytes 6291464 | tf_op jit(solution)/shard_map/ppermute | solution.py:55
  209.7 45.3 %collective-permute-start.8 = (f32[2,1024,256]{2,1,0:T(8,128)}, f32[2,1024,256]{2,1,0:T(8,128)}, u32[]{:S(2)}, u32[]{:S(2)}) collective-permute-start(f32[2,1024,256]{2,1,0:T(8,128)} %get-tuple-element.20), channel_id=1, source_target_pairs={{0,1},{1,2},{2,3},{4,5},{5,6},{6,7},{8,9},{9,10},{10,11},{12,13},{... | collective-permute-start | bytes 6291464 | tf_op jit(solution)/shard_map/ppermute | solution.py:54
  259.7 1.0 collective-permute-start.18
  262.9 23.4 %collective-permute-start.19 = (f32[1024,256]{1,0:T(8,128)S(1)}, f32[1024,256]{1,0:T(8,128)S(1)}, u32[]{:S(2)}, u32[]{:S(2)}) collective-permute-start(f32[1024,256]{1,0:T(8,128)S(1)} %fusion.63), channel_id=1, source_target_pairs={{8,4},{9,5},{10,6},{11,7},{24,20},{25,21},{26,22},{27,23}} | collective-permute-start | bytes 3145736 | tf_op jit(solution)/shard_map/ppermute | solution.py:160
  288.7 3.6 %collective-permute-start.20 = (f32[1024,256]{1,0:T(8,128)S(1)}, f32[1024,256]{1,0:T(8,128)S(1)}, u32[]{:S(2)}, u32[]{:S(2)}) collective-permute-start(f32[1024,256]{1,0:T(8,128)S(1)} %fusion.61), channel_id=1, source_target_pairs={{4,0},{5,1},{6,2},{7,3},{20,16},{21,17},{22,18},{23,19}} | collective-permute-start | bytes 3145736 | tf_op jit(solution)/shard_map/ppermute | solution.py:160
  (1 other events, 1.6 us)

commit v6 on v3

--- a/solution.py
+++ b/solution.py
@@ -158,7 +158,10 @@
         sender = relays - 1 - step
         leaving = local if step == 0 else local + apply(across_parts, entering)
         entering = entering + lax.ppermute(leaving, "tm", [(sender, sender - 1)])
-    finals = chain(entering, False)
+    if block_count == 2:
+        finals = [local + apply(across_parts, entering), driven[1] + apply(coupling_parts[1], entering)]
+    else:
+        finals = chain(entering, False)
     return pick_rows(jnp.stack(finals, axis=0), order)
 
 

time: 304 us -> 304 us (level)
  no operation moved by 1% of the time
where the time goes in v6:
time: 304 us; the launch traced here: 303 us
  waiting for transfers between devices  194 us (64%)
  starting transfers between devices  54.2 us (18%)
  matrix products  26 us (9%)
  other arithmetic  18.6 us (6%)
  Pallas kernels  5.24 us (2%)
  local copies, waits for them, and re-layouts  4.49 us (1%)
    ppermute x3, waiting for transfers between devices, line_reduce_scatter(): lax.ppermute(tile(me - count + step) + leftward, axis, left_route)  100 us
    ppermute x3, waiting for transfers between devices, line_all_to_all(): lax.ppermute(own_rows(me - distance), axis, [(k, k - distance) for k in r...  34.2 us
    ppermute x3, waiting for transfers between devices, line_all_to_all(): lax.ppermute(own_rows(me + distance), axis, [(k, k + distance) for k in r...  31.1 us
    dot_general x16, matrix products, bdot(): return jnp.dot(left, right, preferred_element_type=jnp.float32)  26 us
    ppermute x3, starting transfers between devices, line_reduce_scatter(): lax.ppermute(tile(me - count + step) + leftward, axis, left_route)  24.9 us
    ppermute x3, waiting for transfers between devices, shards(): entering = entering + lax.ppermute(leaving, 'tm', [(sender, sender - 1)])  24.3 us
    ppermute x3, starting transfers between devices, line_all_to_all(): lax.ppermute(own_rows(me - distance), axis, [(k, k - distance) for k in r...  7.66 us
    add x2, other arithmetic, line_reduce_scatter(): tile(me - count + step) + leftward  7.4 us
  transfers between devices with their start and end apart: 21, of which 11 were waited for; matrix products, arithmetic and copies ran while one was open for 10% of the time, Pallas kernels for 0%

profile of v6, /device:TPU:25, one launch (start us, length us, event | category | flops | bytes accessed | tf_op | source)
XLA Modules:
  0.0 303.1 jit_solution(17187749155264322895)
XLA Ops:
  3.3 4.0 %collective-permute-start.1 = (f32[2,256,256]{2,1,0:T(8,128)S(1)}, f32[2,256,256]{2,1,0:T(8,128)S(1)}, u32[]{:S(2)}, u32[]{:S(2)}) collective-permute-start(f32[2,256,256]{2,1,0:T(8,128)S(1)} %get-tuple-element.36), channel_id=1, source_target_pairs={{1,0},{2,1},{3,2},{5,4},{6,5},{7,6},{9,8},{10,9},{11,10},{13,12},{... | collective-permute-start | bytes 1572872 | tf_op jit(solution)/shard_map/ppermute | solution.py:96
  10.0 4.1 %collective-permute-start.13 = (f32[2,1024,256]{2,1,0:T(8,128)S(1)}, f32[2,1024,256]{2,1,0:T(8,128)S(1)}, u32[]{:S(2)}, u32[]{:S(2)}) collective-permute-start(f32[2,1024,256]{2,1,0:T(8,128)S(1)} %copy-done.2), channel_id=1, source_target_pairs={{1,0},{2,1},{3,2},{5,4},{6,5},{7,6},{9,8},{10,9},{11,10},{13,12},{... | collective-permute-start | bytes 6291464 | tf_op jit(solution)/shard_map/ppermute | solution.py:78
  14.1 2.6 collective-permute-done
  16.7 2.3 collective-permute-start.3
  20.7 18.5 %collective-permute-done.2 = f32[2,256,256]{2,1,0:T(8,128)S(1)} collective-permute-done((f32[2,256,256]{2,1,0:T(8,128)S(1)}, f32[2,256,256]{2,1,0:T(8,128)S(1)}, u32[]{:S(2)}, u32[]{:S(2)}) %collective-permute-start.2) | collective-permute-done | bytes 524320 | tf_op jit(solution)/shard_map/ppermute | solution.py:95
  40.6 33.2 %collective-permute-done.3 = f32[2,256,256]{2,1,0:T(8,128)S(1)} collective-permute-done((f32[2,256,256]{2,1,0:T(8,128)S(1)}, f32[2,256,256]{2,1,0:T(8,128)S(1)}, u32[]{:S(2)}, u32[]{:S(2)}) %collective-permute-start.3) | collective-permute-done | bytes 524320 | tf_op jit(solution)/shard_map/ppermute | solution.py:96
  74.0 10.0 %collective-permute-done.4 = f32[2,256,256]{2,1,0:T(8,128)S(1)} collective-permute-done((f32[2,256,256]{2,1,0:T(8,128)S(1)}, f32[2,256,256]{2,1,0:T(8,128)S(1)}, u32[]{:S(2)}, u32[]{:S(2)}) %collective-permute-start.4) | collective-permute-done | bytes 524320 | tf_op jit(solution)/shard_map/ppermute | solution.py:95
  92.1 13.7 %collective-permute-start.9 = (f32[2,1024,256]{2,1,0:T(8,128)S(1)}, f32[2,1024,256]{2,1,0:T(8,128)S(1)}, u32[]{:S(2)}, u32[]{:S(2)}) collective-permute-start(f32[2,1024,256]{2,1,0:T(8,128)S(1)} %get-tuple-element.21), channel_id=1, source_target_pairs={{3,2},{7,6},{11,10},{15,14},{19,18},{23,22},{27,26},{31,30}} | collective-permute-start | bytes 6291464 | tf_op jit(solution)/shard_map/ppermute | solution.py:55
  107.9 40.8 %collective-permute-done.9 = f32[2,1024,256]{2,1,0:T(8,128)S(1)} collective-permute-done((f32[2,1024,256]{2,1,0:T(8,128)S(1)}, f32[2,1024,256]{2,1,0:T(8,128)S(1)}, u32[]{:S(2)}, u32[]{:S(2)}) %collective-permute-start.9) | collective-permute-done | bytes 2097184 | tf_op jit(solution)/shard_map/ppermute | solution.py:55
  148.7 2.9 fusion.31
  151.6 4.1 %collective-permute-start.10 = (f32[2,1024,256]{2,1,0:T(8,128)}, f32[2,1024,256]{2,1,0:T(8,128)S(1)}, u32[]{:S(2)}, u32[]{:S(2)}) collective-permute-start(f32[2,1024,256]{2,1,0:T(8,128)} %get-tuple-element.19), channel_id=1, source_target_pairs={{2,1},{3,2},{6,5},{7,6},{10,9},{11,10},{14,13},{15,14},{18,17},{19... | collective-permute-start | bytes 6291464 | tf_op jit(solution)/shard_map/ppermute | solution.py:55
  155.8 2.1 collective-permute-start.7
  164.3 33.8 %collective-permute-done.10 = f32[2,1024,256]{2,1,0:T(8,128)S(1)} collective-permute-done((f32[2,1024,256]{2,1,0:T(8,128)}, f32[2,1024,256]{2,1,0:T(8,128)S(1)}, u32[]{:S(2)}, u32[]{:S(2)}) %collective-permute-start.10) | collective-permute-done | bytes 2097184 | tf_op jit(solution)/shard_map/ppermute | solution.py:55
  198.1 4.5 %fusion.29 = (f32[2,1024,256]{2,1,0:T(8,128)}, f32[2,1024,256]{2,1,0:T(8,128)}) fusion(f32[2,1024,256]{2,1,0:T(8,128)S(1)} %collective-permute-done.10, s32[]{:T(128)S(6)} %select_n.15, f32[1,1024,1024]{2,1,0:T(8,128)S(1)} %fusion.10, f32[1,1024,1024]{2,1,0:T(8,128)S(1)} %fusion.8, f32[2,1024,256]{2,1,0:T(8,128)} %collective-permute-done.7, s32[]{:T(128)S(6)} %select_n.16), kind=kLoop, calls=%fused_computation.54 | loop fusion | flops 2097152 | bytes 16777224 | tf_op jit(solution)/shard_map/add | solution.py:55
  202.5 7.1 %collective-permute-start.11 = (f32[2,1024,256]{2,1,0:T(8,128)}, f32[2,1024,256]{2,1,0:T(8,128)S(1)}, u32[]{:S(2)}, u32[]{:S(2)}) collective-permute-start(f32[2,1024,256]{2,1,0:T(8,128)} %get-tuple-element.17), channel_id=1, source_target_pairs={{1,0},{2,1},{3,2},{5,4},{6,5},{7,6},{9,8},{10,9},{11,10},{13,12},{... | collective-permute-start | bytes 6291464 | tf_op jit(solution)/shard_map/ppermute | solution.py:55
  213.2 7.0 %fusion.11 = f32[1024,2048]{1,0:T(8,128)} fusion(bf16[1024,1024]{1,0:T(8,128)(2,1)S(1)} %get-tuple-element.16, bf16[1024,1024]{1,0:T(8,128)(2,1)S(1)} %get-tuple-element.15, f32[2,1024,1024]{2,1,0:T(8,128)S(1)} %add_dynamic-update-slice_fusion), kind=kOutput, calls=%fused_computation.36 | convolution fusion | flops 4305453056 | bytes 16777216 | tf_op jit(solution)/shard_map/dot_general | solution.py:29
  220.1 5.0 %fusion.5 = (bf16[1024,1024]{1,0:T(8,128)(2,1)S(1)}, bf16[1024,1024]{1,0:T(8,128)(2,1)S(1)}) fusion(f32[2,1024,1024]{2,1,0:T(8,128)S(1)} %add_dynamic-update-slice_fusion, f32[1024,2048]{1,0:T(8,128)} %fusion.11), kind=kOutput, calls=%fused_computation.27 | convolution fusion | flops 2161115136 | bytes 20971520 | tf_op jit(solution)/shard_map/dot_general | solution.py:29
  225.1 25.9 %collective-permute-done.11 = f32[2,1024,256]{2,1,0:T(8,128)S(1)} collective-permute-done((f32[2,1024,256]{2,1,0:T(8,128)}, f32[2,1024,256]{2,1,0:T(8,128)S(1)}, u32[]{:S(2)}, u32[]{:S(2)}) %collective-permute-start.11) | collective-permute-done | bytes 2097184 | tf_op jit(solution)/shard_map/ppermute | solution.py:55
  251.0 4.0 %collective-permute-done.8 = f32[2,1024,256]{2,1,0:T(8,128)} collective-permute-done((f32[2,1024,256]{2,1,0:T(8,128)}, f32[2,1024,256]{2,1,0:T(8,128)}, u32[]{:S(2)}, u32[]{:S(2)}) %collective-permute-start.8) | collective-permute-done | bytes 2097184 | tf_op jit(solution)/shard_map/ppermute | solution.py:54
  255.0 2.4 fusion.22
  264.0 22.1 %collective-permute-done.19 = f32[1024,256]{1,0:T(8,128)S(1)} collective-permute-done((f32[1024,256]{1,0:T(8,128)S(1)}, f32[1024,256]{1,0:T(8,128)S(1)}, u32[]{:S(2)}, u32[]{:S(2)}) %collective-permute-start.19) | collective-permute-done | bytes 1048608 | tf_op jit(solution)/shard_map/ppermute | solution.py:160
  289.8 2.2 collective-permute-done.20
  296.4 1.5 pad_maximum_fusion.field_ref
  297.9 5.2 %shard_map.46 = f32[2,1024,256]{2,1,0:T(8,128)} custom-call(s32[1024]{0:T(1024)} %order_ref.1, f32[2,1024,256]{2,1,0:T(8,128)} %pad_maximum_fusion.field_ref), custom_call_target="tpu_custom_call" | custom-call | bytes 4194304 | tf_op jit(solution)/shard_map/pallas_call | solution.py:118
  (71 shorter events, 43.5 us)
Async XLA Ops:
  1.6 7.1 %copy-start.2 = (f32[2,1024,256]{2,1,0:T(8,128)S(1)}, f32[2,1024,256]{2,1,0:T(8,128)}, u32[]{:S(2)}) copy-start(f32[2,1024,256]{2,1,0:T(8,128)} %param.6) | copy-start | bytes 6291460
  1.9 14.8 %collective-permute-start = (f32[2,256,256]{2,1,0:T(8,128)S(1)}, f32[2,256,256]{2,1,0:T(8,128)S(1)}, u32[]{:S(2)}, u32[]{:S(2)}) collective-permute-start(f32[2,256,256]{2,1,0:T(8,128)S(1)} %get-tuple-element.37), channel_id=1, source_target_pairs={{0,1},{1,2},{2,3},{4,5},{5,6},{6,7},{8,9},{9,10},{10,11},{12,13},{... | collective-permute-start | bytes 1572872 | tf_op jit(solution)/shard_map/ppermute | solution.py:95
  3.3 15.9 %collective-permute-start.1 = (f32[2,256,256]{2,1,0:T(8,128)S(1)}, f32[2,256,256]{2,1,0:T(8,128)S(1)}, u32[]{:S(2)}, u32[]{:S(2)}) collective-permute-start(f32[2,256,256]{2,1,0:T(8,128)S(1)} %get-tuple-element.36), channel_id=1, source_target_pairs={{1,0},{2,1},{3,2},{5,4},{6,5},{7,6},{9,8},{10,9},{11,10},{13,12},{... | collective-permute-start | bytes 1572872 | tf_op jit(solution)/shard_map/ppermute | solution.py:96
  7.4 31.7 %collective-permute-start.2 = (f32[2,256,256]{2,1,0:T(8,128)S(1)}, f32[2,256,256]{2,1,0:T(8,128)S(1)}, u32[]{:S(2)}, u32[]{:S(2)}) collective-permute-start(f32[2,256,256]{2,1,0:T(8,128)S(1)} %get-tuple-element.35), channel_id=1, source_target_pairs={{0,2},{1,3},{4,6},{5,7},{8,10},{9,11},{12,14},{13,15},{16,18},{17,... | collective-permute-start | bytes 1572872 | tf_op jit(solution)/shard_map/ppermute | solution.py:95
  8.7 97.1 %collective-permute-start.12 = (f32[2,1024,256]{2,1,0:T(8,128)S(1)}, f32[2,1024,256]{2,1,0:T(8,128)S(1)}, u32[]{:S(2)}, u32[]{:S(2)}) collective-permute-start(f32[2,1024,256]{2,1,0:T(8,128)S(1)} %copy-done.2), channel_id=1, source_target_pairs={{0,1},{1,2},{2,3},{4,5},{5,6},{6,7},{8,9},{9,10},{10,11},{12,13},{... | collective-permute-start | bytes 6291464 | tf_op jit(solution)/shard_map/ppermute | solution.py:77
  10.0 97.1 %collective-permute-start.13 = (f32[2,1024,256]{2,1,0:T(8,128)S(1)}, f32[2,1024,256]{2,1,0:T(8,128)S(1)}, u32[]{:S(2)}, u32[]{:S(2)}) collective-permute-start(f32[2,1024,256]{2,1,0:T(8,128)S(1)} %copy-done.2), channel_id=1, source_target_pairs={{1,0},{2,1},{3,2},{5,4},{6,5},{7,6},{9,8},{10,9},{11,10},{13,12},{... | collective-permute-start | bytes 6291464 | tf_op jit(solution)/shard_map/ppermute | solution.py:78
  16.7 57.1 %collective-permute-start.3 = (f32[2,256,256]{2,1,0:T(8,128)S(1)}, f32[2,256,256]{2,1,0:T(8,128)S(1)}, u32[]{:S(2)}, u32[]{:S(2)}) collective-permute-start(f32[2,256,256]{2,1,0:T(8,128)S(1)} %get-tuple-element.34), channel_id=1, source_target_pairs={{2,0},{3,1},{6,4},{7,5},{10,8},{11,9},{14,12},{15,13},{18,16},{19,... | collective-permute-start | bytes 1572872 | tf_op jit(solution)/shard_map/ppermute | solution.py:96
  19.2 64.8 %collective-permute-start.4 = (f32[2,256,256]{2,1,0:T(8,128)S(1)}, f32[2,256,256]{2,1,0:T(8,128)S(1)}, u32[]{:S(2)}, u32[]{:S(2)}) collective-permute-start(f32[2,256,256]{2,1,0:T(8,128)S(1)} %get-tuple-element.39), channel_id=1, source_target_pairs={{0,3},{4,7},{8,11},{12,15},{16,19},{20,23},{24,27},{28,31}} | collective-permute-start | bytes 1572872 | tf_op jit(solution)/shard_map/ppermute | solution.py:95
  39.1 45.9 %collective-permute-start.5 = (f32[2,256,256]{2,1,0:T(8,128)S(1)}, f32[2,256,256]{2,1,0:T(8,128)S(1)}, u32[]{:S(2)}, u32[]{:S(2)}) collective-permute-start(f32[2,256,256]{2,1,0:T(8,128)S(1)} %get-tuple-element.33), channel_id=1, source_target_pairs={{3,0},{7,4},{11,8},{15,12},{19,16},{23,20},{27,24},{31,28}} | collective-permute-start | bytes 1572872 | tf_op jit(solution)/shard_map/ppermute | solution.py:96
  85.2 1.6 copy-start
  91.3 16.6 %collective-permute-start.6 = (f32[2,1024,256]{2,1,0:T(8,128)S(1)}, f32[2,1024,256]{2,1,0:T(8,128)S(1)}, u32[]{:S(2)}, u32[]{:S(2)}) collective-permute-start(f32[2,1024,256]{2,1,0:T(8,128)S(1)} %get-tuple-element.22), channel_id=1, source_target_pairs={{0,1},{4,5},{8,9},{12,13},{16,17},{20,21},{24,25},{28,29}} | collective-permute-start | bytes 6291464 | tf_op jit(solution)/shard_map/ppermute | solution.py:54
  92.1 56.6 %collective-permute-start.9 = (f32[2,1024,256]{2,1,0:T(8,128)S(1)}, f32[2,1024,256]{2,1,0:T(8,128)S(1)}, u32[]{:S(2)}, u32[]{:S(2)}) collective-permute-start(f32[2,1024,256]{2,1,0:T(8,128)S(1)} %get-tuple-element.21), channel_id=1, source_target_pairs={{3,2},{7,6},{11,10},{15,14},{19,18},{23,22},{27,26},{31,30}} | collective-permute-start | bytes 6291464 | tf_op jit(solution)/shard_map/ppermute | solution.py:55
  105.8 52.1 %collective-permute-start.14 = (f32[2,1024,256]{2,1,0:T(8,128)S(1)}, f32[2,1024,256]{2,1,0:T(8,128)S(1)}, u32[]{:S(2)}, u32[]{:S(2)}) collective-permute-start(f32[2,1024,256]{2,1,0:T(8,128)S(1)} %collective-permute-done.12), channel_id=1, source_target_pairs={{1,2},{2,3},{5,6},{6,7},{9,10},{10,11},{13,14},{14,15},{17,18},{18... | collective-permute-start | bytes 6291464 | tf_op jit(solution)/shard_map/ppermute | solution.py:77
  107.1 52.1 %collective-permute-start.15 = (f32[2,1024,256]{2,1,0:T(8,128)S(1)}, f32[2,1024,256]{2,1,0:T(8,128)S(1)}, u32[]{:S(2)}, u32[]{:S(2)}) collective-permute-start(f32[2,1024,256]{2,1,0:T(8,128)S(1)} %collective-permute-done.13), channel_id=1, source_target_pairs={{1,0},{2,1},{5,4},{6,5},{9,8},{10,9},{13,12},{14,13},{17,16},{18,1... | collective-permute-start | bytes 6291464 | tf_op jit(solution)/shard_map/ppermute | solution.py:78
  151.6 46.4 %collective-permute-start.10 = (f32[2,1024,256]{2,1,0:T(8,128)}, f32[2,1024,256]{2,1,0:T(8,128)S(1)}, u32[]{:S(2)}, u32[]{:S(2)}) collective-permute-start(f32[2,1024,256]{2,1,0:T(8,128)} %get-tuple-element.19), channel_id=1, source_target_pairs={{2,1},{3,2},{6,5},{7,6},{10,9},{11,10},{14,13},{15,14},{18,17},{19... | collective-permute-start | bytes 6291464 | tf_op jit(solution)/shard_map/ppermute | solution.py:55
  155.8 5.5 %copy-start.3 = (f32[2,1024,256]{2,1,0:T(8,128)S(1)}, f32[2,1024,256]{2,1,0:T(8,128)}, u32[]{:S(2)}) copy-start(f32[2,1024,256]{2,1,0:T(8,128)} %param.6) | copy-start | bytes 6291460
  155.8 42.3 %collective-permute-start.7 = (f32[2,1024,256]{2,1,0:T(8,128)}, f32[2,1024,256]{2,1,0:T(8,128)}, u32[]{:S(2)}, u32[]{:S(2)}) collective-permute-start(f32[2,1024,256]{2,1,0:T(8,128)} %get-tuple-element.20), channel_id=1, source_target_pairs={{0,1},{1,2},{4,5},{5,6},{8,9},{9,10},{12,13},{13,14},{16,17},{17,1... | collective-permute-start | bytes 6291464 | tf_op jit(solution)/shard_map/ppermute | solution.py:54
  157.9 53.1 %collective-permute-start.16 = (f32[2,1024,256]{2,1,0:T(8,128)S(1)}, f32[2,1024,256]{2,1,0:T(8,128)S(1)}, u32[]{:S(2)}, u32[]{:S(2)}) collective-permute-start(f32[2,1024,256]{2,1,0:T(8,128)S(1)} %collective-permute-done.14), channel_id=1, source_target_pairs={{2,3},{6,7},{10,11},{14,15},{18,19},{22,23},{26,27},{30,31}} | collective-permute-start | bytes 6291464 | tf_op jit(solution)/shard_map/ppermute | solution.py:77
  159.2 52.3 %collective-permute-start.17 = (f32[2,1024,256]{2,1,0:T(8,128)S(1)}, f32[2,1024,256]{2,1,0:T(8,128)S(1)}, u32[]{:S(2)}, u32[]{:S(2)}) collective-permute-start(f32[2,1024,256]{2,1,0:T(8,128)S(1)} %collective-permute-done.15), channel_id=1, source_target_pairs={{1,0},{5,4},{9,8},{13,12},{17,16},{21,20},{25,24},{29,28}} | collective-permute-start | bytes 6291464 | tf_op jit(solution)/shard_map/ppermute | solution.py:78
  202.5 48.5 %collective-permute-start.11 = (f32[2,1024,256]{2,1,0:T(8,128)}, f32[2,1024,256]{2,1,0:T(8,128)S(1)}, u32[]{:S(2)}, u32[]{:S(2)}) collective-permute-start(f32[2,1024,256]{2,1,0:T(8,128)} %get-tuple-element.17), channel_id=1, source_target_pairs={{1,0},{2,1},{3,2},{5,4},{6,5},{7,6},{9,8},{10,9},{11,10},{13,12},{... | collective-permute-start | bytes 6291464 | tf_op jit(solution)/shard_map/ppermute | solution.py:55
  209.7 45.3 %collective-permute-start.8 = (f32[2,1024,256]{2,1,0:T(8,128)}, f32[2,1024,256]{2,1,0:T(8,128)}, u32[]{:S(2)}, u32[]{:S(2)}) collective-permute-start(f32[2,1024,256]{2,1,0:T(8,128)} %get-tuple-element.18), channel_id=1, source_target_pairs={{0,1},{1,2},{2,3},{4,5},{5,6},{6,7},{8,9},{9,10},{10,11},{12,13},{... | collective-permute-start | bytes 6291464 | tf_op jit(solution)/shard_map/ppermute | solution.py:54
  259.6 1.0 collective-permute-start.18
  262.7 23.4 %collective-permute-start.19 = (f32[1024,256]{1,0:T(8,128)S(1)}, f32[1024,256]{1,0:T(8,128)S(1)}, u32[]{:S(2)}, u32[]{:S(2)}) collective-permute-start(f32[1024,256]{1,0:T(8,128)S(1)} %fusion.59), channel_id=1, source_target_pairs={{8,4},{9,5},{10,6},{11,7},{24,20},{25,21},{26,22},{27,23}} | collective-permute-start | bytes 3145736 | tf_op jit(solution)/shard_map/ppermute | solution.py:160
  288.4 3.6 %collective-permute-start.20 = (f32[1024,256]{1,0:T(8,128)S(1)}, f32[1024,256]{1,0:T(8,128)S(1)}, u32[]{:S(2)}, u32[]{:S(2)}) collective-permute-start(f32[1024,256]{1,0:T(8,128)S(1)} %fusion.57), channel_id=1, source_target_pairs={{4,0},{5,1},{6,2},{7,3},{20,16},{21,17},{22,18},{23,19}} | collective-permute-start | bytes 3145736 | tf_op jit(solution)/shard_map/ppermute | solution.py:160
  (1 other events, 1.6 us)

commit v7 on v3

--- a/solution.py
+++ b/solution.py
@@ -137,7 +137,12 @@
     across = coupling_full[block_count - 1]
     for block in range(block_count - 2, -1, -1):
         across = apply(coupling_parts[block], across)
-    driven_all, across_parts = line_reduce_scatter(partial, "cols", split(across, 2))
+    if block_count == 2:
+        picked_maps = pick_rows(jnp.stack([across, coupling_full[1]], axis=0), order)
+        ready = (split(across, 2), split(picked_maps[0], 2), split(picked_maps[1], 2))
+        driven_all, (across_parts, picked_across, picked_last) = line_reduce_scatter(partial, "cols", ready)
+    else:
+        driven_all, across_parts = line_reduce_scatter(partial, "cols", split(across, 2))
     driven = [driven_all[block] for block in range(block_count)]
 
     def chain(entering, skip_last):
@@ -158,6 +163,11 @@
         sender = relays - 1 - step
         leaving = local if step == 0 else local + apply(across_parts, entering)
         entering = entering + lax.ppermute(leaving, "tm", [(sender, sender - 1)])
+    if block_count == 2:
+        picked_vectors = pick_rows(jnp.stack([local, driven[1]], axis=0), order)
+        first_block = picked_vectors[0] + apply(picked_across, entering)
+        last_block = picked_vectors[1] + apply(picked_last, entering)
+        return jnp.stack([first_block, last_block], axis=0)
     finals = chain(entering, False)
     return pick_rows(jnp.stack(finals, axis=0), order)
 

time: 304 us -> 311 us (1.023)
  waiting for transfers between devices: 194 us -> 165 us
  other arithmetic: 18.3 us -> 34.2 us
  Pallas kernels: 5.24 us -> 17.7 us
  local copies, waits for them, and re-layouts: 4.42 us -> 7.76 us
    ppermute x3, waiting for transfers between devices: 101 us -> 74.6 us  [line_reduce_scatter(): lax.ppermute(tile(me - count + step) + leftward, axis, left_route)]
    pallas_call x1 -> x2, Pallas kernels: 5.24 us -> 17.7 us  [pick_rows(): pl.pallas_call(pick_rows_kernel, out_shape=jax.ShapeDtypeStruct(field.sha...]
    convert_element_type x8, other arithmetic: 2.2 us -> 11.5 us  [split(): parts.append(kept.astype(low))]
    another operation x1 -> x3, other arithmetic: 1.48 us -> 7.17 us  [the longest x1 4.25 us: shards(): jnp.stack([across, coupling_full[1]], axis=0)]
  transfers between devices with their start and end apart: 21 -> 21, of which waited for: 11 -> 9; matrix products, arithmetic and copies ran while one was open for 10% -> 15% of each run, Pallas kernels for 0% -> 6%
where the time goes in v7:
time: 311 us; the launch traced here: 310 us
  waiting for transfers between devices  165 us (53%)
  starting transfers between devices  56.4 us (18%)
  other arithmetic  34.2 us (11%)
  matrix products  28.6 us (9%)
  Pallas kernels  17.7 us (6%)
  local copies, waits for them, and re-layouts  7.76 us (2%)
    ppermute x3, waiting for transfers between devices, line_reduce_scatter(): lax.ppermute(tile(me - count + step) + leftward, axis, left_route)  74.6 us
    ppermute x3, waiting for transfers between devices, line_all_to_all(): lax.ppermute(own_rows(me - distance), axis, [(k, k - distance) for k in r...  34.2 us
    ppermute x3, waiting for transfers between devices, line_all_to_all(): lax.ppermute(own_rows(me + distance), axis, [(k, k + distance) for k in r...  31.1 us
    dot_general x16, matrix products, bdot(): return jnp.dot(left, right, preferred_element_type=jnp.float32)  28.6 us
    ppermute x3, starting transfers between devices, line_reduce_scatter(): lax.ppermute(tile(me - count + step) + leftward, axis, left_route)  26.1 us
    ppermute x3, waiting for transfers between devices, shards(): entering = entering + lax.ppermute(leaving, 'tm', [(sender, sender - 1)])  21.8 us
    pallas_call x2, Pallas kernels, pick_rows(): pl.pallas_call(pick_rows_kernel, out_shape=jax.ShapeDtypeStruct(field.sha...  17.7 us
    convert_element_type x8, other arithmetic, split(): parts.append(kept.astype(low))  11.5 us
  transfers between devices with their start and end apart: 21, of which 9 were waited for; matrix products, arithmetic and copies ran while one was open for 15% of the time, Pallas kernels for 6%

profile of v7, /device:TPU:25, one launch (start us, length us, event | category | flops | bytes accessed | tf_op | source)
XLA Modules:
  0.0 310.3 jit_solution(4352503516049980762)
XLA Ops:
  3.3 4.0 %collective-permute-start.1 = (f32[2,256,256]{2,1,0:T(8,128)S(1)}, f32[2,256,256]{2,1,0:T(8,128)S(1)}, u32[]{:S(2)}, u32[]{:S(2)}) collective-permute-start(f32[2,256,256]{2,1,0:T(8,128)S(1)} %get-tuple-element.50), channel_id=1, source_target_pairs={{1,0},{2,1},{3,2},{5,4},{6,5},{7,6},{9,8},{10,9},{11,10},{13,12},{... | collective-permute-start | bytes 1572872 | tf_op jit(solution)/shard_map/ppermute | solution.py:96
  10.0 4.1 %collective-permute-start.13 = (f32[2,1024,256]{2,1,0:T(8,128)S(1)}, f32[2,1024,256]{2,1,0:T(8,128)S(1)}, u32[]{:S(2)}, u32[]{:S(2)}) collective-permute-start(f32[2,1024,256]{2,1,0:T(8,128)S(1)} %copy-done.9), channel_id=1, source_target_pairs={{1,0},{2,1},{3,2},{5,4},{6,5},{7,6},{9,8},{10,9},{11,10},{13,12},{... | collective-permute-start | bytes 6291464 | tf_op jit(solution)/shard_map/ppermute | solution.py:78
  14.1 2.6 collective-permute-done
  16.7 2.3 collective-permute-start.3
  20.7 18.5 %collective-permute-done.2 = f32[2,256,256]{2,1,0:T(8,128)S(1)} collective-permute-done((f32[2,256,256]{2,1,0:T(8,128)S(1)}, f32[2,256,256]{2,1,0:T(8,128)S(1)}, u32[]{:S(2)}, u32[]{:S(2)}) %collective-permute-start.2) | collective-permute-done | bytes 524320 | tf_op jit(solution)/shard_map/ppermute | solution.py:95
  40.6 33.2 %collective-permute-done.3 = f32[2,256,256]{2,1,0:T(8,128)S(1)} collective-permute-done((f32[2,256,256]{2,1,0:T(8,128)S(1)}, f32[2,256,256]{2,1,0:T(8,128)S(1)}, u32[]{:S(2)}, u32[]{:S(2)}) %collective-permute-start.3) | collective-permute-done | bytes 524320 | tf_op jit(solution)/shard_map/ppermute | solution.py:96
  74.0 10.0 %collective-permute-done.4 = f32[2,256,256]{2,1,0:T(8,128)S(1)} collective-permute-done((f32[2,256,256]{2,1,0:T(8,128)S(1)}, f32[2,256,256]{2,1,0:T(8,128)S(1)}, u32[]{:S(2)}, u32[]{:S(2)}) %collective-permute-start.4) | collective-permute-done | bytes 524320 | tf_op jit(solution)/shard_map/ppermute | solution.py:95
  92.2 13.7 %collective-permute-start.9 = (f32[2,1024,256]{2,1,0:T(8,128)S(1)}, f32[2,1024,256]{2,1,0:T(8,128)S(1)}, u32[]{:S(2)}, u32[]{:S(2)}) collective-permute-start(f32[2,1024,256]{2,1,0:T(8,128)S(1)} %get-tuple-element.33), channel_id=1, source_target_pairs={{3,2},{7,6},{11,10},{15,14},{19,18},{23,22},{27,26},{31,30}} | collective-permute-start | bytes 6291464 | tf_op jit(solution)/shard_map/ppermute | solution.py:55
  108.0 40.8 %collective-permute-done.9 = f32[2,1024,256]{2,1,0:T(8,128)S(1)} collective-permute-done((f32[2,1024,256]{2,1,0:T(8,128)S(1)}, f32[2,1024,256]{2,1,0:T(8,128)S(1)}, u32[]{:S(2)}, u32[]{:S(2)}) %collective-permute-start.9) | collective-permute-done | bytes 2097184 | tf_op jit(solution)/shard_map/ppermute | solution.py:55
  148.8 2.9 fusion.35
  151.8 4.1 %collective-permute-start.10 = (f32[2,1024,256]{2,1,0:T(8,128)}, f32[2,1024,256]{2,1,0:T(8,128)S(1)}, u32[]{:S(2)}, u32[]{:S(2)}) collective-permute-start(f32[2,1024,256]{2,1,0:T(8,128)} %get-tuple-element.31), channel_id=1, source_target_pairs={{2,1},{3,2},{6,5},{7,6},{10,9},{11,10},{14,13},{15,14},{18,17},{19... | collective-permute-start | bytes 6291464 | tf_op jit(solution)/shard_map/ppermute | solution.py:55
  164.4 33.8 %collective-permute-done.10 = f32[2,1024,256]{2,1,0:T(8,128)S(1)} collective-permute-done((f32[2,1024,256]{2,1,0:T(8,128)}, f32[2,1024,256]{2,1,0:T(8,128)S(1)}, u32[]{:S(2)}, u32[]{:S(2)}) %collective-permute-start.10) | collective-permute-done | bytes 2097184 | tf_op jit(solution)/shard_map/ppermute | solution.py:55
  198.2 4.5 %fusion.33 = (f32[2,1024,256]{2,1,0:T(8,128)}, f32[2,1024,256]{2,1,0:T(8,128)}) fusion(f32[2,1024,256]{2,1,0:T(8,128)S(1)} %collective-permute-done.10, s32[]{:T(128)S(6)} %select_n.15, f32[1,1024,1024]{2,1,0:T(8,128)S(1)} %fusion.14, f32[1,1024,1024]{2,1,0:T(8,128)S(1)} %fusion.12, f32[2,1024,256]{2,1,0:T(8,128)} %collective-permute-done.7, s32[]{:T(128)S(6)} %select_n.16), kind=kLoop, calls=%fused_computation.65 | loop fusion | flops 2097152 | bytes 16777224 | tf_op jit(solution)/shard_map/add | solution.py:55
  202.7 8.3 %collective-permute-start.11 = (f32[2,1024,256]{2,1,0:T(8,128)}, f32[2,1024,256]{2,1,0:T(8,128)}, u32[]{:S(2)}, u32[]{:S(2)}) collective-permute-start(f32[2,1024,256]{2,1,0:T(8,128)} %get-tuple-element.29), channel_id=1, source_target_pairs={{1,0},{2,1},{3,2},{5,4},{6,5},{7,6},{9,8},{10,9},{11,10},{13,12},{... | collective-permute-start | bytes 6291464 | tf_op jit(solution)/shard_map/ppermute | solution.py:55
  214.5 7.0 %fusion.15 = f32[1024,2048]{1,0:T(8,128)} fusion(bf16[1024,1024]{1,0:T(8,128)(2,1)S(1)} %get-tuple-element.28, bf16[1024,1024]{1,0:T(8,128)(2,1)S(1)} %get-tuple-element.27, f32[2,1024,1024]{2,1,0:T(8,128)S(1)} %add_dynamic-update-slice_fusion), kind=kOutput, calls=%fused_computation.47 | convolution fusion | flops 4305453056 | bytes 16777216 | tf_op jit(solution)/shard_map/dot_general | solution.py:29
  221.9 6.4 %fusion.5 = (bf16[1024,1024]{1,0:T(8,128)(2,1)}, bf16[1024,1024]{1,0:T(8,128)(2,1)}, f32[1024,1024]{1,0:T(8,128)S(1)}) fusion(f32[2,1024,1024]{2,1,0:T(8,128)S(1)} %add_dynamic-update-slice_fusion, f32[1024,2048]{1,0:T(8,128)} %fusion.15), kind=kOutput, calls=%fused_computation.32 | convolution fusion | flops 2161115136 | bytes 25165824 | tf_op jit(solution)/shard_map/dot_general | solution.py:29
  228.3 4.3 %pad_maximum_fusion.field_ref = f32[2,1024,1024]{2,1,0:T(8,128)} fusion(f32[1,1024,1024]{2,1,0:T(8,128)S(1)} %slice.120, f32[1,1024,1024]{2,1,0:T(8,128)S(1)} %bitcast.105), kind=kLoop, calls=%fused_computation.14 | loop fusion | flops 2097152 | bytes 16777216 | tf_op jit(solution)/shard_map/stack | solution.py:141
  232.5 12.5 %shard_map.46 = f32[2,1024,1024]{2,1,0:T(8,128)} custom-call(s32[1024]{0:T(1024)} %order_ref.3, f32[2,1024,1024]{2,1,0:T(8,128)} %pad_maximum_fusion.field_ref), custom_call_target="tpu_custom_call" | custom-call | bytes 16777216 | tf_op jit(solution)/shard_map/pallas_call | solution.py:118
  245.0 8.0 %fusion.9 = (bf16[1024,1024]{1,0:T(8,128)(2,1)}, bf16[1024,1024]{1,0:T(8,128)(2,1)S(1)}, bf16[1024,1024]{1,0:T(8,128)(2,1)}, bf16[1024,1024]{1,0:T(8,128)(2,1)}) fusion(f32[2,1024,1024]{2,1,0:T(8,128)} %shard_map.46), kind=kLoop, calls=%fused_computation.36 | loop fusion | flops 10485760 | bytes 16777216 | tf_op jit(solution)/shard_map/convert_element_type | solution.py:22
  253.0 3.3 %collective-permute-done.8 = f32[2,1024,256]{2,1,0:T(8,128)} collective-permute-done((f32[2,1024,256]{2,1,0:T(8,128)}, f32[2,1024,256]{2,1,0:T(8,128)}, u32[]{:S(2)}, u32[]{:S(2)}) %collective-permute-start.8) | collective-permute-done | bytes 2097184 | tf_op jit(solution)/shard_map/ppermute | solution.py:54
  256.3 2.9 fusion.26
  267.1 21.8 %collective-permute-done.19 = f32[1024,256]{1,0:T(8,128)S(1)} collective-permute-done((f32[1024,256]{1,0:T(8,128)S(1)}, f32[1024,256]{1,0:T(8,128)S(1)}, u32[]{:S(2)}, u32[]{:S(2)}) %collective-permute-start.19) | collective-permute-done | bytes 1048608 | tf_op jit(solution)/shard_map/ppermute | solution.py:165
  292.3 2.3 collective-permute-start.20
  296.0 5.3 %shard_map.47 = f32[2,1024,256]{2,1,0:T(8,128)} custom-call(s32[1024]{0:T(1024)} %order_ref.3, f32[2,1024,256]{2,1,0:T(8,128)} %pad_maximum_fusion.1.field_ref), custom_call_target="tpu_custom_call" | custom-call | bytes 4194304 | tf_op jit(solution)/shard_map/pallas_call | solution.py:118
  (104 shorter events, 53.1 us)
Async XLA Ops:
  1.9 14.8 %collective-permute-start = (f32[2,256,256]{2,1,0:T(8,128)S(1)}, f32[2,256,256]{2,1,0:T(8,128)S(1)}, u32[]{:S(2)}, u32[]{:S(2)}) collective-permute-start(f32[2,256,256]{2,1,0:T(8,128)S(1)} %get-tuple-element.51), channel_id=1, source_target_pairs={{0,1},{1,2},{2,3},{4,5},{5,6},{6,7},{8,9},{9,10},{10,11},{12,13},{... | collective-permute-start | bytes 1572872 | tf_op jit(solution)/shard_map/ppermute | solution.py:95
  3.3 15.9 %collective-permute-start.1 = (f32[2,256,256]{2,1,0:T(8,128)S(1)}, f32[2,256,256]{2,1,0:T(8,128)S(1)}, u32[]{:S(2)}, u32[]{:S(2)}) collective-permute-start(f32[2,256,256]{2,1,0:T(8,128)S(1)} %get-tuple-element.50), channel_id=1, source_target_pairs={{1,0},{2,1},{3,2},{5,4},{6,5},{7,6},{9,8},{10,9},{11,10},{13,12},{... | collective-permute-start | bytes 1572872 | tf_op jit(solution)/shard_map/ppermute | solution.py:96
  7.4 31.7 %collective-permute-start.2 = (f32[2,256,256]{2,1,0:T(8,128)S(1)}, f32[2,256,256]{2,1,0:T(8,128)S(1)}, u32[]{:S(2)}, u32[]{:S(2)}) collective-permute-start(f32[2,256,256]{2,1,0:T(8,128)S(1)} %get-tuple-element.49), channel_id=1, source_target_pairs={{0,2},{1,3},{4,6},{5,7},{8,10},{9,11},{12,14},{13,15},{16,18},{17,... | collective-permute-start | bytes 1572872 | tf_op jit(solution)/shard_map/ppermute | solution.py:95
  8.7 97.2 %collective-permute-start.12 = (f32[2,1024,256]{2,1,0:T(8,128)S(1)}, f32[2,1024,256]{2,1,0:T(8,128)S(1)}, u32[]{:S(2)}, u32[]{:S(2)}) collective-permute-start(f32[2,1024,256]{2,1,0:T(8,128)S(1)} %copy-done.9), channel_id=1, source_target_pairs={{0,1},{1,2},{2,3},{4,5},{5,6},{6,7},{8,9},{9,10},{10,11},{12,13},{... | collective-permute-start | bytes 6291464 | tf_op jit(solution)/shard_map/ppermute | solution.py:77
  10.0 97.2 %collective-permute-start.13 = (f32[2,1024,256]{2,1,0:T(8,128)S(1)}, f32[2,1024,256]{2,1,0:T(8,128)S(1)}, u32[]{:S(2)}, u32[]{:S(2)}) collective-permute-start(f32[2,1024,256]{2,1,0:T(8,128)S(1)} %copy-done.9), channel_id=1, source_target_pairs={{1,0},{2,1},{3,2},{5,4},{6,5},{7,6},{9,8},{10,9},{11,10},{13,12},{... | collective-permute-start | bytes 6291464 | tf_op jit(solution)/shard_map/ppermute | solution.py:78
  16.7 57.1 %collective-permute-start.3 = (f32[2,256,256]{2,1,0:T(8,128)S(1)}, f32[2,256,256]{2,1,0:T(8,128)S(1)}, u32[]{:S(2)}, u32[]{:S(2)}) collective-permute-start(f32[2,256,256]{2,1,0:T(8,128)S(1)} %get-tuple-element.48), channel_id=1, source_target_pairs={{2,0},{3,1},{6,4},{7,5},{10,8},{11,9},{14,12},{15,13},{18,16},{19,... | collective-permute-start | bytes 1572872 | tf_op jit(solution)/shard_map/ppermute | solution.py:96
  19.2 64.8 %collective-permute-start.4 = (f32[2,256,256]{2,1,0:T(8,128)S(1)}, f32[2,256,256]{2,1,0:T(8,128)S(1)}, u32[]{:S(2)}, u32[]{:S(2)}) collective-permute-start(f32[2,256,256]{2,1,0:T(8,128)S(1)} %get-tuple-element.53), channel_id=1, source_target_pairs={{0,3},{4,7},{8,11},{12,15},{16,19},{20,23},{24,27},{28,31}} | collective-permute-start | bytes 1572872 | tf_op jit(solution)/shard_map/ppermute | solution.py:95
  39.1 45.9 %collective-permute-start.5 = (f32[2,256,256]{2,1,0:T(8,128)S(1)}, f32[2,256,256]{2,1,0:T(8,128)S(1)}, u32[]{:S(2)}, u32[]{:S(2)}) collective-permute-start(f32[2,256,256]{2,1,0:T(8,128)S(1)} %get-tuple-element.47), channel_id=1, source_target_pairs={{3,0},{7,4},{11,8},{15,12},{19,16},{23,20},{27,24},{31,28}} | collective-permute-start | bytes 1572872 | tf_op jit(solution)/shard_map/ppermute | solution.py:96
  90.1 108.1 %copy-start.1 = (f32[1,1024,1024]{2,1,0:T(8,128)}, f32[1,1024,1024]{2,1,0:T(8,128)S(1)}, u32[]{:S(2)}) copy-start(f32[1,1024,1024]{2,1,0:T(8,128)S(1)} %fusion.12) | copy-start | bytes 12582916
  90.9 107.3 %copy-start.3 = (f32[1,1024,1024]{2,1,0:T(8,128)}, f32[1,1024,1024]{2,1,0:T(8,128)S(1)}, u32[]{:S(2)}) copy-start(f32[1,1024,1024]{2,1,0:T(8,128)S(1)} %fusion.14) | copy-start | bytes 12582916
  91.4 16.6 %collective-permute-start.6 = (f32[2,1024,256]{2,1,0:T(8,128)S(1)}, f32[2,1024,256]{2,1,0:T(8,128)S(1)}, u32[]{:S(2)}, u32[]{:S(2)}) collective-permute-start(f32[2,1024,256]{2,1,0:T(8,128)S(1)} %get-tuple-element.34), channel_id=1, source_target_pairs={{0,1},{4,5},{8,9},{12,13},{16,17},{20,21},{24,25},{28,29}} | collective-permute-start | bytes 6291464 | tf_op jit(solution)/shard_map/ppermute | solution.py:54
  92.2 56.6 %collective-permute-start.9 = (f32[2,1024,256]{2,1,0:T(8,128)S(1)}, f32[2,1024,256]{2,1,0:T(8,128)S(1)}, u32[]{:S(2)}, u32[]{:S(2)}) collective-permute-start(f32[2,1024,256]{2,1,0:T(8,128)S(1)} %get-tuple-element.33), channel_id=1, source_target_pairs={{3,2},{7,6},{11,10},{15,14},{19,18},{23,22},{27,26},{31,30}} | collective-permute-start | bytes 6291464 | tf_op jit(solution)/shard_map/ppermute | solution.py:55
  105.9 52.1 %collective-permute-start.14 = (f32[2,1024,256]{2,1,0:T(8,128)S(1)}, f32[2,1024,256]{2,1,0:T(8,128)S(1)}, u32[]{:S(2)}, u32[]{:S(2)}) collective-permute-start(f32[2,1024,256]{2,1,0:T(8,128)S(1)} %collective-permute-done.12), channel_id=1, source_target_pairs={{1,2},{2,3},{5,6},{6,7},{9,10},{10,11},{13,14},{14,15},{17,18},{18... | collective-permute-start | bytes 6291464 | tf_op jit(solution)/shard_map/ppermute | solution.py:77
  107.2 52.1 %collective-permute-start.15 = (f32[2,1024,256]{2,1,0:T(8,128)S(1)}, f32[2,1024,256]{2,1,0:T(8,128)S(1)}, u32[]{:S(2)}, u32[]{:S(2)}) collective-permute-start(f32[2,1024,256]{2,1,0:T(8,128)S(1)} %collective-permute-done.13), channel_id=1, source_target_pairs={{1,0},{2,1},{5,4},{6,5},{9,8},{10,9},{13,12},{14,13},{17,16},{18,1... | collective-permute-start | bytes 6291464 | tf_op jit(solution)/shard_map/ppermute | solution.py:78
  151.8 46.4 %collective-permute-start.10 = (f32[2,1024,256]{2,1,0:T(8,128)}, f32[2,1024,256]{2,1,0:T(8,128)S(1)}, u32[]{:S(2)}, u32[]{:S(2)}) collective-permute-start(f32[2,1024,256]{2,1,0:T(8,128)} %get-tuple-element.31), channel_id=1, source_target_pairs={{2,1},{3,2},{6,5},{7,6},{10,9},{11,10},{14,13},{15,14},{18,17},{19... | collective-permute-start | bytes 6291464 | tf_op jit(solution)/shard_map/ppermute | solution.py:55
  155.9 42.3 %collective-permute-start.7 = (f32[2,1024,256]{2,1,0:T(8,128)}, f32[2,1024,256]{2,1,0:T(8,128)}, u32[]{:S(2)}, u32[]{:S(2)}) collective-permute-start(f32[2,1024,256]{2,1,0:T(8,128)} %get-tuple-element.32), channel_id=1, source_target_pairs={{0,1},{1,2},{4,5},{5,6},{8,9},{9,10},{12,13},{13,14},{16,17},{17,1... | collective-permute-start | bytes 6291464 | tf_op jit(solution)/shard_map/ppermute | solution.py:54
  158.0 54.2 %collective-permute-start.16 = (f32[2,1024,256]{2,1,0:T(8,128)S(1)}, f32[2,1024,256]{2,1,0:T(8,128)S(1)}, u32[]{:S(2)}, u32[]{:S(2)}) collective-permute-start(f32[2,1024,256]{2,1,0:T(8,128)S(1)} %collective-permute-done.14), channel_id=1, source_target_pairs={{2,3},{6,7},{10,11},{14,15},{18,19},{22,23},{26,27},{30,31}} | collective-permute-start | bytes 6291464 | tf_op jit(solution)/shard_map/ppermute | solution.py:77
  159.3 53.5 %collective-permute-start.17 = (f32[2,1024,256]{2,1,0:T(8,128)S(1)}, f32[2,1024,256]{2,1,0:T(8,128)S(1)}, u32[]{:S(2)}, u32[]{:S(2)}) collective-permute-start(f32[2,1024,256]{2,1,0:T(8,128)S(1)} %collective-permute-done.15), channel_id=1, source_target_pairs={{1,0},{5,4},{9,8},{13,12},{17,16},{21,20},{25,24},{29,28}} | collective-permute-start | bytes 6291464 | tf_op jit(solution)/shard_map/ppermute | solution.py:78
  202.7 50.4 %collective-permute-start.11 = (f32[2,1024,256]{2,1,0:T(8,128)}, f32[2,1024,256]{2,1,0:T(8,128)}, u32[]{:S(2)}, u32[]{:S(2)}) collective-permute-start(f32[2,1024,256]{2,1,0:T(8,128)} %get-tuple-element.29), channel_id=1, source_target_pairs={{1,0},{2,1},{3,2},{5,4},{6,5},{7,6},{9,8},{10,9},{11,10},{13,12},{... | collective-permute-start | bytes 6291464 | tf_op jit(solution)/shard_map/ppermute | solution.py:55
  211.0 45.3 %collective-permute-start.8 = (f32[2,1024,256]{2,1,0:T(8,128)}, f32[2,1024,256]{2,1,0:T(8,128)}, u32[]{:S(2)}, u32[]{:S(2)}) collective-permute-start(f32[2,1024,256]{2,1,0:T(8,128)} %get-tuple-element.30), channel_id=1, source_target_pairs={{0,1},{1,2},{2,3},{4,5},{5,6},{6,7},{8,9},{9,10},{10,11},{12,13},{... | collective-permute-start | bytes 6291464 | tf_op jit(solution)/shard_map/ppermute | solution.py:54
  245.0 14.4 %slice-start = ((s8[8388608]{0:T(1024)(128)(4,1)}), s8[4194304]{0:T(1024)(128)(4,1)S(1)}, s32[]{:S(2)}) async-start(s8[8388608]{0:T(1024)(128)(4,1)} %bitcast.102), calls=%async_computation | async-start | bytes 8388608
  261.8 1.1 collective-permute-start.18
  265.8 23.1 %collective-permute-start.19 = (f32[1024,256]{1,0:T(8,128)S(1)}, f32[1024,256]{1,0:T(8,128)S(1)}, u32[]{:S(2)}, u32[]{:S(2)}) collective-permute-start(f32[1024,256]{1,0:T(8,128)S(1)} %fusion.63), channel_id=1, source_target_pairs={{8,4},{9,5},{10,6},{11,7},{24,20},{25,21},{26,22},{27,23}} | collective-permute-start | bytes 3145736 | tf_op jit(solution)/shard_map/ppermute | solution.py:165
  292.3 9.0 %collective-permute-start.20 = (f32[1024,256]{1,0:T(8,128)}, f32[1024,256]{1,0:T(8,128)}, u32[]{:S(2)}, u32[]{:S(2)}) collective-permute-start(f32[1024,256]{1,0:T(8,128)} %fusion.61), channel_id=1, source_target_pairs={{4,0},{5,1},{6,2},{7,3},{20,16},{21,17},{22,18},{23,19}} | collective-permute-start | bytes 3145736 | tf_op jit(solution)/shard_map/ppermute | solution.py:165
  (14 other events, 60.0 us)

commit v8 on v6

--- a/solution.py
+++ b/solution.py
@@ -101,7 +101,7 @@
 
 def pick_rows_kernel(order_ref, field_ref, out_ref):
     blocks = field_ref.shape[0]
-    group = 8
+    group = 16
 
     def body(index, carry):
         start = pl.multiple_of(index * group, group)

time: 304 us -> 304 us (level)
  no operation moved by 1% of the time
where the time goes in v8:
time: 304 us; the launch traced here: 303 us
  waiting for transfers between devices  194 us (64%)
  starting transfers between devices  54.2 us (18%)
  matrix products  26 us (9%)
  other arithmetic  18.6 us (6%)
  Pallas kernels  5.02 us (2%)
  local copies, waits for them, and re-layouts  4.49 us (1%)
    ppermute x3, waiting for transfers between devices, line_reduce_scatter(): lax.ppermute(tile(me - count + step) + leftward, axis, left_route)  100 us
    ppermute x3, waiting for transfers between devices, line_all_to_all(): lax.ppermute(own_rows(me - distance), axis, [(k, k - distance) for k in r...  34.2 us
    ppermute x3, waiting for transfers between devices, line_all_to_all(): lax.ppermute(own_rows(me + distance), axis, [(k, k + distance) for k in r...  31.1 us
    dot_general x16, matrix products, bdot(): return jnp.dot(left, right, preferred_element_type=jnp.float32)  26 us
    ppermute x3, starting transfers between devices, line_reduce_scatter(): lax.ppermute(tile(me - count + step) + leftward, axis, left_route)  24.9 us
    ppermute x3, waiting for transfers between devices, shards(): entering = entering + lax.ppermute(leaving, 'tm', [(sender, sender - 1)])  24.3 us
    ppermute x3, starting transfers between devices, line_all_to_all(): lax.ppermute(own_rows(me - distance), axis, [(k, k - distance) for k in r...  7.66 us
    add x2, other arithmetic, line_reduce_scatter(): tile(me - count + step) + leftward  7.4 us
  transfers between devices with their start and end apart: 21, of which 11 were waited for; matrix products, arithmetic and copies ran while one was open for 10% of the time, Pallas kernels for 0%

profile of v8, /device:TPU:25, one launch (start us, length us, event | category | flops | bytes accessed | tf_op | source)
XLA Modules:
  0.0 302.9 jit_solution(4876953154778950380)
XLA Ops:
  3.3 4.0 %collective-permute-start.1 = (f32[2,256,256]{2,1,0:T(8,128)S(1)}, f32[2,256,256]{2,1,0:T(8,128)S(1)}, u32[]{:S(2)}, u32[]{:S(2)}) collective-permute-start(f32[2,256,256]{2,1,0:T(8,128)S(1)} %get-tuple-element.36), channel_id=1, source_target_pairs={{1,0},{2,1},{3,2},{5,4},{6,5},{7,6},{9,8},{10,9},{11,10},{13,12},{... | collective-permute-start | bytes 1572872 | tf_op jit(solution)/shard_map/ppermute | solution.py:96
  10.0 4.1 %collective-permute-start.13 = (f32[2,1024,256]{2,1,0:T(8,128)S(1)}, f32[2,1024,256]{2,1,0:T(8,128)S(1)}, u32[]{:S(2)}, u32[]{:S(2)}) collective-permute-start(f32[2,1024,256]{2,1,0:T(8,128)S(1)} %copy-done.2), channel_id=1, source_target_pairs={{1,0},{2,1},{3,2},{5,4},{6,5},{7,6},{9,8},{10,9},{11,10},{13,12},{... | collective-permute-start | bytes 6291464 | tf_op jit(solution)/shard_map/ppermute | solution.py:78
  14.1 2.6 collective-permute-done
  16.7 2.3 collective-permute-start.3
  20.7 18.5 %collective-permute-done.2 = f32[2,256,256]{2,1,0:T(8,128)S(1)} collective-permute-done((f32[2,256,256]{2,1,0:T(8,128)S(1)}, f32[2,256,256]{2,1,0:T(8,128)S(1)}, u32[]{:S(2)}, u32[]{:S(2)}) %collective-permute-start.2) | collective-permute-done | bytes 524320 | tf_op jit(solution)/shard_map/ppermute | solution.py:95
  40.6 33.2 %collective-permute-done.3 = f32[2,256,256]{2,1,0:T(8,128)S(1)} collective-permute-done((f32[2,256,256]{2,1,0:T(8,128)S(1)}, f32[2,256,256]{2,1,0:T(8,128)S(1)}, u32[]{:S(2)}, u32[]{:S(2)}) %collective-permute-start.3) | collective-permute-done | bytes 524320 | tf_op jit(solution)/shard_map/ppermute | solution.py:96
  74.0 10.0 %collective-permute-done.4 = f32[2,256,256]{2,1,0:T(8,128)S(1)} collective-permute-done((f32[2,256,256]{2,1,0:T(8,128)S(1)}, f32[2,256,256]{2,1,0:T(8,128)S(1)}, u32[]{:S(2)}, u32[]{:S(2)}) %collective-permute-start.4) | collective-permute-done | bytes 524320 | tf_op jit(solution)/shard_map/ppermute | solution.py:95
  92.1 13.7 %collective-permute-start.9 = (f32[2,1024,256]{2,1,0:T(8,128)S(1)}, f32[2,1024,256]{2,1,0:T(8,128)S(1)}, u32[]{:S(2)}, u32[]{:S(2)}) collective-permute-start(f32[2,1024,256]{2,1,0:T(8,128)S(1)} %get-tuple-element.21), channel_id=1, source_target_pairs={{3,2},{7,6},{11,10},{15,14},{19,18},{23,22},{27,26},{31,30}} | collective-permute-start | bytes 6291464 | tf_op jit(solution)/shard_map/ppermute | solution.py:55
  107.9 40.8 %collective-permute-done.9 = f32[2,1024,256]{2,1,0:T(8,128)S(1)} collective-permute-done((f32[2,1024,256]{2,1,0:T(8,128)S(1)}, f32[2,1024,256]{2,1,0:T(8,128)S(1)}, u32[]{:S(2)}, u32[]{:S(2)}) %collective-permute-start.9) | collective-permute-done | bytes 2097184 | tf_op jit(solution)/shard_map/ppermute | solution.py:55
  148.7 2.9 fusion.31
  151.6 4.1 %collective-permute-start.10 = (f32[2,1024,256]{2,1,0:T(8,128)}, f32[2,1024,256]{2,1,0:T(8,128)S(1)}, u32[]{:S(2)}, u32[]{:S(2)}) collective-permute-start(f32[2,1024,256]{2,1,0:T(8,128)} %get-tuple-element.19), channel_id=1, source_target_pairs={{2,1},{3,2},{6,5},{7,6},{10,9},{11,10},{14,13},{15,14},{18,17},{19... | collective-permute-start | bytes 6291464 | tf_op jit(solution)/shard_map/ppermute | solution.py:55
  155.8 2.1 collective-permute-start.7
  164.3 33.8 %collective-permute-done.10 = f32[2,1024,256]{2,1,0:T(8,128)S(1)} collective-permute-done((f32[2,1024,256]{2,1,0:T(8,128)}, f32[2,1024,256]{2,1,0:T(8,128)S(1)}, u32[]{:S(2)}, u32[]{:S(2)}) %collective-permute-start.10) | collective-permute-done | bytes 2097184 | tf_op jit(solution)/shard_map/ppermute | solution.py:55
  198.1 4.5 %fusion.29 = (f32[2,1024,256]{2,1,0:T(8,128)}, f32[2,1024,256]{2,1,0:T(8,128)}) fusion(f32[2,1024,256]{2,1,0:T(8,128)S(1)} %collective-permute-done.10, s32[]{:T(128)S(6)} %select_n.15, f32[1,1024,1024]{2,1,0:T(8,128)S(1)} %fusion.10, f32[1,1024,1024]{2,1,0:T(8,128)S(1)} %fusion.8, f32[2,1024,256]{2,1,0:T(8,128)} %collective-permute-done.7, s32[]{:T(128)S(6)} %select_n.16), kind=kLoop, calls=%fused_computation.54 | loop fusion | flops 2097152 | bytes 16777224 | tf_op jit(solution)/shard_map/add | solution.py:55
  202.5 7.1 %collective-permute-start.11 = (f32[2,1024,256]{2,1,0:T(8,128)}, f32[2,1024,256]{2,1,0:T(8,128)S(1)}, u32[]{:S(2)}, u32[]{:S(2)}) collective-permute-start(f32[2,1024,256]{2,1,0:T(8,128)} %get-tuple-element.17), channel_id=1, source_target_pairs={{1,0},{2,1},{3,2},{5,4},{6,5},{7,6},{9,8},{10,9},{11,10},{13,12},{... | collective-permute-start | bytes 6291464 | tf_op jit(solution)/shard_map/ppermute | solution.py:55
  213.2 7.0 %fusion.11 = f32[1024,2048]{1,0:T(8,128)} fusion(bf16[1024,1024]{1,0:T(8,128)(2,1)S(1)} %get-tuple-element.16, bf16[1024,1024]{1,0:T(8,128)(2,1)S(1)} %get-tuple-element.15, f32[2,1024,1024]{2,1,0:T(8,128)S(1)} %add_dynamic-update-slice_fusion), kind=kOutput, calls=%fused_computation.36 | convolution fusion | flops 4305453056 | bytes 16777216 | tf_op jit(solution)/shard_map/dot_general | solution.py:29
  220.1 5.0 %fusion.5 = (bf16[1024,1024]{1,0:T(8,128)(2,1)S(1)}, bf16[1024,1024]{1,0:T(8,128)(2,1)S(1)}) fusion(f32[2,1024,1024]{2,1,0:T(8,128)S(1)} %add_dynamic-update-slice_fusion, f32[1024,2048]{1,0:T(8,128)} %fusion.11), kind=kOutput, calls=%fused_computation.27 | convolution fusion | flops 2161115136 | bytes 20971520 | tf_op jit(solution)/shard_map/dot_general | solution.py:29
  225.1 25.9 %collective-permute-done.11 = f32[2,1024,256]{2,1,0:T(8,128)S(1)} collective-permute-done((f32[2,1024,256]{2,1,0:T(8,128)}, f32[2,1024,256]{2,1,0:T(8,128)S(1)}, u32[]{:S(2)}, u32[]{:S(2)}) %collective-permute-start.11) | collective-permute-done | bytes 2097184 | tf_op jit(solution)/shard_map/ppermute | solution.py:55
  251.0 4.0 %collective-permute-done.8 = f32[2,1024,256]{2,1,0:T(8,128)} collective-permute-done((f32[2,1024,256]{2,1,0:T(8,128)}, f32[2,1024,256]{2,1,0:T(8,128)}, u32[]{:S(2)}, u32[]{:S(2)}) %collective-permute-start.8) | collective-permute-done | bytes 2097184 | tf_op jit(solution)/shard_map/ppermute | solution.py:54
  255.0 2.4 fusion.22
  264.0 22.1 %collective-permute-done.19 = f32[1024,256]{1,0:T(8,128)S(1)} collective-permute-done((f32[1024,256]{1,0:T(8,128)S(1)}, f32[1024,256]{1,0:T(8,128)S(1)}, u32[]{:S(2)}, u32[]{:S(2)}) %collective-permute-start.19) | collective-permute-done | bytes 1048608 | tf_op jit(solution)/shard_map/ppermute | solution.py:160
  289.8 2.2 collective-permute-done.20
  296.4 1.5 pad_maximum_fusion.field_ref
  297.9 5.0 %shard_map.46 = f32[2,1024,256]{2,1,0:T(8,128)} custom-call(s32[1024]{0:T(1024)} %order_ref.1, f32[2,1024,256]{2,1,0:T(8,128)} %pad_maximum_fusion.field_ref), custom_call_target="tpu_custom_call" | custom-call | bytes 4194304 | tf_op jit(solution)/shard_map/pallas_call | solution.py:118
  (71 shorter events, 43.5 us)
Async XLA Ops:
  1.6 7.1 %copy-start.2 = (f32[2,1024,256]{2,1,0:T(8,128)S(1)}, f32[2,1024,256]{2,1,0:T(8,128)}, u32[]{:S(2)}) copy-start(f32[2,1024,256]{2,1,0:T(8,128)} %param.6) | copy-start | bytes 6291460
  1.9 14.8 %collective-permute-start = (f32[2,256,256]{2,1,0:T(8,128)S(1)}, f32[2,256,256]{2,1,0:T(8,128)S(1)}, u32[]{:S(2)}, u32[]{:S(2)}) collective-permute-start(f32[2,256,256]{2,1,0:T(8,128)S(1)} %get-tuple-element.37), channel_id=1, source_target_pairs={{0,1},{1,2},{2,3},{4,5},{5,6},{6,7},{8,9},{9,10},{10,11},{12,13},{... | collective-permute-start | bytes 1572872 | tf_op jit(solution)/shard_map/ppermute | solution.py:95
  3.3 15.9 %collective-permute-start.1 = (f32[2,256,256]{2,1,0:T(8,128)S(1)}, f32[2,256,256]{2,1,0:T(8,128)S(1)}, u32[]{:S(2)}, u32[]{:S(2)}) collective-permute-start(f32[2,256,256]{2,1,0:T(8,128)S(1)} %get-tuple-element.36), channel_id=1, source_target_pairs={{1,0},{2,1},{3,2},{5,4},{6,5},{7,6},{9,8},{10,9},{11,10},{13,12},{... | collective-permute-start | bytes 1572872 | tf_op jit(solution)/shard_map/ppermute | solution.py:96
  7.4 31.7 %collective-permute-start.2 = (f32[2,256,256]{2,1,0:T(8,128)S(1)}, f32[2,256,256]{2,1,0:T(8,128)S(1)}, u32[]{:S(2)}, u32[]{:S(2)}) collective-permute-start(f32[2,256,256]{2,1,0:T(8,128)S(1)} %get-tuple-element.35), channel_id=1, source_target_pairs={{0,2},{1,3},{4,6},{5,7},{8,10},{9,11},{12,14},{13,15},{16,18},{17,... | collective-permute-start | bytes 1572872 | tf_op jit(solution)/shard_map/ppermute | solution.py:95
  8.7 97.1 %collective-permute-start.12 = (f32[2,1024,256]{2,1,0:T(8,128)S(1)}, f32[2,1024,256]{2,1,0:T(8,128)S(1)}, u32[]{:S(2)}, u32[]{:S(2)}) collective-permute-start(f32[2,1024,256]{2,1,0:T(8,128)S(1)} %copy-done.2), channel_id=1, source_target_pairs={{0,1},{1,2},{2,3},{4,5},{5,6},{6,7},{8,9},{9,10},{10,11},{12,13},{... | collective-permute-start | bytes 6291464 | tf_op jit(solution)/shard_map/ppermute | solution.py:77
  10.0 97.1 %collective-permute-start.13 = (f32[2,1024,256]{2,1,0:T(8,128)S(1)}, f32[2,1024,256]{2,1,0:T(8,128)S(1)}, u32[]{:S(2)}, u32[]{:S(2)}) collective-permute-start(f32[2,1024,256]{2,1,0:T(8,128)S(1)} %copy-done.2), channel_id=1, source_target_pairs={{1,0},{2,1},{3,2},{5,4},{6,5},{7,6},{9,8},{10,9},{11,10},{13,12},{... | collective-permute-start | bytes 6291464 | tf_op jit(solution)/shard_map/ppermute | solution.py:78
  16.7 57.1 %collective-permute-start.3 = (f32[2,256,256]{2,1,0:T(8,128)S(1)}, f32[2,256,256]{2,1,0:T(8,128)S(1)}, u32[]{:S(2)}, u32[]{:S(2)}) collective-permute-start(f32[2,256,256]{2,1,0:T(8,128)S(1)} %get-tuple-element.34), channel_id=1, source_target_pairs={{2,0},{3,1},{6,4},{7,5},{10,8},{11,9},{14,12},{15,13},{18,16},{19,... | collective-permute-start | bytes 1572872 | tf_op jit(solution)/shard_map/ppermute | solution.py:96
  19.2 64.8 %collective-permute-start.4 = (f32[2,256,256]{2,1,0:T(8,128)S(1)}, f32[2,256,256]{2,1,0:T(8,128)S(1)}, u32[]{:S(2)}, u32[]{:S(2)}) collective-permute-start(f32[2,256,256]{2,1,0:T(8,128)S(1)} %get-tuple-element.39), channel_id=1, source_target_pairs={{0,3},{4,7},{8,11},{12,15},{16,19},{20,23},{24,27},{28,31}} | collective-permute-start | bytes 1572872 | tf_op jit(solution)/shard_map/ppermute | solution.py:95
  39.1 45.9 %collective-permute-start.5 = (f32[2,256,256]{2,1,0:T(8,128)S(1)}, f32[2,256,256]{2,1,0:T(8,128)S(1)}, u32[]{:S(2)}, u32[]{:S(2)}) collective-permute-start(f32[2,256,256]{2,1,0:T(8,128)S(1)} %get-tuple-element.33), channel_id=1, source_target_pairs={{3,0},{7,4},{11,8},{15,12},{19,16},{23,20},{27,24},{31,28}} | collective-permute-start | bytes 1572872 | tf_op jit(solution)/shard_map/ppermute | solution.py:96
  85.2 1.6 copy-start
  91.3 16.6 %collective-permute-start.6 = (f32[2,1024,256]{2,1,0:T(8,128)S(1)}, f32[2,1024,256]{2,1,0:T(8,128)S(1)}, u32[]{:S(2)}, u32[]{:S(2)}) collective-permute-start(f32[2,1024,256]{2,1,0:T(8,128)S(1)} %get-tuple-element.22), channel_id=1, source_target_pairs={{0,1},{4,5},{8,9},{12,13},{16,17},{20,21},{24,25},{28,29}} | collective-permute-start | bytes 6291464 | tf_op jit(solution)/shard_map/ppermute | solution.py:54
  92.1 56.6 %collective-permute-start.9 = (f32[2,1024,256]{2,1,0:T(8,128)S(1)}, f32[2,1024,256]{2,1,0:T(8,128)S(1)}, u32[]{:S(2)}, u32[]{:S(2)}) collective-permute-start(f32[2,1024,256]{2,1,0:T(8,128)S(1)} %get-tuple-element.21), channel_id=1, source_target_pairs={{3,2},{7,6},{11,10},{15,14},{19,18},{23,22},{27,26},{31,30}} | collective-permute-start | bytes 6291464 | tf_op jit(solution)/shard_map/ppermute | solution.py:55
  105.8 52.1 %collective-permute-start.14 = (f32[2,1024,256]{2,1,0:T(8,128)S(1)}, f32[2,1024,256]{2,1,0:T(8,128)S(1)}, u32[]{:S(2)}, u32[]{:S(2)}) collective-permute-start(f32[2,1024,256]{2,1,0:T(8,128)S(1)} %collective-permute-done.12), channel_id=1, source_target_pairs={{1,2},{2,3},{5,6},{6,7},{9,10},{10,11},{13,14},{14,15},{17,18},{18... | collective-permute-start | bytes 6291464 | tf_op jit(solution)/shard_map/ppermute | solution.py:77
  107.1 52.1 %collective-permute-start.15 = (f32[2,1024,256]{2,1,0:T(8,128)S(1)}, f32[2,1024,256]{2,1,0:T(8,128)S(1)}, u32[]{:S(2)}, u32[]{:S(2)}) collective-permute-start(f32[2,1024,256]{2,1,0:T(8,128)S(1)} %collective-permute-done.13), channel_id=1, source_target_pairs={{1,0},{2,1},{5,4},{6,5},{9,8},{10,9},{13,12},{14,13},{17,16},{18,1... | collective-permute-start | bytes 6291464 | tf_op jit(solution)/shard_map/ppermute | solution.py:78
  151.6 46.4 %collective-permute-start.10 = (f32[2,1024,256]{2,1,0:T(8,128)}, f32[2,1024,256]{2,1,0:T(8,128)S(1)}, u32[]{:S(2)}, u32[]{:S(2)}) collective-permute-start(f32[2,1024,256]{2,1,0:T(8,128)} %get-tuple-element.19), channel_id=1, source_target_pairs={{2,1},{3,2},{6,5},{7,6},{10,9},{11,10},{14,13},{15,14},{18,17},{19... | collective-permute-start | bytes 6291464 | tf_op jit(solution)/shard_map/ppermute | solution.py:55
  155.8 5.5 %copy-start.3 = (f32[2,1024,256]{2,1,0:T(8,128)S(1)}, f32[2,1024,256]{2,1,0:T(8,128)}, u32[]{:S(2)}) copy-start(f32[2,1024,256]{2,1,0:T(8,128)} %param.6) | copy-start | bytes 6291460
  155.8 42.3 %collective-permute-start.7 = (f32[2,1024,256]{2,1,0:T(8,128)}, f32[2,1024,256]{2,1,0:T(8,128)}, u32[]{:S(2)}, u32[]{:S(2)}) collective-permute-start(f32[2,1024,256]{2,1,0:T(8,128)} %get-tuple-element.20), channel_id=1, source_target_pairs={{0,1},{1,2},{4,5},{5,6},{8,9},{9,10},{12,13},{13,14},{16,17},{17,1... | collective-permute-start | bytes 6291464 | tf_op jit(solution)/shard_map/ppermute | solution.py:54
  157.9 53.1 %collective-permute-start.16 = (f32[2,1024,256]{2,1,0:T(8,128)S(1)}, f32[2,1024,256]{2,1,0:T(8,128)S(1)}, u32[]{:S(2)}, u32[]{:S(2)}) collective-permute-start(f32[2,1024,256]{2,1,0:T(8,128)S(1)} %collective-permute-done.14), channel_id=1, source_target_pairs={{2,3},{6,7},{10,11},{14,15},{18,19},{22,23},{26,27},{30,31}} | collective-permute-start | bytes 6291464 | tf_op jit(solution)/shard_map/ppermute | solution.py:77
  159.2 52.3 %collective-permute-start.17 = (f32[2,1024,256]{2,1,0:T(8,128)S(1)}, f32[2,1024,256]{2,1,0:T(8,128)S(1)}, u32[]{:S(2)}, u32[]{:S(2)}) collective-permute-start(f32[2,1024,256]{2,1,0:T(8,128)S(1)} %collective-permute-done.15), channel_id=1, source_target_pairs={{1,0},{5,4},{9,8},{13,12},{17,16},{21,20},{25,24},{29,28}} | collective-permute-start | bytes 6291464 | tf_op jit(solution)/shard_map/ppermute | solution.py:78
  202.5 48.5 %collective-permute-start.11 = (f32[2,1024,256]{2,1,0:T(8,128)}, f32[2,1024,256]{2,1,0:T(8,128)S(1)}, u32[]{:S(2)}, u32[]{:S(2)}) collective-permute-start(f32[2,1024,256]{2,1,0:T(8,128)} %get-tuple-element.17), channel_id=1, source_target_pairs={{1,0},{2,1},{3,2},{5,4},{6,5},{7,6},{9,8},{10,9},{11,10},{13,12},{... | collective-permute-start | bytes 6291464 | tf_op jit(solution)/shard_map/ppermute | solution.py:55
  209.7 45.3 %collective-permute-start.8 = (f32[2,1024,256]{2,1,0:T(8,128)}, f32[2,1024,256]{2,1,0:T(8,128)}, u32[]{:S(2)}, u32[]{:S(2)}) collective-permute-start(f32[2,1024,256]{2,1,0:T(8,128)} %get-tuple-element.18), channel_id=1, source_target_pairs={{0,1},{1,2},{2,3},{4,5},{5,6},{6,7},{8,9},{9,10},{10,11},{12,13},{... | collective-permute-start | bytes 6291464 | tf_op jit(solution)/shard_map/ppermute | solution.py:54
  259.6 1.0 collective-permute-start.18
  262.7 23.4 %collective-permute-start.19 = (f32[1024,256]{1,0:T(8,128)S(1)}, f32[1024,256]{1,0:T(8,128)S(1)}, u32[]{:S(2)}, u32[]{:S(2)}) collective-permute-start(f32[1024,256]{1,0:T(8,128)S(1)} %fusion.59), channel_id=1, source_target_pairs={{8,4},{9,5},{10,6},{11,7},{24,20},{25,21},{26,22},{27,23}} | collective-permute-start | bytes 3145736 | tf_op jit(solution)/shard_map/ppermute | solution.py:160
  288.4 3.6 %collective-permute-start.20 = (f32[1024,256]{1,0:T(8,128)S(1)}, f32[1024,256]{1,0:T(8,128)S(1)}, u32[]{:S(2)}, u32[]{:S(2)}) collective-permute-start(f32[1024,256]{1,0:T(8,128)S(1)} %fusion.57), channel_id=1, source_target_pairs={{4,0},{5,1},{6,2},{7,3},{20,16},{21,17},{22,18},{23,19}} | collective-permute-start | bytes 3145736 | tf_op jit(solution)/shard_map/ppermute | solution.py:160
  (1 other events, 1.6 us)

commit v9 on v6

--- a/solution.py
+++ b/solution.py
@@ -91,7 +91,7 @@
 
     shape = (value.shape[0], rows, count * value.shape[2])
     whole = add_at(jnp.zeros(shape, value.dtype), own_rows(me), me, 2)
-    for distance in range(1, count):
+    for distance in range(count - 1, 0, -1):
         right = lax.ppermute(own_rows(me + distance), axis, [(k, k + distance) for k in range(0, count - distance)])
         left = lax.ppermute(own_rows(me - distance), axis, [(k, k - distance) for k in range(distance, count)])
         whole = add_at(whole, right, me - distance, 2)

time: 304 us -> 311 us (1.023)
  starting transfers between devices: 54.2 us -> 58.1 us
    ppermute x3, waiting for transfers between devices: 100 us -> 105 us  [line_reduce_scatter(): lax.ppermute(tile(me - count + step) + leftward, axis, left_route)]
  transfers between devices with their start and end apart: 21 -> 21, of which waited for: 11 -> 10; matrix products, arithmetic and copies ran while one was open for 10% -> 10% of each run, Pallas kernels for 0% -> 0%
where the time goes in v9:
time: 311 us; the launch traced here: 310 us
  waiting for transfers between devices  197 us (63%)
  starting transfers between devices  58.1 us (19%)
  matrix products  26 us (8%)
  other arithmetic  18.6 us (6%)
  Pallas kernels  5.24 us (2%)
  local copies, waits for them, and re-layouts  4.49 us (1%)
    ppermute x3, waiting for transfers between devices, line_reduce_scatter(): lax.ppermute(tile(me - count + step) + leftward, axis, left_route)  105 us
    ppermute x3, waiting for transfers between devices, line_all_to_all(): lax.ppermute(own_rows(me + distance), axis, [(k, k + distance) for k in r...  33.5 us
    ppermute x3, waiting for transfers between devices, line_all_to_all(): lax.ppermute(own_rows(me - distance), axis, [(k, k - distance) for k in r...  32.1 us
    ppermute x3, starting transfers between devices, line_reduce_scatter(): lax.ppermute(tile(me - count + step) + leftward, axis, left_route)  27.1 us
    dot_general x16, matrix products, bdot(): return jnp.dot(left, right, preferred_element_type=jnp.float32)  26 us
    ppermute x3, waiting for transfers between devices, shards(): entering = entering + lax.ppermute(leaving, 'tm', [(sender, sender - 1)])  23.1 us
    ppermute x3, starting transfers between devices, line_all_to_all(): lax.ppermute(own_rows(me - distance), axis, [(k, k - distance) for k in r...  9.43 us
    add x2, other arithmetic, line_reduce_scatter(): tile(me - count + step) + leftward  7.4 us
  transfers between devices with their start and end apart: 21, of which 10 were waited for; matrix products, arithmetic and copies ran while one was open for 10% of the time, Pallas kernels for 0%

profile of v9, /device:TPU:25, one launch (start us, length us, event | category | flops | bytes accessed | tf_op | source)
XLA Modules:
  0.0 310.3 jit_solution(14248892854581621052)
XLA Ops:
  3.3 5.8 %collective-permute-start.1 = (f32[2,256,256]{2,1,0:T(8,128)S(1)}, f32[2,256,256]{2,1,0:T(8,128)S(1)}, u32[]{:S(2)}, u32[]{:S(2)}) collective-permute-start(f32[2,256,256]{2,1,0:T(8,128)S(1)} %get-tuple-element.36), channel_id=1, source_target_pairs={{3,0},{7,4},{11,8},{15,12},{19,16},{23,20},{27,24},{31,28}} | collective-permute-start | bytes 1572872 | tf_op jit(solution)/shard_map/ppermute | solution.py:96
  11.8 4.1 %collective-permute-start.13 = (f32[2,1024,256]{2,1,0:T(8,128)S(1)}, f32[2,1024,256]{2,1,0:T(8,128)S(1)}, u32[]{:S(2)}, u32[]{:S(2)}) collective-permute-start(f32[2,1024,256]{2,1,0:T(8,128)S(1)} %copy-done.2), channel_id=1, source_target_pairs={{1,0},{2,1},{3,2},{5,4},{6,5},{7,6},{9,8},{10,9},{11,10},{13,12},{... | collective-permute-start | bytes 6291464 | tf_op jit(solution)/shard_map/ppermute | solution.py:78
  15.9 2.7 collective-permute-done
  18.6 2.3 collective-permute-start.3
  22.5 19.7 %collective-permute-done.2 = f32[2,256,256]{2,1,0:T(8,128)S(1)} collective-permute-done((f32[2,256,256]{2,1,0:T(8,128)S(1)}, f32[2,256,256]{2,1,0:T(8,128)S(1)}, u32[]{:S(2)}, u32[]{:S(2)}) %collective-permute-start.2) | collective-permute-done | bytes 524320 | tf_op jit(solution)/shard_map/ppermute | solution.py:95
  43.6 32.1 %collective-permute-done.3 = f32[2,256,256]{2,1,0:T(8,128)S(1)} collective-permute-done((f32[2,256,256]{2,1,0:T(8,128)S(1)}, f32[2,256,256]{2,1,0:T(8,128)S(1)}, u32[]{:S(2)}, u32[]{:S(2)}) %collective-permute-start.3) | collective-permute-done | bytes 524320 | tf_op jit(solution)/shard_map/ppermute | solution.py:96
  75.8 11.2 %collective-permute-done.4 = f32[2,256,256]{2,1,0:T(8,128)S(1)} collective-permute-done((f32[2,256,256]{2,1,0:T(8,128)S(1)}, f32[2,256,256]{2,1,0:T(8,128)S(1)}, u32[]{:S(2)}, u32[]{:S(2)}) %collective-permute-start.4) | collective-permute-done | bytes 524320 | tf_op jit(solution)/shard_map/ppermute | solution.py:95
  94.2 15.5 %collective-permute-start.9 = (f32[2,1024,256]{2,1,0:T(8,128)S(1)}, f32[2,1024,256]{2,1,0:T(8,128)S(1)}, u32[]{:S(2)}, u32[]{:S(2)}) collective-permute-start(f32[2,1024,256]{2,1,0:T(8,128)S(1)} %get-tuple-element.21), channel_id=1, source_target_pairs={{3,2},{7,6},{11,10},{15,14},{19,18},{23,22},{27,26},{31,30}} | collective-permute-start | bytes 6291464 | tf_op jit(solution)/shard_map/ppermute | solution.py:55
  111.8 42.2 %collective-permute-done.9 = f32[2,1024,256]{2,1,0:T(8,128)S(1)} collective-permute-done((f32[2,1024,256]{2,1,0:T(8,128)S(1)}, f32[2,1024,256]{2,1,0:T(8,128)S(1)}, u32[]{:S(2)}, u32[]{:S(2)}) %collective-permute-start.9) | collective-permute-done | bytes 2097184 | tf_op jit(solution)/shard_map/ppermute | solution.py:55
  154.1 2.9 fusion.31
  157.0 4.1 %collective-permute-start.10 = (f32[2,1024,256]{2,1,0:T(8,128)}, f32[2,1024,256]{2,1,0:T(8,128)S(1)}, u32[]{:S(2)}, u32[]{:S(2)}) collective-permute-start(f32[2,1024,256]{2,1,0:T(8,128)} %get-tuple-element.19), channel_id=1, source_target_pairs={{2,1},{3,2},{6,5},{7,6},{10,9},{11,10},{14,13},{15,14},{18,17},{19... | collective-permute-start | bytes 6291464 | tf_op jit(solution)/shard_map/ppermute | solution.py:55
  161.1 2.1 collective-permute-start.7
  169.6 35.2 %collective-permute-done.10 = f32[2,1024,256]{2,1,0:T(8,128)S(1)} collective-permute-done((f32[2,1024,256]{2,1,0:T(8,128)}, f32[2,1024,256]{2,1,0:T(8,128)S(1)}, u32[]{:S(2)}, u32[]{:S(2)}) %collective-permute-start.10) | collective-permute-done | bytes 2097184 | tf_op jit(solution)/shard_map/ppermute | solution.py:55
  204.9 4.5 %fusion.29 = (f32[2,1024,256]{2,1,0:T(8,128)}, f32[2,1024,256]{2,1,0:T(8,128)}) fusion(f32[2,1024,256]{2,1,0:T(8,128)S(1)} %collective-permute-done.10, s32[]{:T(128)S(6)} %select_n.19, f32[1,1024,1024]{2,1,0:T(8,128)S(1)} %fusion.10, f32[1,1024,1024]{2,1,0:T(8,128)S(1)} %fusion.8, f32[2,1024,256]{2,1,0:T(8,128)} %collective-permute-done.7, s32[]{:T(128)S(6)} %select_n.20), kind=kLoop, calls=%fused_computation.54 | loop fusion | flops 2097152 | bytes 16777224 | tf_op jit(solution)/shard_map/add | solution.py:55
  209.4 7.5 %collective-permute-start.11 = (f32[2,1024,256]{2,1,0:T(8,128)}, f32[2,1024,256]{2,1,0:T(8,128)S(1)}, u32[]{:S(2)}, u32[]{:S(2)}) collective-permute-start(f32[2,1024,256]{2,1,0:T(8,128)} %get-tuple-element.17), channel_id=1, source_target_pairs={{1,0},{2,1},{3,2},{5,4},{6,5},{7,6},{9,8},{10,9},{11,10},{13,12},{... | collective-permute-start | bytes 6291464 | tf_op jit(solution)/shard_map/ppermute | solution.py:55
  220.3 7.0 %fusion.11 = f32[1024,2048]{1,0:T(8,128)} fusion(bf16[1024,1024]{1,0:T(8,128)(2,1)S(1)} %get-tuple-element.16, bf16[1024,1024]{1,0:T(8,128)(2,1)S(1)} %get-tuple-element.15, f32[2,1024,1024]{2,1,0:T(8,128)S(1)} %add_dynamic-update-slice_fusion), kind=kOutput, calls=%fused_computation.36 | convolution fusion | flops 4305453056 | bytes 16777216 | tf_op jit(solution)/shard_map/dot_general | solution.py:29
  227.3 5.0 %fusion.5 = (bf16[1024,1024]{1,0:T(8,128)(2,1)S(1)}, bf16[1024,1024]{1,0:T(8,128)(2,1)S(1)}) fusion(f32[2,1024,1024]{2,1,0:T(8,128)S(1)} %add_dynamic-update-slice_fusion, f32[1024,2048]{1,0:T(8,128)} %fusion.11), kind=kOutput, calls=%fused_computation.27 | convolution fusion | flops 2161115136 | bytes 20971520 | tf_op jit(solution)/shard_map/dot_general | solution.py:29
  232.3 27.1 %collective-permute-done.11 = f32[2,1024,256]{2,1,0:T(8,128)S(1)} collective-permute-done((f32[2,1024,256]{2,1,0:T(8,128)}, f32[2,1024,256]{2,1,0:T(8,128)S(1)}, u32[]{:S(2)}, u32[]{:S(2)}) %collective-permute-start.11) | collective-permute-done | bytes 2097184 | tf_op jit(solution)/shard_map/ppermute | solution.py:55
  259.4 4.0 %collective-permute-done.8 = f32[2,1024,256]{2,1,0:T(8,128)} collective-permute-done((f32[2,1024,256]{2,1,0:T(8,128)}, f32[2,1024,256]{2,1,0:T(8,128)}, u32[]{:S(2)}, u32[]{:S(2)}) %collective-permute-start.8) | collective-permute-done | bytes 2097184 | tf_op jit(solution)/shard_map/ppermute | solution.py:54
  263.3 2.4 fusion.22
  272.4 20.9 %collective-permute-done.19 = f32[1024,256]{1,0:T(8,128)S(1)} collective-permute-done((f32[1024,256]{1,0:T(8,128)S(1)}, f32[1024,256]{1,0:T(8,128)S(1)}, u32[]{:S(2)}, u32[]{:S(2)}) %collective-permute-start.19) | collective-permute-done | bytes 1048608 | tf_op jit(solution)/shard_map/ppermute | solution.py:160
  297.0 2.2 collective-permute-done.20
  303.6 1.5 pad_maximum_fusion.field_ref
  305.0 5.2 %shard_map.46 = f32[2,1024,256]{2,1,0:T(8,128)} custom-call(s32[1024]{0:T(1024)} %order_ref.1, f32[2,1024,256]{2,1,0:T(8,128)} %pad_maximum_fusion.field_ref), custom_call_target="tpu_custom_call" | custom-call | bytes 4194304 | tf_op jit(solution)/shard_map/pallas_call | solution.py:118
  (71 shorter events, 42.6 us)
Async XLA Ops:
  1.6 8.9 %copy-start.2 = (f32[2,1024,256]{2,1,0:T(8,128)S(1)}, f32[2,1024,256]{2,1,0:T(8,128)}, u32[]{:S(2)}) copy-start(f32[2,1024,256]{2,1,0:T(8,128)} %param.6) | copy-start | bytes 6291460
  1.9 16.7 %collective-permute-start = (f32[2,256,256]{2,1,0:T(8,128)S(1)}, f32[2,256,256]{2,1,0:T(8,128)S(1)}, u32[]{:S(2)}, u32[]{:S(2)}) collective-permute-start(f32[2,256,256]{2,1,0:T(8,128)S(1)} %get-tuple-element.37), channel_id=1, source_target_pairs={{0,3},{4,7},{8,11},{12,15},{16,19},{20,23},{24,27},{28,31}} | collective-permute-start | bytes 1572872 | tf_op jit(solution)/shard_map/ppermute | solution.py:95
  3.3 17.7 %collective-permute-start.1 = (f32[2,256,256]{2,1,0:T(8,128)S(1)}, f32[2,256,256]{2,1,0:T(8,128)S(1)}, u32[]{:S(2)}, u32[]{:S(2)}) collective-permute-start(f32[2,256,256]{2,1,0:T(8,128)S(1)} %get-tuple-element.36), channel_id=1, source_target_pairs={{3,0},{7,4},{11,8},{15,12},{19,16},{23,20},{27,24},{31,28}} | collective-permute-start | bytes 1572872 | tf_op jit(solution)/shard_map/ppermute | solution.py:96
  9.2 32.9 %collective-permute-start.2 = (f32[2,256,256]{2,1,0:T(8,128)S(1)}, f32[2,256,256]{2,1,0:T(8,128)S(1)}, u32[]{:S(2)}, u32[]{:S(2)}) collective-permute-start(f32[2,256,256]{2,1,0:T(8,128)S(1)} %get-tuple-element.35), channel_id=1, source_target_pairs={{0,2},{1,3},{4,6},{5,7},{8,10},{9,11},{12,14},{13,15},{16,18},{17,... | collective-permute-start | bytes 1572872 | tf_op jit(solution)/shard_map/ppermute | solution.py:95
  10.5 99.2 %collective-permute-start.12 = (f32[2,1024,256]{2,1,0:T(8,128)S(1)}, f32[2,1024,256]{2,1,0:T(8,128)S(1)}, u32[]{:S(2)}, u32[]{:S(2)}) collective-permute-start(f32[2,1024,256]{2,1,0:T(8,128)S(1)} %copy-done.2), channel_id=1, source_target_pairs={{0,1},{1,2},{2,3},{4,5},{5,6},{6,7},{8,9},{9,10},{10,11},{12,13},{... | collective-permute-start | bytes 6291464 | tf_op jit(solution)/shard_map/ppermute | solution.py:77
  11.8 99.2 %collective-permute-start.13 = (f32[2,1024,256]{2,1,0:T(8,128)S(1)}, f32[2,1024,256]{2,1,0:T(8,128)S(1)}, u32[]{:S(2)}, u32[]{:S(2)}) collective-permute-start(f32[2,1024,256]{2,1,0:T(8,128)S(1)} %copy-done.2), channel_id=1, source_target_pairs={{1,0},{2,1},{3,2},{5,4},{6,5},{7,6},{9,8},{10,9},{11,10},{13,12},{... | collective-permute-start | bytes 6291464 | tf_op jit(solution)/shard_map/ppermute | solution.py:78
  18.6 57.1 %collective-permute-start.3 = (f32[2,256,256]{2,1,0:T(8,128)S(1)}, f32[2,256,256]{2,1,0:T(8,128)S(1)}, u32[]{:S(2)}, u32[]{:S(2)}) collective-permute-start(f32[2,256,256]{2,1,0:T(8,128)S(1)} %get-tuple-element.34), channel_id=1, source_target_pairs={{2,0},{3,1},{6,4},{7,5},{10,8},{11,9},{14,12},{15,13},{18,16},{19,... | collective-permute-start | bytes 1572872 | tf_op jit(solution)/shard_map/ppermute | solution.py:96
  21.0 66.0 %collective-permute-start.4 = (f32[2,256,256]{2,1,0:T(8,128)S(1)}, f32[2,256,256]{2,1,0:T(8,128)S(1)}, u32[]{:S(2)}, u32[]{:S(2)}) collective-permute-start(f32[2,256,256]{2,1,0:T(8,128)S(1)} %get-tuple-element.39), channel_id=1, source_target_pairs={{0,1},{1,2},{2,3},{4,5},{5,6},{6,7},{8,9},{9,10},{10,11},{12,13},{... | collective-permute-start | bytes 1572872 | tf_op jit(solution)/shard_map/ppermute | solution.py:95
  42.1 45.0 %collective-permute-start.5 = (f32[2,256,256]{2,1,0:T(8,128)S(1)}, f32[2,256,256]{2,1,0:T(8,128)S(1)}, u32[]{:S(2)}, u32[]{:S(2)}) collective-permute-start(f32[2,256,256]{2,1,0:T(8,128)S(1)} %get-tuple-element.33), channel_id=1, source_target_pairs={{1,0},{2,1},{3,2},{5,4},{6,5},{7,6},{9,8},{10,9},{11,10},{13,12},{... | collective-permute-start | bytes 1572872 | tf_op jit(solution)/shard_map/ppermute | solution.py:96
  87.3 1.6 copy-start
  93.4 18.5 %collective-permute-start.6 = (f32[2,1024,256]{2,1,0:T(8,128)S(1)}, f32[2,1024,256]{2,1,0:T(8,128)S(1)}, u32[]{:S(2)}, u32[]{:S(2)}) collective-permute-start(f32[2,1024,256]{2,1,0:T(8,128)S(1)} %get-tuple-element.22), channel_id=1, source_target_pairs={{0,1},{4,5},{8,9},{12,13},{16,17},{20,21},{24,25},{28,29}} | collective-permute-start | bytes 6291464 | tf_op jit(solution)/shard_map/ppermute | solution.py:54
  94.2 59.9 %collective-permute-start.9 = (f32[2,1024,256]{2,1,0:T(8,128)S(1)}, f32[2,1024,256]{2,1,0:T(8,128)S(1)}, u32[]{:S(2)}, u32[]{:S(2)}) collective-permute-start(f32[2,1024,256]{2,1,0:T(8,128)S(1)} %get-tuple-element.21), channel_id=1, source_target_pairs={{3,2},{7,6},{11,10},{15,14},{19,18},{23,22},{27,26},{31,30}} | collective-permute-start | bytes 6291464 | tf_op jit(solution)/shard_map/ppermute | solution.py:55
  109.7 53.6 %collective-permute-start.14 = (f32[2,1024,256]{2,1,0:T(8,128)S(1)}, f32[2,1024,256]{2,1,0:T(8,128)S(1)}, u32[]{:S(2)}, u32[]{:S(2)}) collective-permute-start(f32[2,1024,256]{2,1,0:T(8,128)S(1)} %collective-permute-done.12), channel_id=1, source_target_pairs={{1,2},{2,3},{5,6},{6,7},{9,10},{10,11},{13,14},{14,15},{17,18},{18... | collective-permute-start | bytes 6291464 | tf_op jit(solution)/shard_map/ppermute | solution.py:77
  111.0 53.5 %collective-permute-start.15 = (f32[2,1024,256]{2,1,0:T(8,128)S(1)}, f32[2,1024,256]{2,1,0:T(8,128)S(1)}, u32[]{:S(2)}, u32[]{:S(2)}) collective-permute-start(f32[2,1024,256]{2,1,0:T(8,128)S(1)} %collective-permute-done.13), channel_id=1, source_target_pairs={{1,0},{2,1},{5,4},{6,5},{9,8},{10,9},{13,12},{14,13},{17,16},{18,1... | collective-permute-start | bytes 6291464 | tf_op jit(solution)/shard_map/ppermute | solution.py:78
  157.0 47.9 %collective-permute-start.10 = (f32[2,1024,256]{2,1,0:T(8,128)}, f32[2,1024,256]{2,1,0:T(8,128)S(1)}, u32[]{:S(2)}, u32[]{:S(2)}) collective-permute-start(f32[2,1024,256]{2,1,0:T(8,128)} %get-tuple-element.19), channel_id=1, source_target_pairs={{2,1},{3,2},{6,5},{7,6},{10,9},{11,10},{14,13},{15,14},{18,17},{19... | collective-permute-start | bytes 6291464 | tf_op jit(solution)/shard_map/ppermute | solution.py:55
  161.1 5.5 %copy-start.3 = (f32[2,1024,256]{2,1,0:T(8,128)S(1)}, f32[2,1024,256]{2,1,0:T(8,128)}, u32[]{:S(2)}) copy-start(f32[2,1024,256]{2,1,0:T(8,128)} %param.6) | copy-start | bytes 6291460
  161.1 43.7 %collective-permute-start.7 = (f32[2,1024,256]{2,1,0:T(8,128)}, f32[2,1024,256]{2,1,0:T(8,128)}, u32[]{:S(2)}, u32[]{:S(2)}) collective-permute-start(f32[2,1024,256]{2,1,0:T(8,128)} %get-tuple-element.20), channel_id=1, source_target_pairs={{0,1},{1,2},{4,5},{5,6},{8,9},{9,10},{12,13},{13,14},{16,17},{17,1... | collective-permute-start | bytes 6291464 | tf_op jit(solution)/shard_map/ppermute | solution.py:54
  163.3 54.8 %collective-permute-start.16 = (f32[2,1024,256]{2,1,0:T(8,128)S(1)}, f32[2,1024,256]{2,1,0:T(8,128)S(1)}, u32[]{:S(2)}, u32[]{:S(2)}) collective-permute-start(f32[2,1024,256]{2,1,0:T(8,128)S(1)} %collective-permute-done.14), channel_id=1, source_target_pairs={{2,3},{6,7},{10,11},{14,15},{18,19},{22,23},{26,27},{30,31}} | collective-permute-start | bytes 6291464 | tf_op jit(solution)/shard_map/ppermute | solution.py:77
  164.6 54.1 %collective-permute-start.17 = (f32[2,1024,256]{2,1,0:T(8,128)S(1)}, f32[2,1024,256]{2,1,0:T(8,128)S(1)}, u32[]{:S(2)}, u32[]{:S(2)}) collective-permute-start(f32[2,1024,256]{2,1,0:T(8,128)S(1)} %collective-permute-done.15), channel_id=1, source_target_pairs={{1,0},{5,4},{9,8},{13,12},{17,16},{21,20},{25,24},{29,28}} | collective-permute-start | bytes 6291464 | tf_op jit(solution)/shard_map/ppermute | solution.py:78
  209.4 50.0 %collective-permute-start.11 = (f32[2,1024,256]{2,1,0:T(8,128)}, f32[2,1024,256]{2,1,0:T(8,128)S(1)}, u32[]{:S(2)}, u32[]{:S(2)}) collective-permute-start(f32[2,1024,256]{2,1,0:T(8,128)} %get-tuple-element.17), channel_id=1, source_target_pairs={{1,0},{2,1},{3,2},{5,4},{6,5},{7,6},{9,8},{10,9},{11,10},{13,12},{... | collective-permute-start | bytes 6291464 | tf_op jit(solution)/shard_map/ppermute | solution.py:55
  216.8 46.5 %collective-permute-start.8 = (f32[2,1024,256]{2,1,0:T(8,128)}, f32[2,1024,256]{2,1,0:T(8,128)}, u32[]{:S(2)}, u32[]{:S(2)}) collective-permute-start(f32[2,1024,256]{2,1,0:T(8,128)} %get-tuple-element.18), channel_id=1, source_target_pairs={{0,1},{1,2},{2,3},{4,5},{5,6},{6,7},{8,9},{9,10},{10,11},{12,13},{... | collective-permute-start | bytes 6291464 | tf_op jit(solution)/shard_map/ppermute | solution.py:54
  267.9 1.0 collective-permute-start.18
  271.1 22.2 %collective-permute-start.19 = (f32[1024,256]{1,0:T(8,128)S(1)}, f32[1024,256]{1,0:T(8,128)S(1)}, u32[]{:S(2)}, u32[]{:S(2)}) collective-permute-start(f32[1024,256]{1,0:T(8,128)S(1)} %fusion.59), channel_id=1, source_target_pairs={{8,4},{9,5},{10,6},{11,7},{24,20},{25,21},{26,22},{27,23}} | collective-permute-start | bytes 3145736 | tf_op jit(solution)/shard_map/ppermute | solution.py:160
  295.6 3.6 %collective-permute-start.20 = (f32[1024,256]{1,0:T(8,128)S(1)}, f32[1024,256]{1,0:T(8,128)S(1)}, u32[]{:S(2)}, u32[]{:S(2)}) collective-permute-start(f32[1024,256]{1,0:T(8,128)S(1)} %fusion.57), channel_id=1, source_target_pairs={{4,0},{5,1},{6,2},{7,3},{20,16},{21,17},{22,18},{23,19}} | collective-permute-start | bytes 3145736 | tf_op jit(solution)/shard_map/ppermute | solution.py:160
  (1 other events, 1.6 us)

commit v10 on v6

--- a/solution.py
+++ b/solution.py
@@ -48,11 +48,14 @@
 
     rightward = jnp.zeros_like(tile(me))
     leftward = jnp.zeros_like(tile(me))
+    going_right = [tile(me + count - step) for step in range(1, count)]
+    going_left = [tile(me - count + step) for step in range(1, count)]
+    going_right, going_left = lax.optimization_barrier((going_right, going_left))
     for step in range(1, count):
         right_route = [(k, k + 1) for k in range(0, min(step, count - 1))]
         left_route = [(k, k - 1) for k in range(max(count - step, 1), count)]
-        rightward = lax.ppermute(tile(me + count - step) + rightward, axis, right_route)
-        leftward = lax.ppermute(tile(me - count + step) + leftward, axis, left_route)
+        rightward = lax.ppermute(going_right[step - 1] + rightward, axis, right_route)
+        leftward = lax.ppermute(going_left[step - 1] + leftward, axis, left_route)
     if ready is not None:
         rightward, leftward, ready = lax.optimization_barrier((rightward, leftward, ready))
     return tile(me) + (rightward + leftward), ready

time: 304 us -> 302 us (level); the launches traced: 303 us -> 296 us
  waiting for transfers between devices: 194 us -> 186 us
    ppermute x6, waiting for transfers between devices: 104 us -> 97.4 us  [the longest x3 71.1 us: line_reduce_scatter(): leftward = lax.ppermute(going_left[step - 1] + leftward, axis, left_route)]
    add x2 -> x4, other arithmetic: 7.4 us -> 4.12 us  [the longest x2 3.45 us: line_reduce_scatter(): leftward = lax.ppermute(going_left[step - 1] + leftward, axis, left_route)]
  transfers between devices with their start and end apart: 21 -> 21, of which waited for: 11 -> 10; matrix products, arithmetic and copies ran while one was open for 10% -> 11% of each run, Pallas kernels for 0% -> 0%
where the time goes in v10:
time: 302 us; the launch traced here: 296 us
  waiting for transfers between devices  186 us (62%)
  starting transfers between devices  53.8 us (18%)
  matrix products  27 us (9%)
  other arithmetic  17.1 us (6%)
  local copies, waits for them, and re-layouts  6.36 us (2%)
  Pallas kernels  5.24 us (2%)
    ppermute x3, waiting for transfers between devices, line_reduce_scatter(): leftward = lax.ppermute(going_left[step - 1] + leftward, axis, left_route)  71.1 us
    ppermute x3, waiting for transfers between devices, line_all_to_all(): lax.ppermute(own_rows(me - distance), axis, [(k, k - distance) for k in r...  34.1 us
    ppermute x3, waiting for transfers between devices, line_all_to_all(): lax.ppermute(own_rows(me + distance), axis, [(k, k + distance) for k in r...  31.1 us
    dot_general x16, matrix products, bdot(): return jnp.dot(left, right, preferred_element_type=jnp.float32)  27 us
    ppermute x3, waiting for transfers between devices, line_reduce_scatter(): lax.ppermute(going_right[step - 1] + rightward, axis, right_route)  26.3 us
    ppermute x3, starting transfers between devices, line_reduce_scatter(): leftward = lax.ppermute(going_left[step - 1] + leftward, axis, left_route)  25.8 us
    ppermute x3, waiting for transfers between devices, shards(): entering = entering + lax.ppermute(leaving, 'tm', [(sender, sender - 1)])  23 us
    ppermute x3, starting transfers between devices, line_all_to_all(): lax.ppermute(own_rows(me - distance), axis, [(k, k - distance) for k in r...  7.67 us
  transfers between devices with their start and end apart: 21, of which 10 were waited for; matrix products, arithmetic and copies ran while one was open for 11% of the time, Pallas kernels for 0%

profile of v10, /device:TPU:25, one launch (start us, length us, event | category | flops | bytes accessed | tf_op | source)
XLA Modules:
  0.0 295.8 jit_solution(7464440535784998895)
XLA Ops:
  3.3 4.0 %collective-permute-start.1 = (f32[2,256,256]{2,1,0:T(8,128)S(1)}, f32[2,256,256]{2,1,0:T(8,128)S(1)}, u32[]{:S(2)}, u32[]{:S(2)}) collective-permute-start(f32[2,256,256]{2,1,0:T(8,128)S(1)} %get-tuple-element.48), channel_id=1, source_target_pairs={{1,0},{2,1},{3,2},{5,4},{6,5},{7,6},{9,8},{10,9},{11,10},{13,12},{... | collective-permute-start | bytes 1572872 | tf_op jit(solution)/shard_map/ppermute | solution.py:99
  10.0 4.1 %collective-permute-start.13 = (f32[2,1024,256]{2,1,0:T(8,128)S(1)}, f32[2,1024,256]{2,1,0:T(8,128)S(1)}, u32[]{:S(2)}, u32[]{:S(2)}) collective-permute-start(f32[2,1024,256]{2,1,0:T(8,128)S(1)} %copy-done.2), channel_id=1, source_target_pairs={{1,0},{2,1},{3,2},{5,4},{6,5},{7,6},{9,8},{10,9},{11,10},{13,12},{... | collective-permute-start | bytes 6291464 | tf_op jit(solution)/shard_map/ppermute | solution.py:81
  14.1 2.6 collective-permute-done
  16.7 2.3 collective-permute-start.3
  20.7 18.5 %collective-permute-done.2 = f32[2,256,256]{2,1,0:T(8,128)S(1)} collective-permute-done((f32[2,256,256]{2,1,0:T(8,128)S(1)}, f32[2,256,256]{2,1,0:T(8,128)S(1)}, u32[]{:S(2)}, u32[]{:S(2)}) %collective-permute-start.2) | collective-permute-done | bytes 524320 | tf_op jit(solution)/shard_map/ppermute | solution.py:98
  40.6 33.2 %collective-permute-done.3 = f32[2,256,256]{2,1,0:T(8,128)S(1)} collective-permute-done((f32[2,256,256]{2,1,0:T(8,128)S(1)}, f32[2,256,256]{2,1,0:T(8,128)S(1)}, u32[]{:S(2)}, u32[]{:S(2)}) %collective-permute-start.3) | collective-permute-done | bytes 524320 | tf_op jit(solution)/shard_map/ppermute | solution.py:99
  74.0 10.0 %collective-permute-done.4 = f32[2,256,256]{2,1,0:T(8,128)S(1)} collective-permute-done((f32[2,256,256]{2,1,0:T(8,128)S(1)}, f32[2,256,256]{2,1,0:T(8,128)S(1)}, u32[]{:S(2)}, u32[]{:S(2)}) %collective-permute-start.4) | collective-permute-done | bytes 524320 | tf_op jit(solution)/shard_map/ppermute | solution.py:98
  90.9 1.6 fusion.20
  93.3 13.7 %collective-permute-start.9 = (f32[2,1024,256]{2,1,0:T(8,128)S(1)}, f32[2,1024,256]{2,1,0:T(8,128)S(1)}, u32[]{:S(2)}, u32[]{:S(2)}) collective-permute-start(f32[2,1024,256]{2,1,0:T(8,128)S(1)} %get-tuple-element.20), channel_id=1, source_target_pairs={{3,2},{7,6},{11,10},{15,14},{19,18},{23,22},{27,26},{31,30}} | collective-permute-start | bytes 6291464 | tf_op jit(solution)/shard_map/ppermute | solution.py:58
  110.3 39.6 %collective-permute-done.9 = f32[2,1024,256]{2,1,0:T(8,128)S(1)} collective-permute-done((f32[2,1024,256]{2,1,0:T(8,128)S(1)}, f32[2,1024,256]{2,1,0:T(8,128)S(1)}, u32[]{:S(2)}, u32[]{:S(2)}) %collective-permute-start.9) | collective-permute-done | bytes 2097184 | tf_op jit(solution)/shard_map/ppermute | solution.py:58
  149.9 1.6 add.239
  151.5 5.5 %collective-permute-start.10 = (f32[2,1024,256]{2,1,0:T(8,128)}, f32[2,1024,256]{2,1,0:T(8,128)}, u32[]{:S(2)}, u32[]{:S(2)}) collective-permute-start(f32[2,1024,256]{2,1,0:T(8,128)} %add.239), channel_id=1, source_target_pairs={{2,1},{3,2},{6,5},{7,6},{10,9},{11,10},{14,13},{15,14},{18,17},{19... | collective-permute-start | bytes 6291464 | tf_op jit(solution)/shard_map/ppermute | solution.py:58
  160.3 1.9 constant_dynamic-update-slice_fusion
  166.5 31.6 %collective-permute-done.10 = f32[2,1024,256]{2,1,0:T(8,128)} collective-permute-done((f32[2,1024,256]{2,1,0:T(8,128)}, f32[2,1024,256]{2,1,0:T(8,128)}, u32[]{:S(2)}, u32[]{:S(2)}) %collective-permute-start.10) | collective-permute-done | bytes 2097184 | tf_op jit(solution)/shard_map/ppermute | solution.py:58
  198.0 1.9 add.240
  199.9 6.6 %collective-permute-start.11 = (f32[2,1024,256]{2,1,0:T(8,128)S(1)}, f32[2,1024,256]{2,1,0:T(8,128)}, u32[]{:S(2)}, u32[]{:S(2)}) collective-permute-start(f32[2,1024,256]{2,1,0:T(8,128)S(1)} %add.240), channel_id=1, source_target_pairs={{1,0},{2,1},{3,2},{5,4},{6,5},{7,6},{9,8},{10,9},{11,10},{13,12},{... | collective-permute-start | bytes 6291464 | tf_op jit(solution)/shard_map/ppermute | solution.py:58
  208.7 7.0 %fusion.11 = f32[1024,2048]{1,0:T(8,128)} fusion(bf16[1024,1024]{1,0:T(8,128)(2,1)S(1)} %get-tuple-element.28, bf16[1024,1024]{1,0:T(8,128)(2,1)S(1)} %get-tuple-element.27, f32[2,1024,1024]{2,1,0:T(8,128)S(1)} %add_dynamic-update-slice_fusion), kind=kOutput, calls=%fused_computation.36 | convolution fusion | flops 4305453056 | bytes 16777216 | tf_op jit(solution)/shard_map/dot_general | solution.py:29
  215.7 5.9 %fusion.5 = (bf16[1024,1024]{1,0:T(8,128)(2,1)S(1)}, bf16[1024,1024]{1,0:T(8,128)(2,1)}) fusion(f32[2,1024,1024]{2,1,0:T(8,128)S(1)} %add_dynamic-update-slice_fusion, f32[1024,2048]{1,0:T(8,128)} %fusion.11), kind=kOutput, calls=%fused_computation.27 | convolution fusion | flops 2161115136 | bytes 20971520 | tf_op jit(solution)/shard_map/dot_general | solution.py:29
  221.7 26.3 %collective-permute-done.8 = f32[2,1024,256]{2,1,0:T(8,128)} collective-permute-done((f32[2,1024,256]{2,1,0:T(8,128)S(1)}, f32[2,1024,256]{2,1,0:T(8,128)}, u32[]{:S(2)}, u32[]{:S(2)}) %collective-permute-start.8) | collective-permute-done | bytes 2097184 | tf_op jit(solution)/shard_map/ppermute | solution.py:57
  247.9 3.0 %fusion.22 = f32[2,1024,256]{2,1,0:T(8,128)S(1)} fusion(s32[]{:T(128)S(6)} %select_n.14, f32[1,1024,1024]{2,1,0:T(8,128)S(1)} %fusion.10, f32[1,1024,1024]{2,1,0:T(8,128)S(1)} %fusion.8, f32[2,1024,256]{2,1,0:T(8,128)} %collective-permute-done.8, f32[2,1024,256]{2,1,0:T(8,128)} %collective-permute-done.11), kind=kLoop, calls=%fused_computation.47 | loop fusion | flops 1572864 | bytes 14680068 | tf_op jit(solution)/shard_map/add | solution.py:61
  258.1 20.8 %collective-permute-done.19 = f32[1024,256]{1,0:T(8,128)S(1)} collective-permute-done((f32[1024,256]{1,0:T(8,128)S(1)}, f32[1024,256]{1,0:T(8,128)S(1)}, u32[]{:S(2)}, u32[]{:S(2)}) %collective-permute-start.19) | collective-permute-done | bytes 1048608 | tf_op jit(solution)/shard_map/ppermute | solution.py:163
  282.6 2.2 collective-permute-done.20
  289.1 1.5 pad_maximum_fusion.field_ref
  290.5 5.2 %shard_map.46 = f32[2,1024,256]{2,1,0:T(8,128)} custom-call(s32[1024]{0:T(1024)} %order_ref.1, f32[2,1024,256]{2,1,0:T(8,128)} %pad_maximum_fusion.field_ref), custom_call_target="tpu_custom_call" | custom-call | bytes 4194304 | tf_op jit(solution)/shard_map/pallas_call | solution.py:121
  (73 shorter events, 44.6 us)
Async XLA Ops:
  1.6 7.1 %copy-start.2 = (f32[2,1024,256]{2,1,0:T(8,128)S(1)}, f32[2,1024,256]{2,1,0:T(8,128)}, u32[]{:S(2)}) copy-start(f32[2,1024,256]{2,1,0:T(8,128)} %param.6) | copy-start | bytes 6291460
  1.9 14.8 %collective-permute-start = (f32[2,256,256]{2,1,0:T(8,128)S(1)}, f32[2,256,256]{2,1,0:T(8,128)S(1)}, u32[]{:S(2)}, u32[]{:S(2)}) collective-permute-start(f32[2,256,256]{2,1,0:T(8,128)S(1)} %get-tuple-element.49), channel_id=1, source_target_pairs={{0,1},{1,2},{2,3},{4,5},{5,6},{6,7},{8,9},{9,10},{10,11},{12,13},{... | collective-permute-start | bytes 1572872 | tf_op jit(solution)/shard_map/ppermute | solution.py:98
  3.3 15.9 %collective-permute-start.1 = (f32[2,256,256]{2,1,0:T(8,128)S(1)}, f32[2,256,256]{2,1,0:T(8,128)S(1)}, u32[]{:S(2)}, u32[]{:S(2)}) collective-permute-start(f32[2,256,256]{2,1,0:T(8,128)S(1)} %get-tuple-element.48), channel_id=1, source_target_pairs={{1,0},{2,1},{3,2},{5,4},{6,5},{7,6},{9,8},{10,9},{11,10},{13,12},{... | collective-permute-start | bytes 1572872 | tf_op jit(solution)/shard_map/ppermute | solution.py:99
  7.4 31.8 %collective-permute-start.2 = (f32[2,256,256]{2,1,0:T(8,128)S(1)}, f32[2,256,256]{2,1,0:T(8,128)S(1)}, u32[]{:S(2)}, u32[]{:S(2)}) collective-permute-start(f32[2,256,256]{2,1,0:T(8,128)S(1)} %get-tuple-element.47), channel_id=1, source_target_pairs={{0,2},{1,3},{4,6},{5,7},{8,10},{9,11},{12,14},{13,15},{16,18},{17,... | collective-permute-start | bytes 1572872 | tf_op jit(solution)/shard_map/ppermute | solution.py:98
  8.7 98.3 %collective-permute-start.12 = (f32[2,1024,256]{2,1,0:T(8,128)S(1)}, f32[2,1024,256]{2,1,0:T(8,128)S(1)}, u32[]{:S(2)}, u32[]{:S(2)}) collective-permute-start(f32[2,1024,256]{2,1,0:T(8,128)S(1)} %copy-done.2), channel_id=1, source_target_pairs={{0,1},{1,2},{2,3},{4,5},{5,6},{6,7},{8,9},{9,10},{10,11},{12,13},{... | collective-permute-start | bytes 6291464 | tf_op jit(solution)/shard_map/ppermute | solution.py:80
  10.0 98.3 %collective-permute-start.13 = (f32[2,1024,256]{2,1,0:T(8,128)S(1)}, f32[2,1024,256]{2,1,0:T(8,128)S(1)}, u32[]{:S(2)}, u32[]{:S(2)}) collective-permute-start(f32[2,1024,256]{2,1,0:T(8,128)S(1)} %copy-done.2), channel_id=1, source_target_pairs={{1,0},{2,1},{3,2},{5,4},{6,5},{7,6},{9,8},{10,9},{11,10},{13,12},{... | collective-permute-start | bytes 6291464 | tf_op jit(solution)/shard_map/ppermute | solution.py:81
  16.7 57.1 %collective-permute-start.3 = (f32[2,256,256]{2,1,0:T(8,128)S(1)}, f32[2,256,256]{2,1,0:T(8,128)S(1)}, u32[]{:S(2)}, u32[]{:S(2)}) collective-permute-start(f32[2,256,256]{2,1,0:T(8,128)S(1)} %get-tuple-element.46), channel_id=1, source_target_pairs={{2,0},{3,1},{6,4},{7,5},{10,8},{11,9},{14,12},{15,13},{18,16},{19,... | collective-permute-start | bytes 1572872 | tf_op jit(solution)/shard_map/ppermute | solution.py:99
  19.2 64.8 %collective-permute-start.4 = (f32[2,256,256]{2,1,0:T(8,128)S(1)}, f32[2,256,256]{2,1,0:T(8,128)S(1)}, u32[]{:S(2)}, u32[]{:S(2)}) collective-permute-start(f32[2,256,256]{2,1,0:T(8,128)S(1)} %get-tuple-element.51), channel_id=1, source_target_pairs={{0,3},{4,7},{8,11},{12,15},{16,19},{20,23},{24,27},{28,31}} | collective-permute-start | bytes 1572872 | tf_op jit(solution)/shard_map/ppermute | solution.py:98
  39.1 45.9 %collective-permute-start.5 = (f32[2,256,256]{2,1,0:T(8,128)S(1)}, f32[2,256,256]{2,1,0:T(8,128)S(1)}, u32[]{:S(2)}, u32[]{:S(2)}) collective-permute-start(f32[2,256,256]{2,1,0:T(8,128)S(1)} %get-tuple-element.45), channel_id=1, source_target_pairs={{3,0},{7,4},{11,8},{15,12},{19,16},{23,20},{27,24},{31,28}} | collective-permute-start | bytes 1572872 | tf_op jit(solution)/shard_map/ppermute | solution.py:99
  85.2 1.6 copy-start
  92.5 16.6 %collective-permute-start.6 = (f32[2,1024,256]{2,1,0:T(8,128)S(1)}, f32[2,1024,256]{2,1,0:T(8,128)S(1)}, u32[]{:S(2)}, u32[]{:S(2)}) collective-permute-start(f32[2,1024,256]{2,1,0:T(8,128)S(1)} %get-tuple-element.17), channel_id=1, source_target_pairs={{0,1},{4,5},{8,9},{12,13},{16,17},{20,21},{24,25},{28,29}} | collective-permute-start | bytes 6291464 | tf_op jit(solution)/shard_map/ppermute | solution.py:57
  93.3 56.6 %collective-permute-start.9 = (f32[2,1024,256]{2,1,0:T(8,128)S(1)}, f32[2,1024,256]{2,1,0:T(8,128)S(1)}, u32[]{:S(2)}, u32[]{:S(2)}) collective-permute-start(f32[2,1024,256]{2,1,0:T(8,128)S(1)} %get-tuple-element.20), channel_id=1, source_target_pairs={{3,2},{7,6},{11,10},{15,14},{19,18},{23,22},{27,26},{31,30}} | collective-permute-start | bytes 6291464 | tf_op jit(solution)/shard_map/ppermute | solution.py:58
  107.0 49.9 %collective-permute-start.14 = (f32[2,1024,256]{2,1,0:T(8,128)S(1)}, f32[2,1024,256]{2,1,0:T(8,128)S(1)}, u32[]{:S(2)}, u32[]{:S(2)}) collective-permute-start(f32[2,1024,256]{2,1,0:T(8,128)S(1)} %collective-permute-done.12), channel_id=1, source_target_pairs={{1,2},{2,3},{5,6},{6,7},{9,10},{10,11},{13,14},{14,15},{17,18},{18... | collective-permute-start | bytes 6291464 | tf_op jit(solution)/shard_map/ppermute | solution.py:80
  108.3 49.9 %collective-permute-start.15 = (f32[2,1024,256]{2,1,0:T(8,128)S(1)}, f32[2,1024,256]{2,1,0:T(8,128)S(1)}, u32[]{:S(2)}, u32[]{:S(2)}) collective-permute-start(f32[2,1024,256]{2,1,0:T(8,128)S(1)} %collective-permute-done.13), channel_id=1, source_target_pairs={{1,0},{2,1},{5,4},{6,5},{9,8},{10,9},{13,12},{14,13},{17,16},{18,1... | collective-permute-start | bytes 6291464 | tf_op jit(solution)/shard_map/ppermute | solution.py:81
  109.5 55.4 %collective-permute-start.7 = (f32[2,1024,256]{2,1,0:T(8,128)S(1)}, f32[2,1024,256]{2,1,0:T(8,128)S(1)}, u32[]{:S(2)}, u32[]{:S(2)}) collective-permute-start(f32[2,1024,256]{2,1,0:T(8,128)S(1)} %add.237), channel_id=1, source_target_pairs={{0,1},{1,2},{4,5},{5,6},{8,9},{9,10},{12,13},{13,14},{16,17},{17,1... | collective-permute-start | bytes 6291464 | tf_op jit(solution)/shard_map/ppermute | solution.py:57
  151.5 46.5 %collective-permute-start.10 = (f32[2,1024,256]{2,1,0:T(8,128)}, f32[2,1024,256]{2,1,0:T(8,128)}, u32[]{:S(2)}, u32[]{:S(2)}) collective-permute-start(f32[2,1024,256]{2,1,0:T(8,128)} %add.239), channel_id=1, source_target_pairs={{2,1},{3,2},{6,5},{7,6},{10,9},{11,10},{14,13},{15,14},{18,17},{19... | collective-permute-start | bytes 6291464 | tf_op jit(solution)/shard_map/ppermute | solution.py:58
  157.0 49.6 %collective-permute-start.16 = (f32[2,1024,256]{2,1,0:T(8,128)S(1)}, f32[2,1024,256]{2,1,0:T(8,128)S(1)}, u32[]{:S(2)}, u32[]{:S(2)}) collective-permute-start(f32[2,1024,256]{2,1,0:T(8,128)S(1)} %collective-permute-done.14), channel_id=1, source_target_pairs={{2,3},{6,7},{10,11},{14,15},{18,19},{22,23},{26,27},{30,31}} | collective-permute-start | bytes 6291464 | tf_op jit(solution)/shard_map/ppermute | solution.py:80
  158.3 48.9 %collective-permute-start.17 = (f32[2,1024,256]{2,1,0:T(8,128)S(1)}, f32[2,1024,256]{2,1,0:T(8,128)S(1)}, u32[]{:S(2)}, u32[]{:S(2)}) collective-permute-start(f32[2,1024,256]{2,1,0:T(8,128)S(1)} %collective-permute-done.15), channel_id=1, source_target_pairs={{1,0},{5,4},{9,8},{13,12},{17,16},{21,20},{25,24},{29,28}} | collective-permute-start | bytes 6291464 | tf_op jit(solution)/shard_map/ppermute | solution.py:81
  165.2 82.8 %collective-permute-start.8 = (f32[2,1024,256]{2,1,0:T(8,128)S(1)}, f32[2,1024,256]{2,1,0:T(8,128)}, u32[]{:S(2)}, u32[]{:S(2)}) collective-permute-start(f32[2,1024,256]{2,1,0:T(8,128)S(1)} %add.238), channel_id=1, source_target_pairs={{0,1},{1,2},{2,3},{4,5},{5,6},{6,7},{8,9},{9,10},{10,11},{12,13},{... | collective-permute-start | bytes 6291464 | tf_op jit(solution)/shard_map/ppermute | solution.py:57
  199.9 48.0 %collective-permute-start.11 = (f32[2,1024,256]{2,1,0:T(8,128)S(1)}, f32[2,1024,256]{2,1,0:T(8,128)}, u32[]{:S(2)}, u32[]{:S(2)}) collective-permute-start(f32[2,1024,256]{2,1,0:T(8,128)S(1)} %add.240), channel_id=1, source_target_pairs={{1,0},{2,1},{3,2},{5,4},{6,5},{7,6},{9,8},{10,9},{11,10},{13,12},{... | collective-permute-start | bytes 6291464 | tf_op jit(solution)/shard_map/ppermute | solution.py:58
  253.2 1.6 copy-start.3
  253.2 1.1 collective-permute-start.18
  256.8 22.1 %collective-permute-start.19 = (f32[1024,256]{1,0:T(8,128)S(1)}, f32[1024,256]{1,0:T(8,128)S(1)}, u32[]{:S(2)}, u32[]{:S(2)}) collective-permute-start(f32[1024,256]{1,0:T(8,128)S(1)} %fusion.55), channel_id=1, source_target_pairs={{8,4},{9,5},{10,6},{11,7},{24,20},{25,21},{26,22},{27,23}} | collective-permute-start | bytes 3145736 | tf_op jit(solution)/shard_map/ppermute | solution.py:163
  281.2 3.6 %collective-permute-start.20 = (f32[1024,256]{1,0:T(8,128)S(1)}, f32[1024,256]{1,0:T(8,128)S(1)}, u32[]{:S(2)}, u32[]{:S(2)}) collective-permute-start(f32[1024,256]{1,0:T(8,128)S(1)} %fusion.53), channel_id=1, source_target_pairs={{4,0},{5,1},{6,2},{7,3},{20,16},{21,17},{22,18},{23,19}} | collective-permute-start | bytes 3145736 | tf_op jit(solution)/shard_map/ppermute | solution.py:163
  (1 other events, 1.6 us)

commit v11 on v10

--- a/solution.py
+++ b/solution.py
@@ -50,7 +50,8 @@
     leftward = jnp.zeros_like(tile(me))
     going_right = [tile(me + count - step) for step in range(1, count)]
     going_left = [tile(me - count + step) for step in range(1, count)]
-    going_right, going_left = lax.optimization_barrier((going_right, going_left))
+    own_tile = tile(me)
+    going_right, going_left, own_tile = lax.optimization_barrier((going_right, going_left, own_tile))
     for step in range(1, count):
         right_route = [(k, k + 1) for k in range(0, min(step, count - 1))]
         left_route = [(k, k - 1) for k in range(max(count - step, 1), count)]
@@ -58,7 +59,7 @@
         leftward = lax.ppermute(going_left[step - 1] + leftward, axis, left_route)
     if ready is not None:
         rightward, leftward, ready = lax.optimization_barrier((rightward, leftward, ready))
-    return tile(me) + (rightward + leftward), ready
+    return own_tile + (rightward + leftward), ready
 
 
 def add_at(whole, piece, slot, axis):

time: 302 us -> 297 us (0.983)
  other arithmetic: 17.1 us -> 12 us
  waiting for transfers between devices: 186 us -> 191 us
    ppermute x3, waiting for transfers between devices: 26.3 us -> 29.7 us  [line_reduce_scatter(): lax.ppermute(going_right[step - 1] + rightward, axis, right_route)]
  transfers between devices with their start and end apart: 21 -> 21, of which waited for: 10 -> 10; matrix products, arithmetic and copies ran while one was open for 11% -> 9% of each run, Pallas kernels for 0% -> 0%
where the time goes in v11:
time: 297 us; the launch traced here: 292 us
  waiting for transfers between devices  191 us (64%)
  starting transfers between devices  52.2 us (18%)
  matrix products  26.1 us (9%)
  other arithmetic  12 us (4%)
  Pallas kernels  5.24 us (2%)
  local copies, waits for them, and re-layouts  4.47 us (2%)
    ppermute x3, waiting for transfers between devices, line_reduce_scatter(): leftward = lax.ppermute(going_left[step - 1] + leftward, axis, left_route)  73.6 us
    ppermute x3, waiting for transfers between devices, line_all_to_all(): lax.ppermute(own_rows(me - distance), axis, [(k, k - distance) for k in r...  34.1 us
    ppermute x3, waiting for transfers between devices, line_all_to_all(): lax.ppermute(own_rows(me + distance), axis, [(k, k + distance) for k in r...  31.1 us
    ppermute x3, waiting for transfers between devices, line_reduce_scatter(): lax.ppermute(going_right[step - 1] + rightward, axis, right_route)  29.7 us
    dot_general x16, matrix products, bdot(): return jnp.dot(left, right, preferred_element_type=jnp.float32)  26.1 us
    ppermute x3, starting transfers between devices, line_reduce_scatter(): leftward = lax.ppermute(going_left[step - 1] + leftward, axis, left_route)  24.3 us
    ppermute x3, waiting for transfers between devices, shards(): entering = entering + lax.ppermute(leaving, 'tm', [(sender, sender - 1)])  22.8 us
    ppermute x3, starting transfers between devices, line_all_to_all(): lax.ppermute(own_rows(me - distance), axis, [(k, k - distance) for k in r...  7.67 us
  transfers between devices with their start and end apart: 21, of which 10 were waited for; matrix products, arithmetic and copies ran while one was open for 9% of the time, Pallas kernels for 0%

profile of v11, /device:TPU:25, one launch (start us, length us, event | category | flops | bytes accessed | tf_op | source)
XLA Modules:
  0.0 291.9 jit_solution(1569163839854906537)
XLA Ops:
  0.3 1.3 copy-done.1
  2.0 1.4 collective-permute-start
  3.4 4.0 %collective-permute-start.1 = (f32[2,256,256]{2,1,0:T(8,128)S(1)}, f32[2,256,256]{2,1,0:T(8,128)S(1)}, u32[]{:S(2)}, u32[]{:S(2)}) collective-permute-start(f32[2,256,256]{2,1,0:T(8,128)S(1)} %get-tuple-element.50), channel_id=1, source_target_pairs={{1,0},{2,1},{3,2},{5,4},{6,5},{7,6},{9,8},{10,9},{11,10},{13,12},{... | collective-permute-start | bytes 1572872 | tf_op jit(solution)/shard_map/ppermute | solution.py:100
  10.0 4.1 %collective-permute-start.13 = (f32[2,1024,256]{2,1,0:T(8,128)S(1)}, f32[2,1024,256]{2,1,0:T(8,128)S(1)}, u32[]{:S(2)}, u32[]{:S(2)}) collective-permute-start(f32[2,1024,256]{2,1,0:T(8,128)S(1)} %copy-done.2), channel_id=1, source_target_pairs={{1,0},{2,1},{3,2},{5,4},{6,5},{7,6},{9,8},{10,9},{11,10},{13,12},{... | collective-permute-start | bytes 6291464 | tf_op jit(solution)/shard_map/ppermute | solution.py:82
  14.2 2.6 collective-permute-done
  16.8 2.3 collective-permute-start.3
  20.7 18.5 %collective-permute-done.2 = f32[2,256,256]{2,1,0:T(8,128)S(1)} collective-permute-done((f32[2,256,256]{2,1,0:T(8,128)S(1)}, f32[2,256,256]{2,1,0:T(8,128)S(1)}, u32[]{:S(2)}, u32[]{:S(2)}) %collective-permute-start.2) | collective-permute-done | bytes 524320 | tf_op jit(solution)/shard_map/ppermute | solution.py:99
  39.2 1.3 collective-permute-start.5
  40.6 33.2 %collective-permute-done.3 = f32[2,256,256]{2,1,0:T(8,128)S(1)} collective-permute-done((f32[2,256,256]{2,1,0:T(8,128)S(1)}, f32[2,256,256]{2,1,0:T(8,128)S(1)}, u32[]{:S(2)}, u32[]{:S(2)}) %collective-permute-start.3) | collective-permute-done | bytes 524320 | tf_op jit(solution)/shard_map/ppermute | solution.py:100
  74.0 10.0 %collective-permute-done.4 = f32[2,256,256]{2,1,0:T(8,128)S(1)} collective-permute-done((f32[2,256,256]{2,1,0:T(8,128)S(1)}, f32[2,256,256]{2,1,0:T(8,128)S(1)}, u32[]{:S(2)}, u32[]{:S(2)}) %collective-permute-start.4) | collective-permute-done | bytes 524320 | tf_op jit(solution)/shard_map/ppermute | solution.py:99
  91.2 1.6 fusion.20
  93.7 13.7 %collective-permute-start.9 = (f32[2,1024,256]{2,1,0:T(8,128)S(1)}, f32[2,1024,256]{2,1,0:T(8,128)S(1)}, u32[]{:S(2)}, u32[]{:S(2)}) collective-permute-start(f32[2,1024,256]{2,1,0:T(8,128)S(1)} %get-tuple-element.22), channel_id=1, source_target_pairs={{3,2},{7,6},{11,10},{15,14},{19,18},{23,22},{27,26},{31,30}} | collective-permute-start | bytes 6291464 | tf_op jit(solution)/shard_map/ppermute | solution.py:59
  110.7 39.6 %collective-permute-done.9 = f32[2,1024,256]{2,1,0:T(8,128)S(1)} collective-permute-done((f32[2,1024,256]{2,1,0:T(8,128)S(1)}, f32[2,1024,256]{2,1,0:T(8,128)S(1)}, u32[]{:S(2)}, u32[]{:S(2)}) %collective-permute-start.9) | collective-permute-done | bytes 2097184 | tf_op jit(solution)/shard_map/ppermute | solution.py:59
  150.7 4.4 %collective-permute-start.10 = (f32[2,1024,256]{2,1,0:T(8,128)S(1)}, f32[2,1024,256]{2,1,0:T(8,128)S(1)}, u32[]{:S(2)}, u32[]{:S(2)}) collective-permute-start(f32[2,1024,256]{2,1,0:T(8,128)S(1)} %add.239), channel_id=1, source_target_pairs={{2,1},{3,2},{6,5},{7,6},{10,9},{11,10},{14,13},{15,14},{18,17},{19... | collective-permute-start | bytes 6291464 | tf_op jit(solution)/shard_map/ppermute | solution.py:59
  163.0 34.0 %collective-permute-done.10 = f32[2,1024,256]{2,1,0:T(8,128)S(1)} collective-permute-done((f32[2,1024,256]{2,1,0:T(8,128)S(1)}, f32[2,1024,256]{2,1,0:T(8,128)S(1)}, u32[]{:S(2)}, u32[]{:S(2)}) %collective-permute-start.10) | collective-permute-done | bytes 2097184 | tf_op jit(solution)/shard_map/ppermute | solution.py:59
  197.3 6.2 %collective-permute-start.11 = (f32[2,1024,256]{2,1,0:T(8,128)S(1)}, f32[2,1024,256]{2,1,0:T(8,128)S(1)}, u32[]{:S(2)}, u32[]{:S(2)}) collective-permute-start(f32[2,1024,256]{2,1,0:T(8,128)S(1)} %add.240), channel_id=1, source_target_pairs={{1,0},{2,1},{3,2},{5,4},{6,5},{7,6},{9,8},{10,9},{11,10},{13,12},{... | collective-permute-start | bytes 6291464 | tf_op jit(solution)/shard_map/ppermute | solution.py:59
  205.7 7.0 %fusion.11 = f32[1024,2048]{1,0:T(8,128)} fusion(bf16[1024,1024]{1,0:T(8,128)(2,1)S(1)} %get-tuple-element.30, bf16[1024,1024]{1,0:T(8,128)(2,1)S(1)} %get-tuple-element.29, f32[2,1024,1024]{2,1,0:T(8,128)S(1)} %add_dynamic-update-slice_fusion), kind=kOutput, calls=%fused_computation.36 | convolution fusion | flops 4305453056 | bytes 16777216 | tf_op jit(solution)/shard_map/dot_general | solution.py:29
  212.7 5.0 %fusion.5 = (bf16[1024,1024]{1,0:T(8,128)(2,1)S(1)}, bf16[1024,1024]{1,0:T(8,128)(2,1)S(1)}) fusion(f32[2,1024,1024]{2,1,0:T(8,128)S(1)} %add_dynamic-update-slice_fusion, f32[1024,2048]{1,0:T(8,128)} %fusion.11), kind=kOutput, calls=%fused_computation.27 | convolution fusion | flops 2161115136 | bytes 20971520 | tf_op jit(solution)/shard_map/dot_general | solution.py:29
  217.7 29.7 %collective-permute-done.8 = f32[2,1024,256]{2,1,0:T(8,128)S(1)} collective-permute-done((f32[2,1024,256]{2,1,0:T(8,128)S(1)}, f32[2,1024,256]{2,1,0:T(8,128)S(1)}, u32[]{:S(2)}, u32[]{:S(2)}) %collective-permute-start.8) | collective-permute-done | bytes 2097184 | tf_op jit(solution)/shard_map/ppermute | solution.py:58
  254.5 20.6 %collective-permute-done.19 = f32[1024,256]{1,0:T(8,128)S(1)} collective-permute-done((f32[1024,256]{1,0:T(8,128)S(1)}, f32[1024,256]{1,0:T(8,128)S(1)}, u32[]{:S(2)}, u32[]{:S(2)}) %collective-permute-start.19) | collective-permute-done | bytes 1048608 | tf_op jit(solution)/shard_map/ppermute | solution.py:164
  277.3 1.4 collective-permute-start.20
  278.7 2.2 collective-permute-done.20
  285.2 1.5 pad_maximum_fusion.field_ref
  286.7 5.2 %shard_map.46 = f32[2,1024,256]{2,1,0:T(8,128)} custom-call(s32[1024]{0:T(1024)} %order_ref.1, f32[2,1024,256]{2,1,0:T(8,128)} %pad_maximum_fusion.field_ref), custom_call_target="tpu_custom_call" | custom-call | bytes 4194304 | tf_op jit(solution)/shard_map/pallas_call | solution.py:122
  (74 shorter events, 40.5 us)
Async XLA Ops:
  1.6 7.1 %copy-start.2 = (f32[2,1024,256]{2,1,0:T(8,128)S(1)}, f32[2,1024,256]{2,1,0:T(8,128)}, u32[]{:S(2)}) copy-start(f32[2,1024,256]{2,1,0:T(8,128)} %param.6) | copy-start | bytes 6291460
  2.0 14.8 %collective-permute-start = (f32[2,256,256]{2,1,0:T(8,128)S(1)}, f32[2,256,256]{2,1,0:T(8,128)S(1)}, u32[]{:S(2)}, u32[]{:S(2)}) collective-permute-start(f32[2,256,256]{2,1,0:T(8,128)S(1)} %get-tuple-element.51), channel_id=1, source_target_pairs={{0,1},{1,2},{2,3},{4,5},{5,6},{6,7},{8,9},{9,10},{10,11},{12,13},{... | collective-permute-start | bytes 1572872 | tf_op jit(solution)/shard_map/ppermute | solution.py:99
  3.4 15.9 %collective-permute-start.1 = (f32[2,256,256]{2,1,0:T(8,128)S(1)}, f32[2,256,256]{2,1,0:T(8,128)S(1)}, u32[]{:S(2)}, u32[]{:S(2)}) collective-permute-start(f32[2,256,256]{2,1,0:T(8,128)S(1)} %get-tuple-element.50), channel_id=1, source_target_pairs={{1,0},{2,1},{3,2},{5,4},{6,5},{7,6},{9,8},{10,9},{11,10},{13,12},{... | collective-permute-start | bytes 1572872 | tf_op jit(solution)/shard_map/ppermute | solution.py:100
  7.4 31.8 %collective-permute-start.2 = (f32[2,256,256]{2,1,0:T(8,128)S(1)}, f32[2,256,256]{2,1,0:T(8,128)S(1)}, u32[]{:S(2)}, u32[]{:S(2)}) collective-permute-start(f32[2,256,256]{2,1,0:T(8,128)S(1)} %get-tuple-element.49), channel_id=1, source_target_pairs={{0,2},{1,3},{4,6},{5,7},{8,10},{9,11},{12,14},{13,15},{16,18},{17,... | collective-permute-start | bytes 1572872 | tf_op jit(solution)/shard_map/ppermute | solution.py:99
  8.7 98.6 %collective-permute-start.12 = (f32[2,1024,256]{2,1,0:T(8,128)S(1)}, f32[2,1024,256]{2,1,0:T(8,128)S(1)}, u32[]{:S(2)}, u32[]{:S(2)}) collective-permute-start(f32[2,1024,256]{2,1,0:T(8,128)S(1)} %copy-done.2), channel_id=1, source_target_pairs={{0,1},{1,2},{2,3},{4,5},{5,6},{6,7},{8,9},{9,10},{10,11},{12,13},{... | collective-permute-start | bytes 6291464 | tf_op jit(solution)/shard_map/ppermute | solution.py:81
  10.0 98.7 %collective-permute-start.13 = (f32[2,1024,256]{2,1,0:T(8,128)S(1)}, f32[2,1024,256]{2,1,0:T(8,128)S(1)}, u32[]{:S(2)}, u32[]{:S(2)}) collective-permute-start(f32[2,1024,256]{2,1,0:T(8,128)S(1)} %copy-done.2), channel_id=1, source_target_pairs={{1,0},{2,1},{3,2},{5,4},{6,5},{7,6},{9,8},{10,9},{11,10},{13,12},{... | collective-permute-start | bytes 6291464 | tf_op jit(solution)/shard_map/ppermute | solution.py:82
  16.8 57.1 %collective-permute-start.3 = (f32[2,256,256]{2,1,0:T(8,128)S(1)}, f32[2,256,256]{2,1,0:T(8,128)S(1)}, u32[]{:S(2)}, u32[]{:S(2)}) collective-permute-start(f32[2,256,256]{2,1,0:T(8,128)S(1)} %get-tuple-element.48), channel_id=1, source_target_pairs={{2,0},{3,1},{6,4},{7,5},{10,8},{11,9},{14,12},{15,13},{18,16},{19,... | collective-permute-start | bytes 1572872 | tf_op jit(solution)/shard_map/ppermute | solution.py:100
  19.3 64.8 %collective-permute-start.4 = (f32[2,256,256]{2,1,0:T(8,128)S(1)}, f32[2,256,256]{2,1,0:T(8,128)S(1)}, u32[]{:S(2)}, u32[]{:S(2)}) collective-permute-start(f32[2,256,256]{2,1,0:T(8,128)S(1)} %get-tuple-element.53), channel_id=1, source_target_pairs={{0,3},{4,7},{8,11},{12,15},{16,19},{20,23},{24,27},{28,31}} | collective-permute-start | bytes 1572872 | tf_op jit(solution)/shard_map/ppermute | solution.py:99
  39.2 45.9 %collective-permute-start.5 = (f32[2,256,256]{2,1,0:T(8,128)S(1)}, f32[2,256,256]{2,1,0:T(8,128)S(1)}, u32[]{:S(2)}, u32[]{:S(2)}) collective-permute-start(f32[2,256,256]{2,1,0:T(8,128)S(1)} %get-tuple-element.47), channel_id=1, source_target_pairs={{3,0},{7,4},{11,8},{15,12},{19,16},{23,20},{27,24},{31,28}} | collective-permute-start | bytes 1572872 | tf_op jit(solution)/shard_map/ppermute | solution.py:100
  85.2 1.6 copy-start
  92.9 16.6 %collective-permute-start.6 = (f32[2,1024,256]{2,1,0:T(8,128)S(1)}, f32[2,1024,256]{2,1,0:T(8,128)S(1)}, u32[]{:S(2)}, u32[]{:S(2)}) collective-permute-start(f32[2,1024,256]{2,1,0:T(8,128)S(1)} %get-tuple-element.19), channel_id=1, source_target_pairs={{0,1},{4,5},{8,9},{12,13},{16,17},{20,21},{24,25},{28,29}} | collective-permute-start | bytes 6291464 | tf_op jit(solution)/shard_map/ppermute | solution.py:58
  93.7 56.6 %collective-permute-start.9 = (f32[2,1024,256]{2,1,0:T(8,128)S(1)}, f32[2,1024,256]{2,1,0:T(8,128)S(1)}, u32[]{:S(2)}, u32[]{:S(2)}) collective-permute-start(f32[2,1024,256]{2,1,0:T(8,128)S(1)} %get-tuple-element.22), channel_id=1, source_target_pairs={{3,2},{7,6},{11,10},{15,14},{19,18},{23,22},{27,26},{31,30}} | collective-permute-start | bytes 6291464 | tf_op jit(solution)/shard_map/ppermute | solution.py:59
  107.4 47.7 %collective-permute-start.14 = (f32[2,1024,256]{2,1,0:T(8,128)S(1)}, f32[2,1024,256]{2,1,0:T(8,128)S(1)}, u32[]{:S(2)}, u32[]{:S(2)}) collective-permute-start(f32[2,1024,256]{2,1,0:T(8,128)S(1)} %collective-permute-done.12), channel_id=1, source_target_pairs={{1,2},{2,3},{5,6},{6,7},{9,10},{10,11},{13,14},{14,15},{17,18},{18... | collective-permute-start | bytes 6291464 | tf_op jit(solution)/shard_map/ppermute | solution.py:81
  108.7 47.7 %collective-permute-start.15 = (f32[2,1024,256]{2,1,0:T(8,128)S(1)}, f32[2,1024,256]{2,1,0:T(8,128)S(1)}, u32[]{:S(2)}, u32[]{:S(2)}) collective-permute-start(f32[2,1024,256]{2,1,0:T(8,128)S(1)} %collective-permute-done.13), channel_id=1, source_target_pairs={{1,0},{2,1},{5,4},{6,5},{9,8},{10,9},{13,12},{14,13},{17,16},{18,1... | collective-permute-start | bytes 6291464 | tf_op jit(solution)/shard_map/ppermute | solution.py:82
  109.9 51.5 %collective-permute-start.7 = (f32[2,1024,256]{2,1,0:T(8,128)S(1)}, f32[2,1024,256]{2,1,0:T(8,128)S(1)}, u32[]{:S(2)}, u32[]{:S(2)}) collective-permute-start(f32[2,1024,256]{2,1,0:T(8,128)S(1)} %add.237), channel_id=1, source_target_pairs={{0,1},{1,2},{4,5},{5,6},{8,9},{9,10},{12,13},{13,14},{16,17},{17,1... | collective-permute-start | bytes 6291464 | tf_op jit(solution)/shard_map/ppermute | solution.py:58
  150.7 7.8 %copy-start.3 = (f32[2,1024,256]{2,1,0:T(8,128)S(1)}, f32[2,1024,256]{2,1,0:T(8,128)}, u32[]{:S(2)}) copy-start(f32[2,1024,256]{2,1,0:T(8,128)} %param.6) | copy-start | bytes 6291460
  150.7 46.4 %collective-permute-start.10 = (f32[2,1024,256]{2,1,0:T(8,128)S(1)}, f32[2,1024,256]{2,1,0:T(8,128)S(1)}, u32[]{:S(2)}, u32[]{:S(2)}) collective-permute-start(f32[2,1024,256]{2,1,0:T(8,128)S(1)} %add.239), channel_id=1, source_target_pairs={{2,1},{3,2},{6,5},{7,6},{10,9},{11,10},{14,13},{15,14},{18,17},{19... | collective-permute-start | bytes 6291464 | tf_op jit(solution)/shard_map/ppermute | solution.py:59
  155.1 48.4 %collective-permute-start.16 = (f32[2,1024,256]{2,1,0:T(8,128)S(1)}, f32[2,1024,256]{2,1,0:T(8,128)S(1)}, u32[]{:S(2)}, u32[]{:S(2)}) collective-permute-start(f32[2,1024,256]{2,1,0:T(8,128)S(1)} %collective-permute-done.14), channel_id=1, source_target_pairs={{2,3},{6,7},{10,11},{14,15},{18,19},{22,23},{26,27},{30,31}} | collective-permute-start | bytes 6291464 | tf_op jit(solution)/shard_map/ppermute | solution.py:81
  156.4 47.7 %collective-permute-start.17 = (f32[2,1024,256]{2,1,0:T(8,128)S(1)}, f32[2,1024,256]{2,1,0:T(8,128)S(1)}, u32[]{:S(2)}, u32[]{:S(2)}) collective-permute-start(f32[2,1024,256]{2,1,0:T(8,128)S(1)} %collective-permute-done.15), channel_id=1, source_target_pairs={{1,0},{5,4},{9,8},{13,12},{17,16},{21,20},{25,24},{29,28}} | collective-permute-start | bytes 6291464 | tf_op jit(solution)/shard_map/ppermute | solution.py:82
  161.7 85.7 %collective-permute-start.8 = (f32[2,1024,256]{2,1,0:T(8,128)S(1)}, f32[2,1024,256]{2,1,0:T(8,128)S(1)}, u32[]{:S(2)}, u32[]{:S(2)}) collective-permute-start(f32[2,1024,256]{2,1,0:T(8,128)S(1)} %add.238), channel_id=1, source_target_pairs={{0,1},{1,2},{2,3},{4,5},{5,6},{6,7},{8,9},{9,10},{10,11},{12,13},{... | collective-permute-start | bytes 6291464 | tf_op jit(solution)/shard_map/ppermute | solution.py:58
  197.3 50.1 %collective-permute-start.11 = (f32[2,1024,256]{2,1,0:T(8,128)S(1)}, f32[2,1024,256]{2,1,0:T(8,128)S(1)}, u32[]{:S(2)}, u32[]{:S(2)}) collective-permute-start(f32[2,1024,256]{2,1,0:T(8,128)S(1)} %add.240), channel_id=1, source_target_pairs={{1,0},{2,1},{3,2},{5,4},{6,5},{7,6},{9,8},{10,9},{11,10},{13,12},{... | collective-permute-start | bytes 6291464 | tf_op jit(solution)/shard_map/ppermute | solution.py:59
  250.0 1.0 collective-permute-start.18
  253.2 21.9 %collective-permute-start.19 = (f32[1024,256]{1,0:T(8,128)S(1)}, f32[1024,256]{1,0:T(8,128)S(1)}, u32[]{:S(2)}, u32[]{:S(2)}) collective-permute-start(f32[1024,256]{1,0:T(8,128)S(1)} %fusion.54), channel_id=1, source_target_pairs={{8,4},{9,5},{10,6},{11,7},{24,20},{25,21},{26,22},{27,23}} | collective-permute-start | bytes 3145736 | tf_op jit(solution)/shard_map/ppermute | solution.py:164
  277.3 3.6 %collective-permute-start.20 = (f32[1024,256]{1,0:T(8,128)S(1)}, f32[1024,256]{1,0:T(8,128)S(1)}, u32[]{:S(2)}, u32[]{:S(2)}) collective-permute-start(f32[1024,256]{1,0:T(8,128)S(1)} %fusion.52), channel_id=1, source_target_pairs={{4,0},{5,1},{6,2},{7,3},{20,16},{21,17},{22,18},{23,19}} | collective-permute-start | bytes 3145736 | tf_op jit(solution)/shard_map/ppermute | solution.py:164
  (1 other events, 1.6 us)

commit v12 on v11

--- a/solution.py
+++ b/solution.py
@@ -95,9 +95,12 @@
 
     shape = (value.shape[0], rows, count * value.shape[2])
     whole = add_at(jnp.zeros(shape, value.dtype), own_rows(me), me, 2)
+    sending = lax.optimization_barrier(
+        [(own_rows(me + distance), own_rows(me - distance)) for distance in range(1, count)]
+    )
     for distance in range(1, count):
-        right = lax.ppermute(own_rows(me + distance), axis, [(k, k + distance) for k in range(0, count - distance)])
-        left = lax.ppermute(own_rows(me - distance), axis, [(k, k - distance) for k in range(distance, count)])
+        right = lax.ppermute(sending[distance - 1][0], axis, [(k, k + distance) for k in range(0, count - distance)])
+        left = lax.ppermute(sending[distance - 1][1], axis, [(k, k - distance) for k in range(distance, count)])
         whole = add_at(whole, right, me - distance, 2)
         whole = add_at(whole, left, me + distance, 2)
     return whole

time: 297 us -> 297 us (level)
  no operation moved by 1% of the time
where the time goes in v12:
time: 297 us; the launch traced here: 292 us
  waiting for transfers between devices  191 us (64%)
  starting transfers between devices  52.2 us (18%)
  matrix products  26.1 us (9%)
  other arithmetic  12 us (4%)
  Pallas kernels  5.24 us (2%)
  local copies, waits for them, and re-layouts  4.47 us (2%)
    ppermute x3, waiting for transfers between devices, line_reduce_scatter(): leftward = lax.ppermute(going_left[step - 1] + leftward, axis, left_route)  73.6 us
    ppermute x3, waiting for transfers between devices, line_all_to_all(): lax.ppermute(sending[distance - 1][1], axis, [(k, k - distance) for k in...  34.1 us
    ppermute x3, waiting for transfers between devices, line_all_to_all(): lax.ppermute(sending[distance - 1][0], axis, [(k, k + distance) for k in...  31.1 us
    ppermute x3, waiting for transfers between devices, line_reduce_scatter(): lax.ppermute(going_right[step - 1] + rightward, axis, right_route)  29.7 us
    dot_general x16, matrix products, bdot(): return jnp.dot(left, right, preferred_element_type=jnp.float32)  26.1 us
    ppermute x3, starting transfers between devices, line_reduce_scatter(): leftward = lax.ppermute(going_left[step - 1] + leftward, axis, left_route)  24.3 us
    ppermute x3, waiting for transfers between devices, shards(): entering = entering + lax.ppermute(leaving, 'tm', [(sender, sender - 1)])  22.8 us
    ppermute x3, starting transfers between devices, line_all_to_all(): lax.ppermute(sending[distance - 1][1], axis, [(k, k - distance) for k in...  7.67 us
  transfers between devices with their start and end apart: 21, of which 10 were waited for; matrix products, arithmetic and copies ran while one was open for 9% of the time, Pallas kernels for 0%

profile of v12, /device:TPU:25, one launch (start us, length us, event | category | flops | bytes accessed | tf_op | source)
XLA Modules:
  0.0 291.9 jit_solution(8041259620086873461)
XLA Ops:
  0.3 1.3 copy-done.1
  2.0 1.4 collective-permute-start
  3.4 4.0 %collective-permute-start.1 = (f32[2,256,256]{2,1,0:T(8,128)S(1)}, f32[2,256,256]{2,1,0:T(8,128)S(1)}, u32[]{:S(2)}, u32[]{:S(2)}) collective-permute-start(f32[2,256,256]{2,1,0:T(8,128)S(1)} %get-tuple-element.23), channel_id=1, source_target_pairs={{1,0},{2,1},{3,2},{5,4},{6,5},{7,6},{9,8},{10,9},{11,10},{13,12},{... | collective-permute-start | bytes 1572872 | tf_op jit(solution)/shard_map/ppermute | solution.py:103
  10.0 4.1 %collective-permute-start.13 = (f32[2,1024,256]{2,1,0:T(8,128)S(1)}, f32[2,1024,256]{2,1,0:T(8,128)S(1)}, u32[]{:S(2)}, u32[]{:S(2)}) collective-permute-start(f32[2,1024,256]{2,1,0:T(8,128)S(1)} %copy-done.2), channel_id=1, source_target_pairs={{1,0},{2,1},{3,2},{5,4},{6,5},{7,6},{9,8},{10,9},{11,10},{13,12},{... | collective-permute-start | bytes 6291464 | tf_op jit(solution)/shard_map/ppermute | solution.py:82
  14.2 2.6 collective-permute-done
  16.8 2.3 collective-permute-start.3
  20.7 18.5 %collective-permute-done.2 = f32[2,256,256]{2,1,0:T(8,128)S(1)} collective-permute-done((f32[2,256,256]{2,1,0:T(8,128)S(1)}, f32[2,256,256]{2,1,0:T(8,128)S(1)}, u32[]{:S(2)}, u32[]{:S(2)}) %collective-permute-start.2) | collective-permute-done | bytes 524320 | tf_op jit(solution)/shard_map/ppermute | solution.py:102
  39.2 1.3 collective-permute-start.5
  40.6 33.2 %collective-permute-done.3 = f32[2,256,256]{2,1,0:T(8,128)S(1)} collective-permute-done((f32[2,256,256]{2,1,0:T(8,128)S(1)}, f32[2,256,256]{2,1,0:T(8,128)S(1)}, u32[]{:S(2)}, u32[]{:S(2)}) %collective-permute-start.3) | collective-permute-done | bytes 524320 | tf_op jit(solution)/shard_map/ppermute | solution.py:103
  74.0 10.0 %collective-permute-done.4 = f32[2,256,256]{2,1,0:T(8,128)S(1)} collective-permute-done((f32[2,256,256]{2,1,0:T(8,128)S(1)}, f32[2,256,256]{2,1,0:T(8,128)S(1)}, u32[]{:S(2)}, u32[]{:S(2)}) %collective-permute-start.4) | collective-permute-done | bytes 524320 | tf_op jit(solution)/shard_map/ppermute | solution.py:102
  91.2 1.6 fusion.20
  93.7 13.7 %collective-permute-start.9 = (f32[2,1024,256]{2,1,0:T(8,128)S(1)}, f32[2,1024,256]{2,1,0:T(8,128)S(1)}, u32[]{:S(2)}, u32[]{:S(2)}) collective-permute-start(f32[2,1024,256]{2,1,0:T(8,128)S(1)} %get-tuple-element.34), channel_id=1, source_target_pairs={{3,2},{7,6},{11,10},{15,14},{19,18},{23,22},{27,26},{31,30}} | collective-permute-start | bytes 6291464 | tf_op jit(solution)/shard_map/ppermute | solution.py:59
  110.7 39.6 %collective-permute-done.9 = f32[2,1024,256]{2,1,0:T(8,128)S(1)} collective-permute-done((f32[2,1024,256]{2,1,0:T(8,128)S(1)}, f32[2,1024,256]{2,1,0:T(8,128)S(1)}, u32[]{:S(2)}, u32[]{:S(2)}) %collective-permute-start.9) | collective-permute-done | bytes 2097184 | tf_op jit(solution)/shard_map/ppermute | solution.py:59
  150.7 4.4 %collective-permute-start.10 = (f32[2,1024,256]{2,1,0:T(8,128)S(1)}, f32[2,1024,256]{2,1,0:T(8,128)S(1)}, u32[]{:S(2)}, u32[]{:S(2)}) collective-permute-start(f32[2,1024,256]{2,1,0:T(8,128)S(1)} %add.239), channel_id=1, source_target_pairs={{2,1},{3,2},{6,5},{7,6},{10,9},{11,10},{14,13},{15,14},{18,17},{19... | collective-permute-start | bytes 6291464 | tf_op jit(solution)/shard_map/ppermute | solution.py:59
  163.0 34.0 %collective-permute-done.10 = f32[2,1024,256]{2,1,0:T(8,128)S(1)} collective-permute-done((f32[2,1024,256]{2,1,0:T(8,128)S(1)}, f32[2,1024,256]{2,1,0:T(8,128)S(1)}, u32[]{:S(2)}, u32[]{:S(2)}) %collective-permute-start.10) | collective-permute-done | bytes 2097184 | tf_op jit(solution)/shard_map/ppermute | solution.py:59
  197.3 6.2 %collective-permute-start.11 = (f32[2,1024,256]{2,1,0:T(8,128)S(1)}, f32[2,1024,256]{2,1,0:T(8,128)S(1)}, u32[]{:S(2)}, u32[]{:S(2)}) collective-permute-start(f32[2,1024,256]{2,1,0:T(8,128)S(1)} %add.240), channel_id=1, source_target_pairs={{1,0},{2,1},{3,2},{5,4},{6,5},{7,6},{9,8},{10,9},{11,10},{13,12},{... | collective-permute-start | bytes 6291464 | tf_op jit(solution)/shard_map/ppermute | solution.py:59
  205.7 7.0 %fusion.11 = f32[1024,2048]{1,0:T(8,128)} fusion(bf16[1024,1024]{1,0:T(8,128)(2,1)S(1)} %get-tuple-element.42, bf16[1024,1024]{1,0:T(8,128)(2,1)S(1)} %get-tuple-element.41, f32[2,1024,1024]{2,1,0:T(8,128)S(1)} %add_dynamic-update-slice_fusion), kind=kOutput, calls=%fused_computation.36 | convolution fusion | flops 4305453056 | bytes 16777216 | tf_op jit(solution)/shard_map/dot_general | solution.py:29
  212.7 5.0 %fusion.5 = (bf16[1024,1024]{1,0:T(8,128)(2,1)S(1)}, bf16[1024,1024]{1,0:T(8,128)(2,1)S(1)}) fusion(f32[2,1024,1024]{2,1,0:T(8,128)S(1)} %add_dynamic-update-slice_fusion, f32[1024,2048]{1,0:T(8,128)} %fusion.11), kind=kOutput, calls=%fused_computation.27 | convolution fusion | flops 2161115136 | bytes 20971520 | tf_op jit(solution)/shard_map/dot_general | solution.py:29
  217.7 29.7 %collective-permute-done.8 = f32[2,1024,256]{2,1,0:T(8,128)S(1)} collective-permute-done((f32[2,1024,256]{2,1,0:T(8,128)S(1)}, f32[2,1024,256]{2,1,0:T(8,128)S(1)}, u32[]{:S(2)}, u32[]{:S(2)}) %collective-permute-start.8) | collective-permute-done | bytes 2097184 | tf_op jit(solution)/shard_map/ppermute | solution.py:58
  254.5 20.6 %collective-permute-done.19 = f32[1024,256]{1,0:T(8,128)S(1)} collective-permute-done((f32[1024,256]{1,0:T(8,128)S(1)}, f32[1024,256]{1,0:T(8,128)S(1)}, u32[]{:S(2)}, u32[]{:S(2)}) %collective-permute-start.19) | collective-permute-done | bytes 1048608 | tf_op jit(solution)/shard_map/ppermute | solution.py:167
  277.3 1.4 collective-permute-start.20
  278.7 2.2 collective-permute-done.20
  285.2 1.5 pad_maximum_fusion.field_ref
  286.7 5.2 %shard_map.46 = f32[2,1024,256]{2,1,0:T(8,128)} custom-call(s32[1024]{0:T(1024)} %order_ref.1, f32[2,1024,256]{2,1,0:T(8,128)} %pad_maximum_fusion.field_ref), custom_call_target="tpu_custom_call" | custom-call | bytes 4194304 | tf_op jit(solution)/shard_map/pallas_call | solution.py:125
  (74 shorter events, 40.5 us)
Async XLA Ops:
  1.6 7.1 %copy-start.2 = (f32[2,1024,256]{2,1,0:T(8,128)S(1)}, f32[2,1024,256]{2,1,0:T(8,128)}, u32[]{:S(2)}) copy-start(f32[2,1024,256]{2,1,0:T(8,128)} %param.6) | copy-start | bytes 6291460
  2.0 14.8 %collective-permute-start = (f32[2,256,256]{2,1,0:T(8,128)S(1)}, f32[2,256,256]{2,1,0:T(8,128)S(1)}, u32[]{:S(2)}, u32[]{:S(2)}) collective-permute-start(f32[2,256,256]{2,1,0:T(8,128)S(1)} %get-tuple-element.22), channel_id=1, source_target_pairs={{0,1},{1,2},{2,3},{4,5},{5,6},{6,7},{8,9},{9,10},{10,11},{12,13},{... | collective-permute-start | bytes 1572872 | tf_op jit(solution)/shard_map/ppermute | solution.py:102
  3.4 15.9 %collective-permute-start.1 = (f32[2,256,256]{2,1,0:T(8,128)S(1)}, f32[2,256,256]{2,1,0:T(8,128)S(1)}, u32[]{:S(2)}, u32[]{:S(2)}) collective-permute-start(f32[2,256,256]{2,1,0:T(8,128)S(1)} %get-tuple-element.23), channel_id=1, source_target_pairs={{1,0},{2,1},{3,2},{5,4},{6,5},{7,6},{9,8},{10,9},{11,10},{13,12},{... | collective-permute-start | bytes 1572872 | tf_op jit(solution)/shard_map/ppermute | solution.py:103
  7.4 31.8 %collective-permute-start.2 = (f32[2,256,256]{2,1,0:T(8,128)S(1)}, f32[2,256,256]{2,1,0:T(8,128)S(1)}, u32[]{:S(2)}, u32[]{:S(2)}) collective-permute-start(f32[2,256,256]{2,1,0:T(8,128)S(1)} %get-tuple-element.24), channel_id=1, source_target_pairs={{0,2},{1,3},{4,6},{5,7},{8,10},{9,11},{12,14},{13,15},{16,18},{17,... | collective-permute-start | bytes 1572872 | tf_op jit(solution)/shard_map/ppermute | solution.py:102
  8.7 98.6 %collective-permute-start.12 = (f32[2,1024,256]{2,1,0:T(8,128)S(1)}, f32[2,1024,256]{2,1,0:T(8,128)S(1)}, u32[]{:S(2)}, u32[]{:S(2)}) collective-permute-start(f32[2,1024,256]{2,1,0:T(8,128)S(1)} %copy-done.2), channel_id=1, source_target_pairs={{0,1},{1,2},{2,3},{4,5},{5,6},{6,7},{8,9},{9,10},{10,11},{12,13},{... | collective-permute-start | bytes 6291464 | tf_op jit(solution)/shard_map/ppermute | solution.py:81
  10.0 98.7 %collective-permute-start.13 = (f32[2,1024,256]{2,1,0:T(8,128)S(1)}, f32[2,1024,256]{2,1,0:T(8,128)S(1)}, u32[]{:S(2)}, u32[]{:S(2)}) collective-permute-start(f32[2,1024,256]{2,1,0:T(8,128)S(1)} %copy-done.2), channel_id=1, source_target_pairs={{1,0},{2,1},{3,2},{5,4},{6,5},{7,6},{9,8},{10,9},{11,10},{13,12},{... | collective-permute-start | bytes 6291464 | tf_op jit(solution)/shard_map/ppermute | solution.py:82
  16.8 57.1 %collective-permute-start.3 = (f32[2,256,256]{2,1,0:T(8,128)S(1)}, f32[2,256,256]{2,1,0:T(8,128)S(1)}, u32[]{:S(2)}, u32[]{:S(2)}) collective-permute-start(f32[2,256,256]{2,1,0:T(8,128)S(1)} %get-tuple-element.25), channel_id=1, source_target_pairs={{2,0},{3,1},{6,4},{7,5},{10,8},{11,9},{14,12},{15,13},{18,16},{19,... | collective-permute-start | bytes 1572872 | tf_op jit(solution)/shard_map/ppermute | solution.py:103
  19.3 64.8 %collective-permute-start.4 = (f32[2,256,256]{2,1,0:T(8,128)S(1)}, f32[2,256,256]{2,1,0:T(8,128)S(1)}, u32[]{:S(2)}, u32[]{:S(2)}) collective-permute-start(f32[2,256,256]{2,1,0:T(8,128)S(1)} %get-tuple-element.26), channel_id=1, source_target_pairs={{0,3},{4,7},{8,11},{12,15},{16,19},{20,23},{24,27},{28,31}} | collective-permute-start | bytes 1572872 | tf_op jit(solution)/shard_map/ppermute | solution.py:102
  39.2 45.9 %collective-permute-start.5 = (f32[2,256,256]{2,1,0:T(8,128)S(1)}, f32[2,256,256]{2,1,0:T(8,128)S(1)}, u32[]{:S(2)}, u32[]{:S(2)}) collective-permute-start(f32[2,256,256]{2,1,0:T(8,128)S(1)} %get-tuple-element.27), channel_id=1, source_target_pairs={{3,0},{7,4},{11,8},{15,12},{19,16},{23,20},{27,24},{31,28}} | collective-permute-start | bytes 1572872 | tf_op jit(solution)/shard_map/ppermute | solution.py:103
  85.2 1.6 copy-start
  92.9 16.6 %collective-permute-start.6 = (f32[2,1024,256]{2,1,0:T(8,128)S(1)}, f32[2,1024,256]{2,1,0:T(8,128)S(1)}, u32[]{:S(2)}, u32[]{:S(2)}) collective-permute-start(f32[2,1024,256]{2,1,0:T(8,128)S(1)} %get-tuple-element.31), channel_id=1, source_target_pairs={{0,1},{4,5},{8,9},{12,13},{16,17},{20,21},{24,25},{28,29}} | collective-permute-start | bytes 6291464 | tf_op jit(solution)/shard_map/ppermute | solution.py:58
  93.7 56.6 %collective-permute-start.9 = (f32[2,1024,256]{2,1,0:T(8,128)S(1)}, f32[2,1024,256]{2,1,0:T(8,128)S(1)}, u32[]{:S(2)}, u32[]{:S(2)}) collective-permute-start(f32[2,1024,256]{2,1,0:T(8,128)S(1)} %get-tuple-element.34), channel_id=1, source_target_pairs={{3,2},{7,6},{11,10},{15,14},{19,18},{23,22},{27,26},{31,30}} | collective-permute-start | bytes 6291464 | tf_op jit(solution)/shard_map/ppermute | solution.py:59
  107.4 47.7 %collective-permute-start.14 = (f32[2,1024,256]{2,1,0:T(8,128)S(1)}, f32[2,1024,256]{2,1,0:T(8,128)S(1)}, u32[]{:S(2)}, u32[]{:S(2)}) collective-permute-start(f32[2,1024,256]{2,1,0:T(8,128)S(1)} %collective-permute-done.12), channel_id=1, source_target_pairs={{1,2},{2,3},{5,6},{6,7},{9,10},{10,11},{13,14},{14,15},{17,18},{18... | collective-permute-start | bytes 6291464 | tf_op jit(solution)/shard_map/ppermute | solution.py:81
  108.7 47.7 %collective-permute-start.15 = (f32[2,1024,256]{2,1,0:T(8,128)S(1)}, f32[2,1024,256]{2,1,0:T(8,128)S(1)}, u32[]{:S(2)}, u32[]{:S(2)}) collective-permute-start(f32[2,1024,256]{2,1,0:T(8,128)S(1)} %collective-permute-done.13), channel_id=1, source_target_pairs={{1,0},{2,1},{5,4},{6,5},{9,8},{10,9},{13,12},{14,13},{17,16},{18,1... | collective-permute-start | bytes 6291464 | tf_op jit(solution)/shard_map/ppermute | solution.py:82
  109.9 51.5 %collective-permute-start.7 = (f32[2,1024,256]{2,1,0:T(8,128)S(1)}, f32[2,1024,256]{2,1,0:T(8,128)S(1)}, u32[]{:S(2)}, u32[]{:S(2)}) collective-permute-start(f32[2,1024,256]{2,1,0:T(8,128)S(1)} %add.237), channel_id=1, source_target_pairs={{0,1},{1,2},{4,5},{5,6},{8,9},{9,10},{12,13},{13,14},{16,17},{17,1... | collective-permute-start | bytes 6291464 | tf_op jit(solution)/shard_map/ppermute | solution.py:58
  150.7 7.8 %copy-start.3 = (f32[2,1024,256]{2,1,0:T(8,128)S(1)}, f32[2,1024,256]{2,1,0:T(8,128)}, u32[]{:S(2)}) copy-start(f32[2,1024,256]{2,1,0:T(8,128)} %param.6) | copy-start | bytes 6291460
  150.7 46.4 %collective-permute-start.10 = (f32[2,1024,256]{2,1,0:T(8,128)S(1)}, f32[2,1024,256]{2,1,0:T(8,128)S(1)}, u32[]{:S(2)}, u32[]{:S(2)}) collective-permute-start(f32[2,1024,256]{2,1,0:T(8,128)S(1)} %add.239), channel_id=1, source_target_pairs={{2,1},{3,2},{6,5},{7,6},{10,9},{11,10},{14,13},{15,14},{18,17},{19... | collective-permute-start | bytes 6291464 | tf_op jit(solution)/shard_map/ppermute | solution.py:59
  155.1 48.4 %collective-permute-start.16 = (f32[2,1024,256]{2,1,0:T(8,128)S(1)}, f32[2,1024,256]{2,1,0:T(8,128)S(1)}, u32[]{:S(2)}, u32[]{:S(2)}) collective-permute-start(f32[2,1024,256]{2,1,0:T(8,128)S(1)} %collective-permute-done.14), channel_id=1, source_target_pairs={{2,3},{6,7},{10,11},{14,15},{18,19},{22,23},{26,27},{30,31}} | collective-permute-start | bytes 6291464 | tf_op jit(solution)/shard_map/ppermute | solution.py:81
  156.4 47.7 %collective-permute-start.17 = (f32[2,1024,256]{2,1,0:T(8,128)S(1)}, f32[2,1024,256]{2,1,0:T(8,128)S(1)}, u32[]{:S(2)}, u32[]{:S(2)}) collective-permute-start(f32[2,1024,256]{2,1,0:T(8,128)S(1)} %collective-permute-done.15), channel_id=1, source_target_pairs={{1,0},{5,4},{9,8},{13,12},{17,16},{21,20},{25,24},{29,28}} | collective-permute-start | bytes 6291464 | tf_op jit(solution)/shard_map/ppermute | solution.py:82
  161.7 85.7 %collective-permute-start.8 = (f32[2,1024,256]{2,1,0:T(8,128)S(1)}, f32[2,1024,256]{2,1,0:T(8,128)S(1)}, u32[]{:S(2)}, u32[]{:S(2)}) collective-permute-start(f32[2,1024,256]{2,1,0:T(8,128)S(1)} %add.238), channel_id=1, source_target_pairs={{0,1},{1,2},{2,3},{4,5},{5,6},{6,7},{8,9},{9,10},{10,11},{12,13},{... | collective-permute-start | bytes 6291464 | tf_op jit(solution)/shard_map/ppermute | solution.py:58
  197.3 50.1 %collective-permute-start.11 = (f32[2,1024,256]{2,1,0:T(8,128)S(1)}, f32[2,1024,256]{2,1,0:T(8,128)S(1)}, u32[]{:S(2)}, u32[]{:S(2)}) collective-permute-start(f32[2,1024,256]{2,1,0:T(8,128)S(1)} %add.240), channel_id=1, source_target_pairs={{1,0},{2,1},{3,2},{5,4},{6,5},{7,6},{9,8},{10,9},{11,10},{13,12},{... | collective-permute-start | bytes 6291464 | tf_op jit(solution)/shard_map/ppermute | solution.py:59
  250.0 1.0 collective-permute-start.18
  253.2 21.9 %collective-permute-start.19 = (f32[1024,256]{1,0:T(8,128)S(1)}, f32[1024,256]{1,0:T(8,128)S(1)}, u32[]{:S(2)}, u32[]{:S(2)}) collective-permute-start(f32[1024,256]{1,0:T(8,128)S(1)} %fusion.54), channel_id=1, source_target_pairs={{8,4},{9,5},{10,6},{11,7},{24,20},{25,21},{26,22},{27,23}} | collective-permute-start | bytes 3145736 | tf_op jit(solution)/shard_map/ppermute | solution.py:167
  277.3 3.6 %collective-permute-start.20 = (f32[1024,256]{1,0:T(8,128)S(1)}, f32[1024,256]{1,0:T(8,128)S(1)}, u32[]{:S(2)}, u32[]{:S(2)}) collective-permute-start(f32[1024,256]{1,0:T(8,128)S(1)} %fusion.52), channel_id=1, source_target_pairs={{4,0},{5,1},{6,2},{7,3},{20,16},{21,17},{22,18},{23,19}} | collective-permute-start | bytes 3145736 | tf_op jit(solution)/shard_map/ppermute | solution.py:167
  (1 other events, 1.6 us)
